TPU v7x, 512 devices: a whole 4x8x8 slice. The times are simulated.
512 devices in a mesh: req: 64 (over y, z), tp: 8 (over x, core).
Axes of the slice: x: 4, y: 8, z: 8, core: 2. Of those that a mesh axis runs over, the one named last changes fastest.
Arguments:
- hidden_in: bfloat16 [64, 512, 1024], P(None, 'req', 'tp'), may hold values from -64 to 64
- cache_keys: bfloat16 [64, 512, 1024], P('req', None, 'tp'), may hold values from -250 to 250
- cache_values: bfloat16 [64, 512, 1024], P('req', None, 'tp'), may hold values from -6 to 6
- cache_lengths: int32 [64], replicated, may hold values from 32 to 512, as said below
- owner_order: int32 [64], replicated, may hold values from 0 to 63, as said below
- request_slot: int32 [64], replicated, may hold values from 0 to 63, as said below
- proj_weight: bfloat16 [3, 1024, 1024], P(None, None, 'tp'), may hold values from -0.0625 to 0.0625
- proj_bias: bfloat16 [3, 1024], P(None, 'tp'), may hold values from -1.5 to 1.5
- output_weight: bfloat16 [1024, 1024], P('tp'), may hold values from -0.75 to 0.75
- output_bias: bfloat16 [1024], replicated, may hold values from -2.5 to 2.5
- norm_gains: bfloat16 [2, 1024], replicated, may hold values from 0.5 to 1.5
- norm_biases: bfloat16 [2, 1024], replicated, may hold values from -2.5 to 2.5
- widen_weight: bfloat16 [1024, 4096], P(None, 'tp'), may hold values from -0.1875 to 0.1875
- widen_bias: bfloat16 [4096], P('tp'), may hold values from -2.5 to 2.5
- narrow_weight: bfloat16 [4096, 1024], P('tp'), may hold values from -0.09375 to 0.09375
- narrow_bias: bfloat16 [1024], replicated, may hold values from -2.5 to 2.5
Outputs:
- hidden_out: bfloat16 [64, 512, 1024], P(None, 'req', 'tp')
- new_cache: bfloat16 [2, 64, 512, 1024], P(None, 'req', None, 'tp')
Inputs may be any that keep to these rules, and one draw needn't show every extreme that they name: owner_order is a permutation of the requests; owner slot s lies on index s // 1 of req. request_slot[owner_order[s]] = s for every slot s. `cache_lengths`: given in request order; the longest is exactly 512.
All inputs are finite; a program needn't handle non-finite values.
Results may differ from a plain program's by a relative error of at most 0.014.
Values may be sent and summed in bfloat16 or wider, within the bound.
No kernel may reach another device: no remote copies, remote signals or barrier semaphores. Data moves between devices by JAX's collectives and lax.ppermute only.
A program may use at most 64 MiB of HBM per device.

v0:
```python
import jax
import jax.numpy as jnp
from jax import lax
from jax.sharding import PartitionSpec as P

HD = 64


def layer_norm(values, scale_row, shift_row):
    average = jnp.mean(values, axis=-1, keepdims=True)
    centred = values - average
    spread = jnp.mean(centred * centred, axis=-1, keepdims=True)
    return centred * lax.rsqrt(spread + 1e-05) * scale_row.astype(jnp.float32) + shift_row.astype(
        jnp.float32
    )


def split_heads(rows_block):
    return rows_block.reshape(rows_block.shape[0], -1, HD)


def block_scores(query_heads, keys_block, allowed):
    scores = jnp.einsum(
        "thd,shd->hts", query_heads, split_heads(keys_block), preferred_element_type=jnp.float32
    )
    return jnp.where(allowed[None], scores, -jnp.inf)


def to_rows(factor):
    return jnp.transpose(factor, (1, 0, 2))


def slot_attention(fields):
    query_rows, key_rows, value_rows, slot_keys, slot_values, length = fields
    fresh_len = query_rows.shape[0]
    block_len = min(512, slot_keys.shape[0])
    block_count = slot_keys.shape[0] // block_len
    query_heads = split_heads(query_rows)
    self_mask = jnp.arange(fresh_len)[:, None] >= jnp.arange(fresh_len)[None, :]
    self_scores = block_scores(query_heads, key_rows, self_mask)
    row_top = jnp.max(self_scores, axis=2, keepdims=True)
    raised = jnp.exp(self_scores - row_top)
    row_total = jnp.sum(raised, axis=2, keepdims=True)
    context = jnp.einsum(
        "hts,shd->thd",
        raised.astype(jnp.bfloat16),
        split_heads(value_rows),
        preferred_element_type=jnp.float32,
    )
    positions = jnp.arange(block_len)

    def one_block(number, carry):
        old_top, old_total, running = carry
        begin_at = number * block_len
        allowed = jnp.broadcast_to((begin_at + positions < length)[None, :], (fresh_len, block_len))
        scores = block_scores(query_heads, slot_keys, allowed)
        new_top = jnp.maximum(old_top, jnp.max(scores, axis=2, keepdims=True))
        factor = jnp.exp(old_top - new_top)
        block_raised = jnp.exp(scores - new_top)
        new_total = old_total * factor + jnp.sum(block_raised, axis=2, keepdims=True)
        added = jnp.einsum(
            "hts,shd->thd",
            block_raised.astype(jnp.bfloat16),
            split_heads(slot_values),
            preferred_element_type=jnp.float32,
        )
        return (new_top, new_total, running * to_rows(factor) + added)

    row_top, row_total, context = lax.fori_loop(
        0, block_count, one_block, (row_top, row_total, context)
    )
    context = context / to_rows(row_total)
    return context.reshape(fresh_len, -1).astype(jnp.bfloat16)


def widen_rows(normed, widen_weight, widen_bias):
    widened = jnp.dot(normed, widen_weight, preferred_element_type=jnp.float32) + widen_bias.astype(
        jnp.float32
    )
    return jax.nn.gelu(widened, approximate=False).astype(jnp.bfloat16)


def on_device(
    hidden_in,
    cache_keys,
    cache_values,
    cache_lengths,
    owner_order,
    request_slot,
    proj_weight,
    proj_bias,
    output_weight,
    output_bias,
    norm_gains,
    norm_biases,
    widen_weight,
    widen_bias,
    narrow_weight,
    narrow_bias,
):
    slot_count = cache_keys.shape[0]
    fresh_len = hidden_in.shape[1] * lax.axis_size("req")
    owned_slots = lax.dynamic_slice_in_dim(
        owner_order, lax.axis_index("req") * slot_count, slot_count
    )
    lengths = jnp.take(cache_lengths, owned_slots)
    gathered = lax.all_gather(hidden_in, "tp", axis=2, tiled=True)
    token_rows = lax.all_to_all(
        jnp.take(gathered, owner_order, axis=0), "req", split_axis=0, concat_axis=1, tiled=True
    )
    flat_rows = token_rows.reshape(slot_count * fresh_len, -1)
    projected = (
        jnp.einsum("td,cdf->ctf", flat_rows, proj_weight, preferred_element_type=jnp.float32)
        + proj_bias.astype(jnp.float32)[:, None, :]
    )
    query_rows = (
        (projected[0] * HD ** (-0.5)).astype(jnp.bfloat16).reshape(slot_count, fresh_len, -1)
    )
    key_rows = projected[1].astype(jnp.bfloat16).reshape(slot_count, fresh_len, -1)
    value_rows = projected[2].astype(jnp.bfloat16).reshape(slot_count, fresh_len, -1)
    new_cache = jnp.stack([key_rows, value_rows], axis=0)
    context = lax.map(
        slot_attention, (query_rows, key_rows, value_rows, cache_keys, cache_values, lengths)
    )
    context = context.reshape(slot_count * fresh_len, -1)
    tp_count = lax.axis_size("tp")
    attended = lax.psum(
        jnp.dot(context, output_weight, preferred_element_type=jnp.float32).astype(jnp.bfloat16),
        "tp",
    ).astype(jnp.float32)
    normed = layer_norm(
        flat_rows.astype(jnp.float32) + attended + output_bias.astype(jnp.float32),
        norm_gains[0],
        norm_biases[0],
    ).astype(jnp.bfloat16)
    activated = widen_rows(normed, widen_weight, widen_bias)
    fed_total = lax.psum(
        jnp.dot(activated, narrow_weight, preferred_element_type=jnp.float32).astype(jnp.bfloat16),
        "tp",
    ).astype(jnp.float32)
    updated = layer_norm(
        normed.astype(jnp.float32) + fed_total + narrow_bias.astype(jnp.float32),
        norm_gains[1],
        norm_biases[1],
    ).astype(jnp.bfloat16)
    column_count = updated.shape[1] // tp_count
    updated = lax.dynamic_slice_in_dim(
        updated, lax.axis_index("tp") * column_count, column_count, 1
    )
    returned = lax.all_to_all(
        updated.reshape(slot_count, fresh_len, -1), "req", split_axis=1, concat_axis=0, tiled=True
    )
    hidden_out = jnp.take(returned, request_slot, axis=0)
    return (hidden_out, new_cache)


def solution(mesh):
    in_specs = (
        P(None, "req", "tp"),
        P("req", None, "tp"),
        P("req", None, "tp"),
        P(),
        P(),
        P(),
        P(None, None, "tp"),
        P(None, "tp"),
        P("tp", None),
        P(),
        P(),
        P(),
        P(None, "tp"),
        P("tp"),
        P("tp", None),
        P(),
    )
    out_specs = (P(None, "req", "tp"), P(None, "req", None, "tp"))
    return jax.shard_map(
        on_device, mesh=mesh, in_specs=in_specs, out_specs=out_specs, check_vma=False
    )
```

profile of v0, /device:TPU:1, one launch (start us, length us, event | category | flops | bytes accessed | tf_op | source)
XLA Modules:
  0.0 282.1 jit_solution(11562906684038777593)
XLA Ops:
  7.2 0.7 all-gather.2.cloned.1.call-update
  7.9 0.7 compare_select_fusion
  8.6 0.7 compare_and_fusion
  9.2 35.4 %all-gather.2.cloned.1.call-done = bf16[64,8,1024]{2,1,0:T(8,128)(2,1)} async-done(((bf16[64,8,128]{2,1,0:T(8,128)(2,1)}), bf16[64,8,1024]{2,1,0:T(8,128)(2,1)}) %all-gather.2.cloned.1.call-update) | async-done | bytes 1048592 | tf_op jit(solution)/shard_map/all_gather | solution.py:107
  44.6 1.8 gather_fusion
  46.5 1.1 broadcast_select_fusion
  47.6 13.1 %all-to-all-start = ((bf16[64,8,1024]{2,1,0:T(8,128)(2,1)}), bf16[64,8,1024]{2,1,0:T(8,128)(2,1)S(1)}, u32[]{:S(2)}, u32[]{:S(2)}) async-start(bf16[64,8,1024]{2,1,0:T(8,128)(2,1)} %broadcast_select_fusion), calls=%async_computation | async-start | bytes 2097152 | tf_op jit(solution)/shard_map/all_to_all | solution.py:108
  61.0 0.6 dynamic_slice.20
  63.5 1.4 copy.36
  64.9 0.8 copy.38
  65.7 0.7 dynamic-slice.5
  67.1 20.8 %all-to-all-done = bf16[64,8,1024]{2,1,0:T(8,128)(2,1)S(1)} async-done(((bf16[64,8,1024]{2,1,0:T(8,128)(2,1)}), bf16[64,8,1024]{2,1,0:T(8,128)(2,1)S(1)}, u32[]{:S(2)}, u32[]{:S(2)}) %all-to-all-start) | async-done | bytes 1048608 | tf_op jit(solution)/shard_map/all_to_all | solution.py:108
  87.9 0.6 fusion.16
  89.3 0.6 select_reduce_fusion.1
  89.9 0.6 convolution_bitcast_fusion
  90.5 0.9 fusion.2
  91.4 0.7 fusion.10
  92.3 1.5 convolution_convert_fusion
  94.2 69.0 %all-reduce.3.cloned.1.call-done = bf16[512,1024]{1,0:T(8,128)(2,1)} async-done(((bf16[512,1024]{1,0:T(8,128)(2,1)}), bf16[512,1024]{1,0:T(8,128)(2,1)}) %all-reduce.3.cloned.1.call-update) | async-done | bytes 1048592 | tf_op jit(solution)/shard_map/psum | solution.py:127
  163.2 1.7 fusion.6
  165.5 0.6 add_convert_fusion
  166.1 5.6 %convolution_convert_fusion.1 = bf16[512,1024]{1,0:T(8,128)(2,1)} fusion(bf16[512,1024]{1,0:T(8,128)(2,1)S(1)} %copy-done, bf16[512,1024]{1,0:T(8,128)(2,1)S(1)} %add_convert_fusion, bf16[1024,512]{1,0:T(8,128)(2,1)} %param.28, f32[512]{0:T(512)S(1)} %convert_element_type.122), kind=kOutput, calls=%fused_computation.20 | convolution fusion | flops 1091567616 | bytes 4196352 | tf_op jit(solution)/shard_map/dot_general | solution.py:138
  172.0 72.7 %all-reduce.5.cloned.1.call-done = bf16[512,1024]{1,0:T(8,128)(2,1)} async-done(((bf16[512,1024]{1,0:T(8,128)(2,1)}), bf16[512,1024]{1,0:T(8,128)(2,1)}) %all-reduce.5.cloned.1.call-update) | async-done | bytes 1048592 | tf_op jit(solution)/shard_map/psum | solution.py:137
  244.7 1.7 fusion.1
  246.4 0.6 multiply_reduce_fusion
  247.9 1.4 reduce
  249.3 0.7 reshape.238
  250.0 12.5 %all-to-all-start.1 = ((bf16[64,2,512]{2,1,0:T(2,128)(2,1)}), bf16[64,2,512]{2,1,0:T(2,128)(2,1)S(1)}, u32[]{:S(2)}, u32[]{:S(2)}) async-start(bf16[64,2,512]{2,1,0:T(2,128)(2,1)} %reshape.238), calls=%async_computation.1 | async-start | bytes 262144 | tf_op jit(solution)/shard_map/all_to_all | solution.py:150
  262.6 0.8 copy.42
  263.4 10.6 %all-to-all-done.1 = bf16[64,2,512]{2,1,0:T(2,128)(2,1)S(1)} async-done(((bf16[64,2,512]{2,1,0:T(2,128)(2,1)}), bf16[64,2,512]{2,1,0:T(2,128)(2,1)S(1)}, u32[]{:S(2)}, u32[]{:S(2)}) %all-to-all-start.1) | async-done | bytes 131104 | tf_op jit(solution)/shard_map/all_to_all | solution.py:150
  274.1 0.6 gather_fusion.1
  274.8 0.8 broadcast_select_fusion.1
  (69 shorter events, 3.4 us)
Async XLA Ops:
  7.2 158.9 %copy-start = (bf16[512,1024]{1,0:T(8,128)(2,1)S(1)}, bf16[512,1024]{1,0:T(8,128)(2,1)}, u32[]{:S(2)}) copy-start(bf16[512,1024]{1,0:T(8,128)(2,1)} %param.30) | copy-start | bytes 3145732
  7.2 37.4 %all-gather.2.cloned.1.call-start = ((), (), s32[]{:S(2)}) async-start(), calls=%async_computation.2 | async-start | bytes 1179648 | tf_op jit(solution)/shard_map/all_gather | solution.py:107
  46.4 14.4 %copy-start.5 = (bf16[1,512,128]{2,1,0:T(8,128)(2,1)S(1)}, bf16[1,512,128]{2,1,0:T(8,128)(2,1)}, u32[]{:S(2)}) copy-start(bf16[1,512,128]{2,1,0:T(8,128)(2,1)} %param.18) | copy-start | bytes 393220
  46.5 14.5 %copy-start.13 = (s32[64]{0:T(128)S(1)}, s32[64]{0:T(128)}, u32[]{:S(2)}) copy-start(s32[64]{0:T(128)} %param.20) | copy-start | bytes 772
  47.6 17.3 %copy-start.11 = (bf16[3,128]{1,0:T(4,128)(2,1)S(1)}, bf16[3,128]{1,0:T(4,128)(2,1)}, u32[]{:S(2)}) copy-start(bf16[3,128]{1,0:T(4,128)(2,1)} %param.23) | copy-start | bytes 2308
  47.6 17.3 %copy-start.6 = (bf16[1,512,128]{2,1,0:T(8,128)(2,1)S(1)}, bf16[1,512,128]{2,1,0:T(8,128)(2,1)}, u32[]{:S(2)}) copy-start(bf16[1,512,128]{2,1,0:T(8,128)(2,1)} %param.17) | copy-start | bytes 393220
  47.6 18.1 %copy-start.14 = (s32[64]{0:T(128)S(1)}, s32[64]{0:T(128)}, u32[]{:S(2)}) copy-start(s32[64]{0:T(128)} %param.19) | copy-start | bytes 772
  47.6 40.3 %all-to-all-start = ((bf16[64,8,1024]{2,1,0:T(8,128)(2,1)}), bf16[64,8,1024]{2,1,0:T(8,128)(2,1)S(1)}, u32[]{:S(2)}, u32[]{:S(2)}) async-start(bf16[64,8,1024]{2,1,0:T(8,128)(2,1)} %broadcast_select_fusion), calls=%async_computation | async-start | bytes 2097152 | tf_op jit(solution)/shard_map/all_to_all | solution.py:108
  60.8 102.4 %all-reduce.3.cloned.1.call-start = ((), (), s32[]{:S(2)}) async-start(), calls=%async_computation.3 | async-start | bytes 2097152 | tf_op jit(solution)/shard_map/psum | solution.py:127
  87.9 0.9 copy-start.3
  91.4 1.0 copy-start.4
  92.1 2.0 copy-start.9
  92.1 2.0 copy-start.12
  92.1 2.0 copy-start.7
  92.1 2.0 copy-start.8
  93.8 150.8 %all-reduce.5.cloned.1.call-start = ((), (), s32[]{:S(2)}) async-start(), calls=%async_computation.4 | async-start | bytes 2097152 | tf_op jit(solution)/shard_map/psum | solution.py:137
  163.2 1.7 copy-start.1
  166.1 5.7 %copy-start.10 = (bf16[1024]{0:T(1024)(128)(2,1)S(1)}, bf16[1024]{0:T(1024)(128)(2,1)}, u32[]{:S(2)}) copy-start(bf16[1024]{0:T(1024)(128)(2,1)} %param.31) | copy-start | bytes 6148
  166.1 5.9 %copy-start.15 = (s32[64]{0:T(128)S(1)}, s32[64]{0:T(128)}, u32[]{:S(2)}) copy-start(s32[64]{0:T(128)} %param.21) | copy-start | bytes 772
  244.7 1.7 copy-start.2
  250.0 24.0 %all-to-all-start.1 = ((bf16[64,2,512]{2,1,0:T(2,128)(2,1)}), bf16[64,2,512]{2,1,0:T(2,128)(2,1)S(1)}, u32[]{:S(2)}, u32[]{:S(2)}) async-start(bf16[64,2,512]{2,1,0:T(2,128)(2,1)} %reshape.238), calls=%async_computation.1 | async-start | bytes 262144 | tf_op jit(solution)/shard_map/all_to_all | solution.py:150
Sparse Core Ops, SparseCore 0:
  10.1 34.4 all-gather.1
  93.9 69.1 all-reduce.2
  171.9 72.6 all-reduce.4
where the time goes:
time: 284 us; the launch traced here: 282 us
  waiting for transfers between devices  209 us (74%)
  starting transfers between devices  25.9 us (9%)
  between operations  16.8 us (6%)
  other arithmetic  11.2 us (4%)
  matrix products  10 us (4%)
  local copies, waits for them, and re-layouts  8.95 us (3%)
    psum x1, waiting for transfers between devices, on_device(): lax.psum(jnp.dot(activated, narrow_weight, preferred_element_type=jnp.flo...  72.7 us
    psum x1, waiting for transfers between devices, on_device(): lax.psum(jnp.dot(context, output_weight, preferred_element_type=jnp.float...  69 us
    all_gather x1, waiting for transfers between devices, on_device(): gathered = lax.all_gather(hidden_in, 'tp', axis=2, tiled=True)  35.4 us
    all_to_all x1, waiting for transfers between devices, on_device(): lax.all_to_all(jnp.take(gathered, owner_order, axis=0), 'req', split_axis...  20.8 us
    all_to_all x1, starting transfers between devices, on_device(): lax.all_to_all(jnp.take(gathered, owner_order, axis=0), 'req', split_axis...  13.1 us
    all_to_all x1, starting transfers between devices, on_device(): lax.all_to_all(updated.reshape(slot_count, fresh_len, -1), 'req', split_a...  12.5 us
    all_to_all x1, waiting for transfers between devices, on_device(): lax.all_to_all(updated.reshape(slot_count, fresh_len, -1), 'req', split_a...  10.6 us
  transfers between devices with their start and end apart: 5, of which 5 were waited for; matrix products, arithmetic and copies ran while one was open for 2% of the time, Pallas kernels for 0%

commit v1 on v0

v1 whole, which is shorter than its diff:
```python
import jax
import jax.numpy as jnp
from jax import lax
from jax.sharding import PartitionSpec as P

HD = 64


def layer_norm(values, scale_row, shift_row):
    average = jnp.mean(values, axis=-1, keepdims=True)
    centred = values - average
    spread = jnp.mean(centred * centred, axis=-1, keepdims=True)
    return centred * lax.rsqrt(spread + 1e-05) * scale_row.astype(jnp.float32) + shift_row.astype(
        jnp.float32
    )


def split_heads(rows_block):
    return rows_block.reshape(rows_block.shape[0], -1, HD)


def block_scores(query_heads, keys_block, allowed):
    scores = jnp.einsum(
        "thd,shd->hts", query_heads, split_heads(keys_block), preferred_element_type=jnp.float32
    )
    return jnp.where(allowed[None], scores, -jnp.inf)


def to_rows(factor):
    return jnp.transpose(factor, (1, 0, 2))


def slot_attention(query_rows, key_rows, value_rows, slot_keys, slot_values, length):
    fresh_len = query_rows.shape[0]
    block_len = min(512, slot_keys.shape[0])
    block_count = slot_keys.shape[0] // block_len
    query_heads = split_heads(query_rows)
    self_mask = jnp.arange(fresh_len)[:, None] >= jnp.arange(fresh_len)[None, :]
    self_scores = block_scores(query_heads, key_rows, self_mask)
    row_top = jnp.max(self_scores, axis=2, keepdims=True)
    raised = jnp.exp(self_scores - row_top)
    row_total = jnp.sum(raised, axis=2, keepdims=True)
    context = jnp.einsum(
        "hts,shd->thd",
        raised.astype(jnp.bfloat16),
        split_heads(value_rows),
        preferred_element_type=jnp.float32,
    )
    positions = jnp.arange(block_len)

    def one_block(number, carry):
        old_top, old_total, running = carry
        begin_at = number * block_len
        keys_block = lax.dynamic_slice_in_dim(slot_keys, begin_at, block_len)
        values_block = lax.dynamic_slice_in_dim(slot_values, begin_at, block_len)
        allowed = jnp.broadcast_to((begin_at + positions < length)[None, :], (fresh_len, block_len))
        scores = block_scores(query_heads, keys_block, allowed)
        new_top = jnp.maximum(old_top, jnp.max(scores, axis=2, keepdims=True))
        factor = jnp.exp(old_top - new_top)
        block_raised = jnp.exp(scores - new_top)
        new_total = old_total * factor + jnp.sum(block_raised, axis=2, keepdims=True)
        added = jnp.einsum(
            "hts,shd->thd",
            block_raised.astype(jnp.bfloat16),
            split_heads(values_block),
            preferred_element_type=jnp.float32,
        )
        return (new_top, new_total, running * to_rows(factor) + added)

    row_top, row_total, context = lax.fori_loop(
        0, block_count, one_block, (row_top, row_total, context)
    )
    context = context / to_rows(row_total)
    return context.reshape(fresh_len, -1).astype(jnp.bfloat16)


def gather_tp(block, tp_count, axis):
    copies = jnp.broadcast_to(
        jnp.expand_dims(block, axis), block.shape[:axis] + (tp_count,) + block.shape[axis:]
    )
    got = lax.all_to_all(copies, "tp", axis, axis, tiled=True)
    return got.reshape(block.shape[:axis] + (-1,) + block.shape[axis + 1 :])


def reduce_tp(partial, tp_count):
    rows = partial.shape[0] // tp_count
    got = lax.all_to_all(partial.reshape(tp_count, rows, -1), "tp", 0, 0, tiled=True)
    return jnp.sum(got.astype(jnp.float32), axis=0)


def on_device(
    hidden_in,
    cache_keys,
    cache_values,
    cache_lengths,
    owner_order,
    request_slot,
    proj_weight,
    proj_bias,
    output_weight,
    output_bias,
    norm_gains,
    norm_biases,
    widen_weight,
    widen_bias,
    narrow_weight,
    narrow_bias,
):
    tp_count = lax.axis_size("tp")
    tp_index = lax.axis_index("tp")
    slot_index = lax.axis_index("req")
    length = cache_lengths[owner_order[slot_index]]
    own_cols = lax.all_to_all(
        jnp.take(hidden_in, owner_order, axis=0), "req", split_axis=0, concat_axis=1, tiled=True
    )[0]
    fresh_len = own_cols.shape[0]
    width = own_cols.shape[1] * tp_count
    token_rows = gather_tp(own_cols, tp_count, 1)
    projected = (
        jnp.einsum("td,cdf->ctf", token_rows, proj_weight, preferred_element_type=jnp.float32)
        + proj_bias.astype(jnp.float32)[:, None, :]
    )
    query_rows = (projected[0] * HD ** (-0.5)).astype(jnp.bfloat16)
    key_rows = projected[1].astype(jnp.bfloat16)
    value_rows = projected[2].astype(jnp.bfloat16)
    new_cache = jnp.stack([key_rows, value_rows], axis=0)[:, None]
    context = slot_attention(
        query_rows, key_rows, value_rows, cache_keys[0], cache_values[0], length
    )
    rows = fresh_len // tp_count
    own_rows = lax.dynamic_slice_in_dim(token_rows, tp_index * rows, rows)
    attended = reduce_tp(
        jnp.dot(context, output_weight, preferred_element_type=jnp.float32).astype(jnp.bfloat16),
        tp_count,
    )
    normed = layer_norm(
        own_rows.astype(jnp.float32) + attended + output_bias.astype(jnp.float32),
        norm_gains[0],
        norm_biases[0],
    ).astype(jnp.bfloat16)
    normed_all = gather_tp(normed, tp_count, 0)
    widened = jnp.dot(normed_all, widen_weight, preferred_element_type=jnp.float32) + widen_bias.astype(
        jnp.float32
    )
    activated = jax.nn.gelu(widened, approximate=False).astype(jnp.bfloat16)
    fed_total = reduce_tp(
        jnp.dot(activated, narrow_weight, preferred_element_type=jnp.float32).astype(jnp.bfloat16),
        tp_count,
    )
    updated = layer_norm(
        normed.astype(jnp.float32) + fed_total + narrow_bias.astype(jnp.float32),
        norm_gains[1],
        norm_biases[1],
    ).astype(jnp.bfloat16)
    by_cols = lax.all_to_all(
        updated.reshape(rows, tp_count, width // tp_count), "tp", 1, 0, tiled=True
    ).reshape(fresh_len, width // tp_count)
    returned = lax.all_to_all(by_cols[None], "req", split_axis=1, concat_axis=0, tiled=True)
    hidden_out = jnp.take(returned, request_slot, axis=0)
    return (hidden_out, new_cache)


def solution(mesh):
    in_specs = (
        P(None, "req", "tp"),
        P("req", None, "tp"),
        P("req", None, "tp"),
        P(),
        P(),
        P(),
        P(None, None, "tp"),
        P(None, "tp"),
        P("tp", None),
        P(),
        P(),
        P(),
        P(None, "tp"),
        P("tp"),
        P("tp", None),
        P(),
    )
    out_specs = (P(None, "req", "tp"), P(None, "req", None, "tp"))
    return jax.shard_map(
        on_device, mesh=mesh, in_specs=in_specs, out_specs=out_specs, check_vma=False
    )
```

time: 284 us -> 163 us (0.57)
  waiting for transfers between devices: 209 us -> 69.3 us
  blocking collectives: 0 us -> 28.4 us
  between operations: 16.8 us -> 2.92 us
  starting transfers between devices: 25.9 us -> 28.9 us
    psum x2 -> x0, waiting for transfers between devices: 142 us -> none  [the longest x1 72.7 us: on_device(): lax.psum(jnp.dot(activated, narrow_weight, preferred_element_type=jnp.flo...]
    all_to_all x2 -> x6, waiting for transfers between devices: 31.4 us -> 69.3 us  [the longest x2 28.7 us: reduce_tp(): lax.all_to_all(partial.reshape(tp_count, rows, -1), 'tp', 0, 0, tiled=True)]
    all_gather x1 -> x0, waiting for transfers between devices: 35.4 us -> none  [on_device(): gathered = lax.all_gather(hidden_in, 'tp', axis=2, tiled=True)]
    all_to_all x0 -> x1, blocking collectives: none -> 28.4 us  [on_device(): lax.all_to_all(jnp.take(hidden_in, owner_order, axis=0), 'req', split_axi...]
    all_to_all x2 -> x6, starting transfers between devices: 25.6 us -> 28.9 us  [the longest x2 11 us: gather_tp(): got = lax.all_to_all(copies, 'tp', axis, axis, tiled=True)]
  transfers between devices with their start and end apart: 5 -> 6, of which waited for: 5 -> 6; matrix products, arithmetic and copies ran while one was open for 2% -> 3% of each run, Pallas kernels for 0% -> 0%
where the time goes in v1:
time: 163 us; the launch traced here: 162 us
  waiting for transfers between devices  69.3 us (43%)
  starting transfers between devices  28.9 us (18%)
  blocking collectives  28.4 us (17%)
  matrix products  11.1 us (7%)
  local copies, waits for them, and re-layouts  10.9 us (7%)
  other arithmetic  10.3 us (6%)
  between operations  2.92 us (2%)
    all_to_all x2, waiting for transfers between devices, reduce_tp(): lax.all_to_all(partial.reshape(tp_count, rows, -1), 'tp', 0, 0, tiled=True)  28.7 us
    all_to_all x1, blocking collectives, on_device(): lax.all_to_all(jnp.take(hidden_in, owner_order, axis=0), 'req', split_axi...  28.4 us
    all_to_all x2, waiting for transfers between devices, gather_tp(): got = lax.all_to_all(copies, 'tp', axis, axis, tiled=True)  24.6 us
    all_to_all x2, starting transfers between devices, gather_tp(): got = lax.all_to_all(copies, 'tp', axis, axis, tiled=True)  11 us
    all_to_all x1, waiting for transfers between devices, on_device(): lax.all_to_all(by_cols[None], 'req', split_axis=1, concat_axis=0, tiled=T...  10.7 us
    all_to_all x2, starting transfers between devices, reduce_tp(): lax.all_to_all(partial.reshape(tp_count, rows, -1), 'tp', 0, 0, tiled=True)  8.98 us
    dot_general x1, matrix products, on_device(): jnp.dot(activated, narrow_weight, preferred_element_type=jnp.float32)  5.61 us
    all_to_all x1, waiting for transfers between devices, on_device(): lax.all_to_all(updated.reshape(rows, tp_count, width // tp_count), 'tp',...  5.26 us
  transfers between devices with their start and end apart: 6, of which 6 were waited for; matrix products, arithmetic and copies ran while one was open for 3% of the time, Pallas kernels for 0%

profile of v1, /device:TPU:1, one launch (start us, length us, event | category | flops | bytes accessed | tf_op | source)
XLA Modules:
  0.0 161.8 jit_solution(2738835346656741920)
XLA Ops:
  0.7 0.8 compare_select_fusion.1
  2.1 1.5 gather_fusion
  3.8 28.4 %all_to_all.56 = bf16[64,8,128]{2,1,0:T(8,128)(2,1)S(1)} all-to-all(bf16[64,8,128]{2,1,0:T(8,128)(2,1)S(1)} %broadcast_select_fusion.1), channel_id=1, replica_groups=mesh['req'=64,'tp'=8] {'req'}, dimensions={0} | all-to-all | bytes 262144 | tf_op jit(solution)/shard_map/all_to_all | solution.py:113
  32.2 1.1 broadcast_in_dim.77
  33.4 6.6 %all-to-all-start.1 = ((bf16[512,8,128]{2,0,1:T(8,128)(2,1)}), bf16[512,8,128]{2,0,1:T(8,128)(2,1)S(1)}, u32[]{:S(2)}, u32[]{:S(2)}) async-start(bf16[512,8,128]{2,0,1:T(8,128)(2,1)} %broadcast_in_dim.77), calls=%async_computation.1 | async-start | bytes 2097152 | tf_op jit(solution)/shard_map/all_to_all | solution.py:81
  41.9 1.2 copy.41
  45.3 9.6 %all-to-all-done.1 = bf16[512,8,128]{2,0,1:T(8,128)(2,1)S(1)} async-done(((bf16[512,8,128]{2,0,1:T(8,128)(2,1)}), bf16[512,8,128]{2,0,1:T(8,128)(2,1)S(1)}, u32[]{:S(2)}, u32[]{:S(2)}) %all-to-all-start.1) | async-done | bytes 1048608 | tf_op jit(solution)/shard_map/all_to_all | solution.py:81
  54.9 1.7 %fusion.96 = f32[512,384]{0,1:S(1)} fusion(bf16[1024,384]{0,1:T(8,128)(2,1)} %bitcast.109, bf16[512,8,128]{2,0,1:T(8,128)(2,1)S(1)} %all-to-all-done.1), kind=kOutput, calls=%fused_computation.151 | convolution fusion | flops 402653184 | bytes 2621440
  58.0 0.9 fusion
  59.5 0.7 fusion.7
  60.4 1.4 convolution_convert_fusion
  61.8 4.4 %all-to-all-start.2 = ((bf16[8,64,1024]{2,1,0:T(8,128)(2,1)}), bf16[8,64,1024]{2,1,0:T(8,128)(2,1)S(1)}, u32[]{:S(2)}, u32[]{:S(2)}) async-start(bf16[8,64,1024]{2,1,0:T(8,128)(2,1)} %bitcast.102), calls=%async_computation.2 | async-start | bytes 2097152 | tf_op jit(solution)/shard_map/all_to_all | solution.py:87
  66.3 1.2 copy_bitcast_fusion
  67.5 13.7 %all-to-all-done.2 = bf16[8,64,1024]{2,1,0:T(8,128)(2,1)S(1)} async-done(((bf16[8,64,1024]{2,1,0:T(8,128)(2,1)}), bf16[8,64,1024]{2,1,0:T(8,128)(2,1)S(1)}, u32[]{:S(2)}, u32[]{:S(2)}) %all-to-all-start.2) | async-done | bytes 1048608 | tf_op jit(solution)/shard_map/all_to_all | solution.py:87
  81.4 1.0 fusion.60
  82.5 1.1 multiply_reduce_fusion.1
  83.6 1.0 add_convert_fusion.1
  84.7 1.1 broadcast_in_dim.81
  85.8 4.4 %all-to-all-start.3 = ((bf16[8,64,1024]{2,1,0:T(8,128)(2,1)}), bf16[8,64,1024]{2,1,0:T(8,128)(2,1)S(1)}, u32[]{:S(2)}, u32[]{:S(2)}) async-start(bf16[8,64,1024]{2,1,0:T(8,128)(2,1)} %broadcast_in_dim.81), calls=%async_computation.3 | async-start | bytes 2097152 | tf_op jit(solution)/shard_map/all_to_all | solution.py:81
  90.2 15.0 %all-to-all-done.3 = bf16[8,64,1024]{2,1,0:T(8,128)(2,1)S(1)} async-done(((bf16[8,64,1024]{2,1,0:T(8,128)(2,1)}), bf16[8,64,1024]{2,1,0:T(8,128)(2,1)S(1)}, u32[]{:S(2)}, u32[]{:S(2)}) %all-to-all-start.3) | async-done | bytes 1048608 | tf_op jit(solution)/shard_map/all_to_all | solution.py:81
  105.2 5.6 %convolution_convert_fusion.1 = bf16[512,1024]{1,0:T(8,128)(2,1)} fusion(bf16[512,1024]{1,0:T(8,128)(2,1)S(1)} %copy-done, bf16[512,1024]{1,0:T(8,128)(2,1)S(1)} %bitcast.108, bf16[1024,512]{1,0:T(8,128)(2,1)} %param.30, f32[512]{0:T(512)S(1)} %convert_element_type.100), kind=kOutput, calls=%fused_computation.14 | convolution fusion | flops 1091567616 | bytes 4196352 | tf_op jit(solution)/shard_map/dot_general | solution.py:147
  110.8 4.6 %all-to-all-start.4 = ((bf16[8,64,1024]{2,1,0:T(8,128)(2,1)}), bf16[8,64,1024]{2,1,0:T(8,128)(2,1)S(1)}, u32[]{:S(2)}, u32[]{:S(2)}) async-start(bf16[8,64,1024]{2,1,0:T(8,128)(2,1)} %bitcast.27), calls=%async_computation.4 | async-start | bytes 2097152 | tf_op jit(solution)/shard_map/all_to_all | solution.py:87
  115.4 15.0 %all-to-all-done.4 = bf16[8,64,1024]{2,1,0:T(8,128)(2,1)S(1)} async-done(((bf16[8,64,1024]{2,1,0:T(8,128)(2,1)}), bf16[8,64,1024]{2,1,0:T(8,128)(2,1)S(1)}, u32[]{:S(2)}, u32[]{:S(2)}) %all-to-all-start.4) | async-done | bytes 1048608 | tf_op jit(solution)/shard_map/all_to_all | solution.py:87
  130.9 0.8 copy_bitcast_fusion.1
  131.7 4.2 %all-to-all-start.5 = ((bf16[64,8,128]{2,0,1:T(8,128)(2,1)}), bf16[64,8,128]{2,0,1:T(8,128)(2,1)S(1)}, u32[]{:S(2)}, u32[]{:S(2)}) async-start(bf16[64,8,128]{2,0,1:T(8,128)(2,1)} %copy_bitcast_fusion.1), calls=%async_computation.5 | async-start | bytes 262144 | tf_op jit(solution)/shard_map/all_to_all | solution.py:155
  135.9 5.3 %all-to-all-done.5 = bf16[64,8,128]{2,0,1:T(8,128)(2,1)S(1)} async-done(((bf16[64,8,128]{2,0,1:T(8,128)(2,1)}), bf16[64,8,128]{2,0,1:T(8,128)(2,1)S(1)}, u32[]{:S(2)}, u32[]{:S(2)}) %all-to-all-start.5) | async-done | bytes 131104 | tf_op jit(solution)/shard_map/all_to_all | solution.py:155
  141.9 1.4 reduce
  143.3 0.7 reshape.181
  144.0 4.6 %all-to-all-start.6 = ((bf16[64,2,512]{2,1,0:T(2,128)(2,1)}), bf16[64,2,512]{2,1,0:T(2,128)(2,1)S(1)}, u32[]{:S(2)}, u32[]{:S(2)}) async-start(bf16[64,2,512]{2,1,0:T(2,128)(2,1)} %reshape.181), calls=%async_computation.6 | async-start | bytes 262144 | tf_op jit(solution)/shard_map/all_to_all | solution.py:158
  148.7 0.8 copy.48
  149.6 10.7 %all-to-all-done.6 = bf16[64,2,512]{2,1,0:T(2,128)(2,1)S(1)} async-done(((bf16[64,2,512]{2,1,0:T(2,128)(2,1)}), bf16[64,2,512]{2,1,0:T(2,128)(2,1)S(1)}, u32[]{:S(2)}, u32[]{:S(2)}) %all-to-all-start.6) | async-done | bytes 131104 | tf_op jit(solution)/shard_map/all_to_all | solution.py:158
  161.0 0.8 broadcast_select_fusion
  (68 shorter events, 7.3 us)
Async XLA Ops:
  0.6 104.6 %copy-start = (bf16[512,1024]{1,0:T(8,128)(2,1)S(1)}, bf16[512,1024]{1,0:T(8,128)(2,1)}, u32[]{:S(2)}) copy-start(bf16[512,1024]{1,0:T(8,128)(2,1)} %param.32) | copy-start | bytes 3145732
  0.6 39.3 %copy-start.11 = (s32[64]{0:T(128)S(1)}, s32[64]{0:T(128)}, u32[]{:S(2)}) copy-start(s32[64]{0:T(128)} %param.22) | copy-start | bytes 772
  0.7 41.2 %copy-start.1 = (bf16[3,1024,128]{2,1,0:T(8,128)(2,1)S(1)}, bf16[3,1024,128]{2,1,0:T(8,128)(2,1)}, u32[]{:S(2)}) copy-start(bf16[3,1024,128]{2,1,0:T(8,128)(2,1)} %param.24) | copy-start | bytes 2359300
  33.4 9.7 %copy-start.9 = (bf16[3,128]{1,0:T(4,128)(2,1)S(1)}, bf16[3,128]{1,0:T(4,128)(2,1)}, u32[]{:S(2)}) copy-start(bf16[3,128]{1,0:T(4,128)(2,1)} %param.25) | copy-start | bytes 2308
  33.4 9.7 %copy-start.3 = (bf16[1,512,128]{2,1,0:T(8,128)(2,1)S(1)}, bf16[1,512,128]{2,1,0:T(8,128)(2,1)}, u32[]{:S(2)}) copy-start(bf16[1,512,128]{2,1,0:T(8,128)(2,1)} %param.19) | copy-start | bytes 393220
  33.4 9.8 %copy-start.4 = (bf16[1,512,128]{2,1,0:T(8,128)(2,1)S(1)}, bf16[1,512,128]{2,1,0:T(8,128)(2,1)}, u32[]{:S(2)}) copy-start(bf16[1,512,128]{2,1,0:T(8,128)(2,1)} %param.20) | copy-start | bytes 393220
  33.4 10.6 %copy-start.12 = (s32[64]{0:T(128)S(1)}, s32[64]{0:T(128)}, u32[]{:S(2)}) copy-start(s32[64]{0:T(128)} %param.21) | copy-start | bytes 772
  33.4 21.6 %all-to-all-start.1 = ((bf16[512,8,128]{2,0,1:T(8,128)(2,1)}), bf16[512,8,128]{2,0,1:T(8,128)(2,1)S(1)}, u32[]{:S(2)}, u32[]{:S(2)}) async-start(bf16[512,8,128]{2,0,1:T(8,128)(2,1)} %broadcast_in_dim.77), calls=%async_computation.1 | async-start | bytes 2097152 | tf_op jit(solution)/shard_map/all_to_all | solution.py:81
  59.4 1.0 copy-start.2
  60.1 6.1 %copy-start.7 = (bf16[1024]{0:T(1024)(128)(2,1)S(1)}, bf16[1024]{0:T(1024)(128)(2,1)}, u32[]{:S(2)}) copy-start(bf16[1024]{0:T(1024)(128)(2,1)} %param.27) | copy-start | bytes 6148
  60.1 6.1 %copy-start.5 = (bf16[2,1024]{1,0:T(2,128)(2,1)S(1)}, bf16[2,1024]{1,0:T(2,128)(2,1)}, u32[]{:S(2)}) copy-start(bf16[2,1024]{1,0:T(2,128)(2,1)} %param.28) | copy-start | bytes 12292
  60.1 6.1 %copy-start.6 = (bf16[2,1024]{1,0:T(2,128)(2,1)S(1)}, bf16[2,1024]{1,0:T(2,128)(2,1)}, u32[]{:S(2)}) copy-start(bf16[2,1024]{1,0:T(2,128)(2,1)} %param.29) | copy-start | bytes 12292
  61.8 19.4 %all-to-all-start.2 = ((bf16[8,64,1024]{2,1,0:T(8,128)(2,1)}), bf16[8,64,1024]{2,1,0:T(8,128)(2,1)S(1)}, u32[]{:S(2)}, u32[]{:S(2)}) async-start(bf16[8,64,1024]{2,1,0:T(8,128)(2,1)} %bitcast.102), calls=%async_computation.2 | async-start | bytes 2097152 | tf_op jit(solution)/shard_map/all_to_all | solution.py:87
  82.5 7.7 %copy-start.10 = (bf16[512]{0:T(512)(128)(2,1)S(1)}, bf16[512]{0:T(512)(128)(2,1)}, u32[]{:S(2)}) copy-start(bf16[512]{0:T(512)(128)(2,1)} %param.31) | copy-start | bytes 3076
  85.8 19.4 %all-to-all-start.3 = ((bf16[8,64,1024]{2,1,0:T(8,128)(2,1)}), bf16[8,64,1024]{2,1,0:T(8,128)(2,1)S(1)}, u32[]{:S(2)}, u32[]{:S(2)}) async-start(bf16[8,64,1024]{2,1,0:T(8,128)(2,1)} %broadcast_in_dim.81), calls=%async_computation.3 | async-start | bytes 2097152 | tf_op jit(solution)/shard_map/all_to_all | solution.py:81
  110.8 4.6 %copy-start.8 = (bf16[1024]{0:T(1024)(128)(2,1)S(1)}, bf16[1024]{0:T(1024)(128)(2,1)}, u32[]{:S(2)}) copy-start(bf16[1024]{0:T(1024)(128)(2,1)} %param.33) | copy-start | bytes 6148
  110.8 25.1 %copy-start.13 = (s32[64]{0:T(128)S(1)}, s32[64]{0:T(128)}, u32[]{:S(2)}) copy-start(s32[64]{0:T(128)} %param.23) | copy-start | bytes 772
  110.8 19.6 %all-to-all-start.4 = ((bf16[8,64,1024]{2,1,0:T(8,128)(2,1)}), bf16[8,64,1024]{2,1,0:T(8,128)(2,1)S(1)}, u32[]{:S(2)}, u32[]{:S(2)}) async-start(bf16[8,64,1024]{2,1,0:T(8,128)(2,1)} %bitcast.27), calls=%async_computation.4 | async-start | bytes 2097152 | tf_op jit(solution)/shard_map/all_to_all | solution.py:87
  131.7 9.5 %all-to-all-start.5 = ((bf16[64,8,128]{2,0,1:T(8,128)(2,1)}), bf16[64,8,128]{2,0,1:T(8,128)(2,1)S(1)}, u32[]{:S(2)}, u32[]{:S(2)}) async-start(bf16[64,8,128]{2,0,1:T(8,128)(2,1)} %copy_bitcast_fusion.1), calls=%async_computation.5 | async-start | bytes 262144 | tf_op jit(solution)/shard_map/all_to_all | solution.py:155
  144.0 16.2 %all-to-all-start.6 = ((bf16[64,2,512]{2,1,0:T(2,128)(2,1)}), bf16[64,2,512]{2,1,0:T(2,128)(2,1)S(1)}, u32[]{:S(2)}, u32[]{:S(2)}) async-start(bf16[64,2,512]{2,1,0:T(2,128)(2,1)} %reshape.181), calls=%async_computation.6 | async-start | bytes 262144 | tf_op jit(solution)/shard_map/all_to_all | solution.py:158

commit v2 on v1

--- a/solution.py
+++ b/solution.py
@@ -111,15 +111,20 @@
     slot_index = lax.axis_index("req")
     length = cache_lengths[owner_order[slot_index]]
     own_cols = lax.all_to_all(
-        jnp.take(hidden_in, owner_order, axis=0), "req", split_axis=0, concat_axis=1, tiled=True
+        hidden_in.at[owner_order].get(mode="promise_in_bounds", unique_indices=True),
+        "req",
+        split_axis=0,
+        concat_axis=1,
+        tiled=True,
     )[0]
     fresh_len = own_cols.shape[0]
     width = own_cols.shape[1] * tp_count
     token_rows = gather_tp(own_cols, tp_count, 1)
-    projected = (
-        jnp.einsum("td,cdf->ctf", token_rows, proj_weight, preferred_element_type=jnp.float32)
-        + proj_bias.astype(jnp.float32)[:, None, :]
-    )
+    projected = [
+        jnp.dot(token_rows, proj_weight[c], preferred_element_type=jnp.float32)
+        + proj_bias[c].astype(jnp.float32)
+        for c in range(3)
+    ]
     query_rows = (projected[0] * HD ** (-0.5)).astype(jnp.bfloat16)
     key_rows = projected[1].astype(jnp.bfloat16)
     value_rows = projected[2].astype(jnp.bfloat16)
@@ -128,13 +133,16 @@
         query_rows, key_rows, value_rows, cache_keys[0], cache_values[0], length
     )
     rows = fresh_len // tp_count
-    own_rows = lax.dynamic_slice_in_dim(token_rows, tp_index * rows, rows)
+    own_rows = lax.optimization_barrier(
+        lax.dynamic_slice_in_dim(token_rows, tp_index * rows, rows).astype(jnp.float32)
+        + output_bias.astype(jnp.float32)
+    )
     attended = reduce_tp(
         jnp.dot(context, output_weight, preferred_element_type=jnp.float32).astype(jnp.bfloat16),
         tp_count,
     )
     normed = layer_norm(
-        own_rows.astype(jnp.float32) + attended + output_bias.astype(jnp.float32),
+        own_rows + attended,
         norm_gains[0],
         norm_biases[0],
     ).astype(jnp.bfloat16)
@@ -142,7 +150,9 @@
     widened = jnp.dot(normed_all, widen_weight, preferred_element_type=jnp.float32) + widen_bias.astype(
         jnp.float32
     )
-    activated = jax.nn.gelu(widened, approximate=False).astype(jnp.bfloat16)
+    activated = lax.optimization_barrier(
+        jax.nn.gelu(widened, approximate=False).astype(jnp.bfloat16)
+    )
     fed_total = reduce_tp(
         jnp.dot(activated, narrow_weight, preferred_element_type=jnp.float32).astype(jnp.bfloat16),
         tp_count,
@@ -156,7 +166,7 @@
         updated.reshape(rows, tp_count, width // tp_count), "tp", 1, 0, tiled=True
     ).reshape(fresh_len, width // tp_count)
     returned = lax.all_to_all(by_cols[None], "req", split_axis=1, concat_axis=0, tiled=True)
-    hidden_out = jnp.take(returned, request_slot, axis=0)
+    hidden_out = returned.at[request_slot].get(mode="promise_in_bounds", unique_indices=True)
     return (hidden_out, new_cache)
 
 

time: 163 us -> 160 us (0.982)
  blocking collectives: 28.4 us -> 37 us
  other arithmetic: 10.3 us -> 5.37 us
  starting transfers between devices: 28.9 us -> 24.4 us
  waiting for transfers between devices: 69.3 us -> 65.4 us
  matrix products: 11.1 us -> 13.7 us
    all_to_all x1 -> x2, blocking collectives: 28.4 us -> 37 us  [the longest x1 28.4 us: on_device(): lax.all_to_all(hidden_in.at[owner_order].get(mode='promise_in_bounds', un...]
    dot_general x0 -> x4, matrix products: none -> 8.27 us  [the longest x1 4.27 us: on_device(): jnp.dot(normed_all, widen_weight, preferred_element_type=jnp.float32)]
    all_to_all x1 -> x0, waiting for transfers between devices: 5.26 us -> none  [on_device(): lax.all_to_all(updated.reshape(rows, tp_count, width // tp_count), 'tp',...]
    all_to_all x1 -> x0, starting transfers between devices: 4.24 us -> none  [on_device(): lax.all_to_all(updated.reshape(rows, tp_count, width // tp_count), 'tp',...]
    dot_general x1, matrix products: 5.61 us -> 1.68 us  [on_device(): jnp.dot(activated, narrow_weight, preferred_element_type=jnp.float32)]
    unnamed x1 -> x0, matrix products: 1.73 us -> none
    unnamed x36 -> x44, local copies, waits for them, and re-layouts: 3.9 us -> 3.5 us
  transfers between devices with their start and end apart: 6 -> 5, of which waited for: 6 -> 5; matrix products, arithmetic and copies ran while one was open for 3% -> 3% of each run, Pallas kernels for 0% -> 0%
where the time goes in v2:
time: 160 us; the launch traced here: 159 us
  waiting for transfers between devices  65.4 us (41%)
  blocking collectives  37 us (23%)
  starting transfers between devices  24.4 us (15%)
  matrix products  13.7 us (9%)
  local copies, waits for them, and re-layouts  10.5 us (7%)
  other arithmetic  5.37 us (3%)
  between operations  3.05 us (2%)
    all_to_all x2, waiting for transfers between devices, reduce_tp(): lax.all_to_all(partial.reshape(tp_count, rows, -1), 'tp', 0, 0, tiled=True)  29.6 us
    all_to_all x1, blocking collectives, on_device(): lax.all_to_all(hidden_in.at[owner_order].get(mode='promise_in_bounds', un...  28.4 us
    all_to_all x2, waiting for transfers between devices, gather_tp(): got = lax.all_to_all(copies, 'tp', axis, axis, tiled=True)  25.2 us
    all_to_all x2, starting transfers between devices, gather_tp(): got = lax.all_to_all(copies, 'tp', axis, axis, tiled=True)  10.9 us
    all_to_all x1, waiting for transfers between devices, on_device(): lax.all_to_all(by_cols[None], 'req', split_axis=1, concat_axis=0, tiled=T...  10.7 us
    all_to_all x2, starting transfers between devices, reduce_tp(): lax.all_to_all(partial.reshape(tp_count, rows, -1), 'tp', 0, 0, tiled=True)  8.85 us
    all_to_all x1, blocking collectives, on_device(): lax.all_to_all(updated.reshape(rows, tp_count, width // tp_count), 'tp',...  8.59 us
    all_to_all x1, starting transfers between devices, on_device(): lax.all_to_all(by_cols[None], 'req', split_axis=1, concat_axis=0, tiled=T...  4.62 us
  transfers between devices with their start and end apart: 5, of which 5 were waited for; matrix products, arithmetic and copies ran while one was open for 3% of the time, Pallas kernels for 0%

profile of v2, /device:TPU:1, one launch (start us, length us, event | category | flops | bytes accessed | tf_op | source)
XLA Modules:
  0.0 159.4 jit_solution(9914192271503058407)
XLA Ops:
  0.7 0.8 compare_select_fusion.1
  1.4 1.5 gather_fusion
  3.0 28.4 %all_to_all.56 = bf16[64,8,128]{2,1,0:T(8,128)(2,1)S(1)} all-to-all(bf16[64,8,128]{2,1,0:T(8,128)(2,1)S(1)} %gather_fusion), channel_id=1, replica_groups=mesh['req'=64,'tp'=8] {'req'}, dimensions={0} | all-to-all | bytes 262144 | tf_op jit(solution)/shard_map/all_to_all | solution.py:113
  31.4 1.1 broadcast_in_dim.48
  32.5 6.5 %all-to-all-start.1 = ((bf16[512,8,128]{2,0,1:T(8,128)(2,1)}), bf16[512,8,128]{2,0,1:T(8,128)(2,1)S(1)}, u32[]{:S(2)}, u32[]{:S(2)}) async-start(bf16[512,8,128]{2,0,1:T(8,128)(2,1)} %broadcast_in_dim.48), calls=%async_computation.1 | async-start | bytes 2097152 | tf_op jit(solution)/shard_map/all_to_all | solution.py:81
  39.0 0.6 dynamic_slice.14
  40.9 0.8 copy.54
  42.4 0.6 dynamic_slice.15
  43.0 0.6 iota_compare_fusion.1
  43.8 10.2 %all-to-all-done.1 = bf16[512,8,128]{2,0,1:T(8,128)(2,1)S(1)} async-done(((bf16[512,8,128]{2,0,1:T(8,128)(2,1)}), bf16[512,8,128]{2,0,1:T(8,128)(2,1)S(1)}, u32[]{:S(2)}, u32[]{:S(2)}) %all-to-all-start.1) | async-done | bytes 1048608 | tf_op jit(solution)/shard_map/all_to_all | solution.py:81
  54.5 1.3 fusion.10
  55.8 1.3 fusion.8
  57.2 1.3 fusion.9
  59.7 0.9 fusion
  61.1 0.7 fusion.11
  62.0 1.4 convolution_convert_fusion
  63.5 4.4 %all-to-all-start.2 = ((bf16[8,64,1024]{2,1,0:T(8,128)(2,1)}), bf16[8,64,1024]{2,1,0:T(8,128)(2,1)S(1)}, u32[]{:S(2)}, u32[]{:S(2)}) async-start(bf16[8,64,1024]{2,1,0:T(8,128)(2,1)} %bitcast.26), calls=%async_computation.2 | async-start | bytes 2097152 | tf_op jit(solution)/shard_map/all_to_all | solution.py:87
  68.3 14.6 %all-to-all-done.2 = bf16[8,64,1024]{2,1,0:T(8,128)(2,1)S(1)} async-done(((bf16[8,64,1024]{2,1,0:T(8,128)(2,1)}), bf16[8,64,1024]{2,1,0:T(8,128)(2,1)S(1)}, u32[]{:S(2)}, u32[]{:S(2)}) %all-to-all-start.2) | async-done | bytes 1048608 | tf_op jit(solution)/shard_map/all_to_all | solution.py:87
  83.6 1.1 broadcast_in_dim.81
  84.7 4.4 %all-to-all-start.3 = ((bf16[8,64,1024]{2,1,0:T(8,128)(2,1)}), bf16[8,64,1024]{2,1,0:T(8,128)(2,1)S(1)}, u32[]{:S(2)}, u32[]{:S(2)}) async-start(bf16[8,64,1024]{2,1,0:T(8,128)(2,1)} %broadcast_in_dim.81), calls=%async_computation.3 | async-start | bytes 2097152 | tf_op jit(solution)/shard_map/all_to_all | solution.py:81
  89.1 15.0 %all-to-all-done.3 = bf16[8,64,1024]{2,1,0:T(8,128)(2,1)S(1)} async-done(((bf16[8,64,1024]{2,1,0:T(8,128)(2,1)}), bf16[8,64,1024]{2,1,0:T(8,128)(2,1)S(1)}, u32[]{:S(2)}, u32[]{:S(2)}) %all-to-all-start.3) | async-done | bytes 1048608 | tf_op jit(solution)/shard_map/all_to_all | solution.py:81
  104.1 4.3 %fusion.14 = bf16[512,512]{1,0:T(8,128)(2,1)S(1)} fusion(bf16[512,1024]{1,0:T(8,128)(2,1)S(1)} %bitcast.117, bf16[1024,512]{1,0:T(8,128)(2,1)} %param.28, f32[512]{0:T(512)S(1)} %convert_element_type.85), kind=kOutput, calls=%fused_computation.31 | convolution fusion | flops 554172416 | bytes 2623488 | tf_op jit(solution)/shard_map/dot_general | solution.py:150
  108.4 1.7 %convolution_convert_fusion.1 = bf16[512,1024]{1,0:T(8,128)(2,1)} fusion(bf16[512,512]{1,0:T(8,128)(2,1)S(1)} %fusion.14, bf16[512,1024]{1,0:T(8,128)(2,1)S(1)} %copy-done), kind=kOutput, calls=%fused_computation.14 | convolution fusion | flops 537395200 | bytes 2621440 | tf_op jit(solution)/shard_map/dot_general | solution.py:157
  110.1 4.4 %all-to-all-start.4 = ((bf16[8,64,1024]{2,1,0:T(8,128)(2,1)}), bf16[8,64,1024]{2,1,0:T(8,128)(2,1)S(1)}, u32[]{:S(2)}, u32[]{:S(2)}) async-start(bf16[8,64,1024]{2,1,0:T(8,128)(2,1)} %bitcast.30), calls=%async_computation.4 | async-start | bytes 2097152 | tf_op jit(solution)/shard_map/all_to_all | solution.py:87
  114.5 15.0 %all-to-all-done.4 = bf16[8,64,1024]{2,1,0:T(8,128)(2,1)S(1)} async-done(((bf16[8,64,1024]{2,1,0:T(8,128)(2,1)}), bf16[8,64,1024]{2,1,0:T(8,128)(2,1)S(1)}, u32[]{:S(2)}, u32[]{:S(2)}) %all-to-all-start.4) | async-done | bytes 1048608 | tf_op jit(solution)/shard_map/all_to_all | solution.py:87
  130.4 8.6 %all_to_all.57 = bf16[64,8,128]{2,0,1:T(8,128)(2,1)S(1)} all-to-all(bf16[64,8,128]{2,0,1:T(8,128)(2,1)S(1)} %copy_bitcast_fusion), channel_id=1, replica_groups=mesh['req'=64,'tp'=8] {'tp'}, dimensions={1} | all-to-all | bytes 262144 | tf_op jit(solution)/shard_map/all_to_all | solution.py:165
  139.7 1.4 reduce
  141.1 0.7 reshape.173
  141.8 4.6 %all-to-all-start.6 = ((bf16[64,2,512]{2,1,0:T(2,128)(2,1)}), bf16[64,2,512]{2,1,0:T(2,128)(2,1)S(1)}, u32[]{:S(2)}, u32[]{:S(2)}) async-start(bf16[64,2,512]{2,1,0:T(2,128)(2,1)} %reshape.173), calls=%async_computation.6 | async-start | bytes 262144 | tf_op jit(solution)/shard_map/all_to_all | solution.py:168
  146.5 0.8 copy.59
  147.4 10.7 %all-to-all-done.6 = bf16[64,2,512]{2,1,0:T(2,128)(2,1)S(1)} async-done(((bf16[64,2,512]{2,1,0:T(2,128)(2,1)}), bf16[64,2,512]{2,1,0:T(2,128)(2,1)S(1)}, u32[]{:S(2)}, u32[]{:S(2)}) %all-to-all-start.6) | async-done | bytes 131104 | tf_op jit(solution)/shard_map/all_to_all | solution.py:168
  158.2 1.3 gather_fusion.1
  (73 shorter events, 5.4 us)
Async XLA Ops:
  0.6 107.7 %copy-start = (bf16[512,1024]{1,0:T(8,128)(2,1)S(1)}, bf16[512,1024]{1,0:T(8,128)(2,1)}, u32[]{:S(2)}) copy-start(bf16[512,1024]{1,0:T(8,128)(2,1)} %param.30) | copy-start | bytes 3145732
  0.6 38.3 %copy-start.15 = (s32[64]{0:T(128)S(1)}, s32[64]{0:T(128)}, u32[]{:S(2)}) copy-start(s32[64]{0:T(128)} %param.20) | copy-start | bytes 772
  0.7 40.2 %copy-start.5 = (bf16[1,512,128]{2,1,0:T(8,128)(2,1)S(1)}, bf16[1,512,128]{2,1,0:T(8,128)(2,1)}, u32[]{:S(2)}) copy-start(bf16[1,512,128]{2,1,0:T(8,128)(2,1)} %param.17) | copy-start | bytes 393220
  0.7 41.0 %copy-start.6 = (bf16[1,512,128]{2,1,0:T(8,128)(2,1)S(1)}, bf16[1,512,128]{2,1,0:T(8,128)(2,1)}, u32[]{:S(2)}) copy-start(bf16[1,512,128]{2,1,0:T(8,128)(2,1)} %param.18) | copy-start | bytes 393220
  3.0 39.4 %copy-start.16 = (s32[64]{0:T(128)S(1)}, s32[64]{0:T(128)}, u32[]{:S(2)}) copy-start(s32[64]{0:T(128)} %param.19) | copy-start | bytes 772
  31.4 12.3 %copy-start.11 = (bf16[3,128]{1,0:T(4,128)(2,1)S(1)}, bf16[3,128]{1,0:T(4,128)(2,1)}, u32[]{:S(2)}) copy-start(bf16[3,128]{1,0:T(4,128)(2,1)} %param.23) | copy-start | bytes 2308
  32.5 21.4 %all-to-all-start.1 = ((bf16[512,8,128]{2,0,1:T(8,128)(2,1)}), bf16[512,8,128]{2,0,1:T(8,128)(2,1)S(1)}, u32[]{:S(2)}, u32[]{:S(2)}) async-start(bf16[512,8,128]{2,0,1:T(8,128)(2,1)} %broadcast_in_dim.48), calls=%async_computation.1 | async-start | bytes 2097152 | tf_op jit(solution)/shard_map/all_to_all | solution.py:81
  54.5 4.1 %copy-start.3 = (bf16[1,512,128]{1,2,0:T(8,128)(2,1)S(1)}, bf16[1,512,128]{1,2,0:T(8,128)(2,1)}, u32[]{:S(2)}) copy-start(bf16[1,512,128]{1,2,0:T(8,128)(2,1)} %copy.54) | copy-start | bytes 393220
  55.8 3.2 %copy-start.1 = (bf16[512,128]{0,1:T(8,128)(2,1)}, bf16[512,128]{0,1:T(8,128)(2,1)S(1)}, u32[]{:S(2)}) copy-start(bf16[512,128]{0,1:T(8,128)(2,1)S(1)} %fusion.10) | copy-start | bytes 393220
  57.2 4.0 %copy-start.7 = (bf16[512,128]{0,1:T(8,128)(2,1)}, bf16[512,128]{0,1:T(8,128)(2,1)S(1)}, u32[]{:S(2)}) copy-start(bf16[512,128]{0,1:T(8,128)(2,1)S(1)} %fusion.8) | copy-start | bytes 393220
  61.1 1.0 copy-start.4
  61.8 6.1 %copy-start.12 = (bf16[1024]{0:T(1024)(128)(2,1)S(1)}, bf16[1024]{0:T(1024)(128)(2,1)}, u32[]{:S(2)}) copy-start(bf16[1024]{0:T(1024)(128)(2,1)} %param.25) | copy-start | bytes 6148
  61.8 6.1 %copy-start.9 = (bf16[2,1024]{1,0:T(2,128)(2,1)S(1)}, bf16[2,1024]{1,0:T(2,128)(2,1)}, u32[]{:S(2)}) copy-start(bf16[2,1024]{1,0:T(2,128)(2,1)} %param.26) | copy-start | bytes 12292
  61.8 6.1 %copy-start.10 = (bf16[2,1024]{1,0:T(2,128)(2,1)S(1)}, bf16[2,1024]{1,0:T(2,128)(2,1)}, u32[]{:S(2)}) copy-start(bf16[2,1024]{1,0:T(2,128)(2,1)} %param.27) | copy-start | bytes 12292
  63.5 19.4 %all-to-all-start.2 = ((bf16[8,64,1024]{2,1,0:T(8,128)(2,1)}), bf16[8,64,1024]{2,1,0:T(8,128)(2,1)S(1)}, u32[]{:S(2)}, u32[]{:S(2)}) async-start(bf16[8,64,1024]{2,1,0:T(8,128)(2,1)} %bitcast.26), calls=%async_computation.2 | async-start | bytes 2097152 | tf_op jit(solution)/shard_map/all_to_all | solution.py:87
  83.2 5.9 %copy-start.14 = (bf16[512]{0:T(512)(128)(2,1)S(1)}, bf16[512]{0:T(512)(128)(2,1)}, u32[]{:S(2)}) copy-start(bf16[512]{0:T(512)(128)(2,1)} %param.29) | copy-start | bytes 3076
  84.7 19.4 %all-to-all-start.3 = ((bf16[8,64,1024]{2,1,0:T(8,128)(2,1)}), bf16[8,64,1024]{2,1,0:T(8,128)(2,1)S(1)}, u32[]{:S(2)}, u32[]{:S(2)}) async-start(bf16[8,64,1024]{2,1,0:T(8,128)(2,1)} %broadcast_in_dim.81), calls=%async_computation.3 | async-start | bytes 2097152 | tf_op jit(solution)/shard_map/all_to_all | solution.py:81
  108.4 6.1 %copy-start.13 = (bf16[1024]{0:T(1024)(128)(2,1)S(1)}, bf16[1024]{0:T(1024)(128)(2,1)}, u32[]{:S(2)}) copy-start(bf16[1024]{0:T(1024)(128)(2,1)} %param.31) | copy-start | bytes 6148
  110.1 19.4 %all-to-all-start.4 = ((bf16[8,64,1024]{2,1,0:T(8,128)(2,1)}), bf16[8,64,1024]{2,1,0:T(8,128)(2,1)S(1)}, u32[]{:S(2)}, u32[]{:S(2)}) async-start(bf16[8,64,1024]{2,1,0:T(8,128)(2,1)} %bitcast.30), calls=%async_computation.4 | async-start | bytes 2097152 | tf_op jit(solution)/shard_map/all_to_all | solution.py:87
  114.5 31.9 %copy-start.17 = (s32[64]{0:T(128)S(1)}, s32[64]{0:T(128)}, u32[]{:S(2)}) copy-start(s32[64]{0:T(128)} %param.21) | copy-start | bytes 772
  114.5 32.0 %copy-start.2 = (bf16[512,128]{0,1:T(8,128)(2,1)S(1)}, bf16[512,128]{0,1:T(8,128)(2,1)}, u32[]{:S(2)}) copy-start(bf16[512,128]{0,1:T(8,128)(2,1)} %copy-done.1) | copy-start | bytes 393220
  114.5 32.0 %copy-start.8 = (bf16[512,128]{0,1:T(8,128)(2,1)S(1)}, bf16[512,128]{0,1:T(8,128)(2,1)}, u32[]{:S(2)}) copy-start(bf16[512,128]{0,1:T(8,128)(2,1)} %copy-done.7) | copy-start | bytes 393220
  141.8 16.2 %all-to-all-start.6 = ((bf16[64,2,512]{2,1,0:T(2,128)(2,1)}), bf16[64,2,512]{2,1,0:T(2,128)(2,1)S(1)}, u32[]{:S(2)}, u32[]{:S(2)}) async-start(bf16[64,2,512]{2,1,0:T(2,128)(2,1)} %reshape.173), calls=%async_computation.6 | async-start | bytes 262144 | tf_op jit(solution)/shard_map/all_to_all | solution.py:168

commit v3 on v2

--- a/solution.py
+++ b/solution.py
@@ -120,11 +120,10 @@
     fresh_len = own_cols.shape[0]
     width = own_cols.shape[1] * tp_count
     token_rows = gather_tp(own_cols, tp_count, 1)
-    projected = [
-        jnp.dot(token_rows, proj_weight[c], preferred_element_type=jnp.float32)
-        + proj_bias[c].astype(jnp.float32)
-        for c in range(3)
-    ]
+    projected = (
+        jnp.einsum("td,cdf->ctf", token_rows, proj_weight, preferred_element_type=jnp.float32)
+        + proj_bias.astype(jnp.float32)[:, None, :]
+    )
     query_rows = (projected[0] * HD ** (-0.5)).astype(jnp.bfloat16)
     key_rows = projected[1].astype(jnp.bfloat16)
     value_rows = projected[2].astype(jnp.bfloat16)
@@ -153,19 +152,31 @@
     activated = lax.optimization_barrier(
         jax.nn.gelu(widened, approximate=False).astype(jnp.bfloat16)
     )
+    chunk_count = fresh_len // tp_count
+    partial = jnp.dot(activated, narrow_weight, preferred_element_type=jnp.float32).astype(
+        jnp.bfloat16
+    )
     fed_total = reduce_tp(
-        jnp.dot(activated, narrow_weight, preferred_element_type=jnp.float32).astype(jnp.bfloat16),
+        jnp.transpose(partial.reshape(chunk_count, tp_count, width), (1, 0, 2)).reshape(
+            fresh_len, width
+        ),
         tp_count,
     )
+    residual = lax.dynamic_index_in_dim(
+        normed_all.reshape(chunk_count, tp_count, width), tp_index, 1, keepdims=False
+    )
     updated = layer_norm(
-        normed.astype(jnp.float32) + fed_total + narrow_bias.astype(jnp.float32),
+        residual.astype(jnp.float32) + fed_total + narrow_bias.astype(jnp.float32),
         norm_gains[1],
         norm_biases[1],
     ).astype(jnp.bfloat16)
-    by_cols = lax.all_to_all(
-        updated.reshape(rows, tp_count, width // tp_count), "tp", 1, 0, tiled=True
-    ).reshape(fresh_len, width // tp_count)
-    returned = lax.all_to_all(by_cols[None], "req", split_axis=1, concat_axis=0, tiled=True)
+    returned = lax.all_to_all(
+        updated.reshape(chunk_count * tp_count, width // tp_count),
+        ("req", "tp"),
+        0,
+        0,
+        tiled=True,
+    ).reshape(-1, tp_count, width // tp_count)
     hidden_out = returned.at[request_slot].get(mode="promise_in_bounds", unique_indices=True)
     return (hidden_out, new_cache)
 

time: 160 us -> 157 us (0.981)
  blocking collectives: 37 us -> 28.4 us
  starting transfers between devices: 24.4 us -> 29.2 us
  matrix products: 13.7 us -> 9.18 us
  waiting for transfers between devices: 65.4 us -> 69.6 us
    all_to_all x1 -> x0, blocking collectives: 8.59 us -> none  [on_device(): lax.all_to_all(updated.reshape(rows, tp_count, width // tp_count), 'tp',...]
    all_to_all x1, waiting for transfers between devices: 10.7 us -> 16.7 us  [on_device(): lax.all_to_all(updated.reshape(chunk_count * tp_count, width // tp_count)...]
    all_to_all x1, starting transfers between devices: 4.62 us -> 9.29 us  [on_device(): lax.all_to_all(updated.reshape(chunk_count * tp_count, width // tp_count)...]
    dot_general x3 -> x0, matrix products: 4.01 us -> none  [on_device(): jnp.dot(token_rows, proj_weight[c], preferred_element_type=jnp.float32)]
    reshape x0 -> x2, local copies, waits for them, and re-layouts: none -> 1.75 us  [the longest x1 1.6 us: on_device(): partial.reshape(chunk_count, tp_count, width)]
    unnamed x0 -> x1, matrix products: none -> 1.73 us
    convert_element_type x1 -> x4, other arithmetic: 0.01 us -> 1.68 us  [the longest x1 1.44 us: on_device(): residual.astype(jnp.float32) + fed_total + narrow_bias.astype(jnp.float32)]
    unnamed x44 -> x37, local copies, waits for them, and re-layouts: 3.5 us -> 2.61 us
  transfers between devices with their start and end apart: 5 -> 5, of which waited for: 5 -> 5; matrix products, arithmetic and copies ran while one was open for 3% -> 4% of each run, Pallas kernels for 0% -> 0%
where the time goes in v3:
time: 157 us
  waiting for transfers between devices  69.6 us (44%)
  starting transfers between devices  29.2 us (19%)
  blocking collectives  28.4 us (18%)
  local copies, waits for them, and re-layouts  11.9 us (8%)
  matrix products  9.18 us (6%)
  other arithmetic  5.48 us (3%)
  between operations  2.98 us (2%)
    all_to_all x1, blocking collectives, on_device(): lax.all_to_all(hidden_in.at[owner_order].get(mode='promise_in_bounds', un...  28.4 us
    all_to_all x2, waiting for transfers between devices, reduce_tp(): lax.all_to_all(partial.reshape(tp_count, rows, -1), 'tp', 0, 0, tiled=True)  28.3 us
    all_to_all x2, waiting for transfers between devices, gather_tp(): got = lax.all_to_all(copies, 'tp', axis, axis, tiled=True)  24.6 us
    all_to_all x1, waiting for transfers between devices, on_device(): lax.all_to_all(updated.reshape(chunk_count * tp_count, width // tp_count)...  16.7 us
    all_to_all x2, starting transfers between devices, gather_tp(): got = lax.all_to_all(copies, 'tp', axis, axis, tiled=True)  11 us
    all_to_all x1, starting transfers between devices, on_device(): lax.all_to_all(updated.reshape(chunk_count * tp_count, width // tp_count)...  9.29 us
    all_to_all x2, starting transfers between devices, reduce_tp(): lax.all_to_all(partial.reshape(tp_count, rows, -1), 'tp', 0, 0, tiled=True)  8.84 us
  transfers between devices with their start and end apart: 5, of which 5 were waited for; matrix products, arithmetic and copies ran while one was open for 4% of the time, Pallas kernels for 0%

profile of v3, /device:TPU:1, one launch (start us, length us, event | category | flops | bytes accessed | tf_op | source)
XLA Modules:
  0.0 156.7 jit_solution(8526933420183440276)
XLA Ops:
  0.7 0.8 compare_select_fusion.1
  1.5 1.5 gather_fusion
  3.0 28.4 %all_to_all.35 = bf16[64,8,128]{2,1,0:T(8,128)(2,1)S(1)} all-to-all(bf16[64,8,128]{2,1,0:T(8,128)(2,1)S(1)} %gather_fusion), channel_id=1, replica_groups=mesh['req'=64,'tp'=8] {'req'}, dimensions={0} | all-to-all | bytes 262144 | tf_op jit(solution)/shard_map/all_to_all | solution.py:113
  31.4 1.1 broadcast_in_dim.75
  32.6 6.6 %all-to-all-start.1 = ((bf16[512,8,128]{2,0,1:T(8,128)(2,1)}), bf16[512,8,128]{2,0,1:T(8,128)(2,1)S(1)}, u32[]{:S(2)}, u32[]{:S(2)}) async-start(bf16[512,8,128]{2,0,1:T(8,128)(2,1)} %broadcast_in_dim.75), calls=%async_computation.1 | async-start | bytes 2097152 | tf_op jit(solution)/shard_map/all_to_all | solution.py:81
  39.2 0.6 dynamic_slice.18
  41.2 1.2 copy.57
  43.2 0.6 dynamic_slice.19
  43.8 0.6 iota_compare_fusion.1
  44.5 9.6 %all-to-all-done.1 = bf16[512,8,128]{2,0,1:T(8,128)(2,1)S(1)} async-done(((bf16[512,8,128]{2,0,1:T(8,128)(2,1)}), bf16[512,8,128]{2,0,1:T(8,128)(2,1)S(1)}, u32[]{:S(2)}, u32[]{:S(2)}) %all-to-all-start.1) | async-done | bytes 1048608 | tf_op jit(solution)/shard_map/all_to_all | solution.py:81
  54.1 1.7 %fusion.38 = f32[512,384]{0,1:S(1)} fusion(bf16[1024,384]{0,1:T(8,128)(2,1)} %bitcast.128, bf16[512,8,128]{2,0,1:T(8,128)(2,1)S(1)} %all-to-all-done.1), kind=kOutput, calls=%fused_computation.93 | convolution fusion | flops 402653184 | bytes 2621440
  56.6 0.6 select_reduce_fusion.1
  57.2 0.6 convolution_bitcast_fusion
  57.7 0.9 fusion
  58.6 0.7 fusion.8
  59.6 1.4 convolution_convert_fusion
  61.0 4.4 %all-to-all-start.2 = ((bf16[8,64,1024]{2,1,0:T(8,128)(2,1)}), bf16[8,64,1024]{2,1,0:T(8,128)(2,1)S(1)}, u32[]{:S(2)}, u32[]{:S(2)}) async-start(bf16[8,64,1024]{2,1,0:T(8,128)(2,1)} %bitcast.121), calls=%async_computation.2 | async-start | bytes 2097152 | tf_op jit(solution)/shard_map/all_to_all | solution.py:87
  65.7 14.8 %all-to-all-done.2 = bf16[8,64,1024]{2,1,0:T(8,128)(2,1)S(1)} async-done(((bf16[8,64,1024]{2,1,0:T(8,128)(2,1)}), bf16[8,64,1024]{2,1,0:T(8,128)(2,1)S(1)}, u32[]{:S(2)}, u32[]{:S(2)}) %all-to-all-start.2) | async-done | bytes 1048608 | tf_op jit(solution)/shard_map/all_to_all | solution.py:87
  81.1 1.1 broadcast_in_dim.79
  82.2 4.4 %all-to-all-start.3 = ((bf16[8,64,1024]{2,1,0:T(8,128)(2,1)}), bf16[8,64,1024]{2,1,0:T(8,128)(2,1)S(1)}, u32[]{:S(2)}, u32[]{:S(2)}) async-start(bf16[8,64,1024]{2,1,0:T(8,128)(2,1)} %broadcast_in_dim.79), calls=%async_computation.3 | async-start | bytes 2097152 | tf_op jit(solution)/shard_map/all_to_all | solution.py:81
  86.6 15.0 %all-to-all-done.3 = bf16[8,64,1024]{2,1,0:T(8,128)(2,1)S(1)} async-done(((bf16[8,64,1024]{2,1,0:T(8,128)(2,1)}), bf16[8,64,1024]{2,1,0:T(8,128)(2,1)S(1)}, u32[]{:S(2)}, u32[]{:S(2)}) %all-to-all-start.3) | async-done | bytes 1048608 | tf_op jit(solution)/shard_map/all_to_all | solution.py:81
  101.6 2.9 %fusion.11 = bf16[512,512]{1,0:T(8,128)(2,1)S(1)} fusion(bf16[512,1024]{1,0:T(8,128)(2,1)S(1)} %bitcast.123, bf16[1024,512]{1,0:T(8,128)(2,1)S(1)} %copy-done.12, f32[512]{0:T(512)S(1)} %convert_element_type.125), kind=kOutput, calls=%fused_computation.25 | convolution fusion | flops 554172416 | bytes 2623488 | tf_op jit(solution)/shard_map/dot_general | solution.py:149
  104.6 0.7 fusion.4
  105.4 1.6 %copy.79 = bf16[64,8,1024]{2,0,1:T(8,128)(2,1)} copy(bf16[64,8,1024]{2,1,0:T(8,128)(2,1)S(1)} %fusion.4) | data formatting | bytes 2097152 | tf_op jit(solution)/shard_map/reshape | solution.py:160
  107.0 4.4 %all-to-all-start.4 = ((bf16[8,64,1024]{2,1,0:T(8,128)(2,1)}), bf16[8,64,1024]{2,1,0:T(8,128)(2,1)S(1)}, u32[]{:S(2)}, u32[]{:S(2)}) async-start(bf16[8,64,1024]{2,1,0:T(8,128)(2,1)} %bitcast.119), calls=%async_computation.4 | async-start | bytes 2097152 | tf_op jit(solution)/shard_map/all_to_all | solution.py:87
  111.4 1.4 dynamic-slice_convert_fusion
  112.8 13.5 %all-to-all-done.4 = bf16[8,64,1024]{2,1,0:T(8,128)(2,1)S(1)} async-done(((bf16[8,64,1024]{2,1,0:T(8,128)(2,1)}), bf16[8,64,1024]{2,1,0:T(8,128)(2,1)S(1)}, u32[]{:S(2)}, u32[]{:S(2)}) %all-to-all-start.4) | async-done | bytes 1048608 | tf_op jit(solution)/shard_map/all_to_all | solution.py:87
  127.5 0.9 copy.63
  128.4 9.3 %all-to-all-start.5 = ((bf16[512,1,128]{2,1,0:T(2,128)(2,1)}), bf16[512,1,128]{2,1,0:T(2,128)(2,1)S(1)}, u32[]{:S(2)}, u32[]{:S(2)}) async-start(bf16[512,1,128]{2,1,0:T(2,128)(2,1)} %copy.63), calls=%async_computation.5 | async-start | bytes 524288 | tf_op jit(solution)/shard_map/all_to_all | solution.py:173
  137.8 0.8 copy.64
  138.7 16.7 %all-to-all-done.5 = bf16[512,1,128]{2,1,0:T(2,128)(2,1)S(1)} async-done(((bf16[512,1,128]{2,1,0:T(2,128)(2,1)}), bf16[512,1,128]{2,1,0:T(2,128)(2,1)S(1)}, u32[]{:S(2)}, u32[]{:S(2)}) %all-to-all-start.5) | async-done | bytes 131104 | tf_op jit(solution)/shard_map/all_to_all | solution.py:173
  155.4 1.3 gather_fusion.1
  (71 shorter events, 3.4 us)
Async XLA Ops:
  0.6 104.0 %copy-start = (bf16[512,1024]{1,0:T(8,128)(2,1)S(1)}, bf16[512,1024]{1,0:T(8,128)(2,1)}, u32[]{:S(2)}) copy-start(bf16[512,1024]{1,0:T(8,128)(2,1)} %param.30) | copy-start | bytes 3145732
  0.6 38.5 %copy-start.13 = (s32[64]{0:T(128)S(1)}, s32[64]{0:T(128)}, u32[]{:S(2)}) copy-start(s32[64]{0:T(128)} %param.20) | copy-start | bytes 772
  0.7 40.4 %copy-start.8 = (bf16[1024]{0:T(1024)(128)(2,1)S(1)}, bf16[1024]{0:T(1024)(128)(2,1)}, u32[]{:S(2)}) copy-start(bf16[1024]{0:T(1024)(128)(2,1)} %param.25) | copy-start | bytes 6148
  0.7 40.4 %copy-start.4 = (bf16[1,512,128]{2,1,0:T(8,128)(2,1)S(1)}, bf16[1,512,128]{2,1,0:T(8,128)(2,1)}, u32[]{:S(2)}) copy-start(bf16[1,512,128]{2,1,0:T(8,128)(2,1)} %param.18) | copy-start | bytes 393220
  0.7 40.5 %copy-start.2 = (bf16[3,1024,128]{2,1,0:T(8,128)(2,1)S(1)}, bf16[3,1024,128]{2,1,0:T(8,128)(2,1)}, u32[]{:S(2)}) copy-start(bf16[3,1024,128]{2,1,0:T(8,128)(2,1)} %param.22) | copy-start | bytes 2359300
  32.6 9.9 %copy-start.10 = (bf16[3,128]{1,0:T(4,128)(2,1)S(1)}, bf16[3,128]{1,0:T(4,128)(2,1)}, u32[]{:S(2)}) copy-start(bf16[3,128]{1,0:T(4,128)(2,1)} %param.23) | copy-start | bytes 2308
  32.6 9.9 %copy-start.5 = (bf16[1,512,128]{2,1,0:T(8,128)(2,1)S(1)}, bf16[1,512,128]{2,1,0:T(8,128)(2,1)}, u32[]{:S(2)}) copy-start(bf16[1,512,128]{2,1,0:T(8,128)(2,1)} %param.17) | copy-start | bytes 393220
  32.6 10.6 %copy-start.14 = (s32[64]{0:T(128)S(1)}, s32[64]{0:T(128)}, u32[]{:S(2)}) copy-start(s32[64]{0:T(128)} %param.19) | copy-start | bytes 772
  32.6 21.6 %all-to-all-start.1 = ((bf16[512,8,128]{2,0,1:T(8,128)(2,1)}), bf16[512,8,128]{2,0,1:T(8,128)(2,1)S(1)}, u32[]{:S(2)}, u32[]{:S(2)}) async-start(bf16[512,8,128]{2,0,1:T(8,128)(2,1)} %broadcast_in_dim.75), calls=%async_computation.1 | async-start | bytes 2097152 | tf_op jit(solution)/shard_map/all_to_all | solution.py:81
  58.6 1.0 copy-start.3
  59.3 6.1 %copy-start.6 = (bf16[2,1024]{1,0:T(2,128)(2,1)S(1)}, bf16[2,1024]{1,0:T(2,128)(2,1)}, u32[]{:S(2)}) copy-start(bf16[2,1024]{1,0:T(2,128)(2,1)} %param.27) | copy-start | bytes 12292
  59.3 6.1 %copy-start.7 = (bf16[2,1024]{1,0:T(2,128)(2,1)S(1)}, bf16[2,1024]{1,0:T(2,128)(2,1)}, u32[]{:S(2)}) copy-start(bf16[2,1024]{1,0:T(2,128)(2,1)} %param.26) | copy-start | bytes 12292
  61.0 19.4 %all-to-all-start.2 = ((bf16[8,64,1024]{2,1,0:T(8,128)(2,1)}), bf16[8,64,1024]{2,1,0:T(8,128)(2,1)S(1)}, u32[]{:S(2)}, u32[]{:S(2)}) async-start(bf16[8,64,1024]{2,1,0:T(8,128)(2,1)} %bitcast.121), calls=%async_computation.2 | async-start | bytes 2097152 | tf_op jit(solution)/shard_map/all_to_all | solution.py:87
  80.7 5.9 %copy-start.11 = (bf16[512]{0:T(512)(128)(2,1)S(1)}, bf16[512]{0:T(512)(128)(2,1)}, u32[]{:S(2)}) copy-start(bf16[512]{0:T(512)(128)(2,1)} %param.29) | copy-start | bytes 3076
  80.7 20.9 %copy-start.12 = (bf16[1024,512]{1,0:T(8,128)(2,1)S(1)}, bf16[1024,512]{1,0:T(8,128)(2,1)}, u32[]{:S(2)}) copy-start(bf16[1024,512]{1,0:T(8,128)(2,1)} %param.28) | copy-start | bytes 3145732
  82.2 19.4 %all-to-all-start.3 = ((bf16[8,64,1024]{2,1,0:T(8,128)(2,1)}), bf16[8,64,1024]{2,1,0:T(8,128)(2,1)S(1)}, u32[]{:S(2)}, u32[]{:S(2)}) async-start(bf16[8,64,1024]{2,1,0:T(8,128)(2,1)} %broadcast_in_dim.79), calls=%async_computation.3 | async-start | bytes 2097152 | tf_op jit(solution)/shard_map/all_to_all | solution.py:81
  101.6 3.0 %copy-start.1 = (bf16[8,64,1024]{2,1,0:T(8,128)(2,1)}, bf16[8,64,1024]{2,1,0:T(8,128)(2,1)S(1)}, u32[]{:S(2)}) copy-start(bf16[8,64,1024]{2,1,0:T(8,128)(2,1)S(1)} %all-to-all-done.3) | copy-start | bytes 3145732
  105.4 6.0 %copy-start.9 = (bf16[1024]{0:T(1024)(128)(2,1)S(1)}, bf16[1024]{0:T(1024)(128)(2,1)}, u32[]{:S(2)}) copy-start(bf16[1024]{0:T(1024)(128)(2,1)} %param.31) | copy-start | bytes 6148
  107.0 19.4 %all-to-all-start.4 = ((bf16[8,64,1024]{2,1,0:T(8,128)(2,1)}), bf16[8,64,1024]{2,1,0:T(8,128)(2,1)S(1)}, u32[]{:S(2)}, u32[]{:S(2)}) async-start(bf16[8,64,1024]{2,1,0:T(8,128)(2,1)} %bitcast.119), calls=%async_computation.4 | async-start | bytes 2097152 | tf_op jit(solution)/shard_map/all_to_all | solution.py:87
  112.8 24.9 %copy-start.15 = (s32[64]{0:T(128)S(1)}, s32[64]{0:T(128)}, u32[]{:S(2)}) copy-start(s32[64]{0:T(128)} %param.21) | copy-start | bytes 772
  128.4 26.9 %all-to-all-start.5 = ((bf16[512,1,128]{2,1,0:T(2,128)(2,1)}), bf16[512,1,128]{2,1,0:T(2,128)(2,1)S(1)}, u32[]{:S(2)}, u32[]{:S(2)}) async-start(bf16[512,1,128]{2,1,0:T(2,128)(2,1)} %copy.63), calls=%async_computation.5 | async-start | bytes 524288 | tf_op jit(solution)/shard_map/all_to_all | solution.py:173

commit v4 on v3

--- a/solution.py
+++ b/solution.py
@@ -30,12 +30,12 @@
     return jnp.transpose(factor, (1, 0, 2))
 
 
-def slot_attention(query_rows, key_rows, value_rows, slot_keys, slot_values, length):
+def slot_attention(query_rows, key_rows, value_rows, slot_keys, slot_values, length, position):
     fresh_len = query_rows.shape[0]
     block_len = min(512, slot_keys.shape[0])
     block_count = slot_keys.shape[0] // block_len
     query_heads = split_heads(query_rows)
-    self_mask = jnp.arange(fresh_len)[:, None] >= jnp.arange(fresh_len)[None, :]
+    self_mask = position[:, None] >= position[None, :]
     self_scores = block_scores(query_heads, key_rows, self_mask)
     row_top = jnp.max(self_scores, axis=2, keepdims=True)
     raised = jnp.exp(self_scores - row_top)
@@ -110,15 +110,17 @@
     tp_index = lax.axis_index("tp")
     slot_index = lax.axis_index("req")
     length = cache_lengths[owner_order[slot_index]]
+    routed_in = hidden_in.at[owner_order].get(mode="promise_in_bounds", unique_indices=True)
+    chunk_len = routed_in.shape[1]
     own_cols = lax.all_to_all(
-        hidden_in.at[owner_order].get(mode="promise_in_bounds", unique_indices=True),
-        "req",
-        split_axis=0,
-        concat_axis=1,
-        tiled=True,
-    )[0]
+        jnp.transpose(routed_in, (1, 0, 2)), "req", split_axis=1, concat_axis=1, tiled=True
+    )
+    chunk_count = own_cols.shape[1]
+    own_cols = own_cols.reshape(chunk_len * chunk_count, -1)
     fresh_len = own_cols.shape[0]
     width = own_cols.shape[1] * tp_count
+    row_ids = jnp.arange(fresh_len)
+    position = (row_ids % chunk_count) * chunk_len + row_ids // chunk_count
     token_rows = gather_tp(own_cols, tp_count, 1)
     projected = (
         jnp.einsum("td,cdf->ctf", token_rows, proj_weight, preferred_element_type=jnp.float32)
@@ -127,9 +129,10 @@
     query_rows = (projected[0] * HD ** (-0.5)).astype(jnp.bfloat16)
     key_rows = projected[1].astype(jnp.bfloat16)
     value_rows = projected[2].astype(jnp.bfloat16)
-    new_cache = jnp.stack([key_rows, value_rows], axis=0)[:, None]
+    new_cache = jnp.stack([key_rows, value_rows], axis=0).reshape(2, chunk_len, chunk_count, -1)
+    new_cache = jnp.transpose(new_cache, (0, 2, 1, 3)).reshape(2, 1, fresh_len, -1)
     context = slot_attention(
-        query_rows, key_rows, value_rows, cache_keys[0], cache_values[0], length
+        query_rows, key_rows, value_rows, cache_keys[0], cache_values[0], length, position
     )
     rows = fresh_len // tp_count
     own_rows = lax.optimization_barrier(
@@ -152,26 +155,17 @@
     activated = lax.optimization_barrier(
         jax.nn.gelu(widened, approximate=False).astype(jnp.bfloat16)
     )
-    chunk_count = fresh_len // tp_count
-    partial = jnp.dot(activated, narrow_weight, preferred_element_type=jnp.float32).astype(
-        jnp.bfloat16
-    )
     fed_total = reduce_tp(
-        jnp.transpose(partial.reshape(chunk_count, tp_count, width), (1, 0, 2)).reshape(
-            fresh_len, width
-        ),
+        jnp.dot(activated, narrow_weight, preferred_element_type=jnp.float32).astype(jnp.bfloat16),
         tp_count,
     )
-    residual = lax.dynamic_index_in_dim(
-        normed_all.reshape(chunk_count, tp_count, width), tp_index, 1, keepdims=False
-    )
     updated = layer_norm(
-        residual.astype(jnp.float32) + fed_total + narrow_bias.astype(jnp.float32),
+        normed.astype(jnp.float32) + fed_total + narrow_bias.astype(jnp.float32),
         norm_gains[1],
         norm_biases[1],
     ).astype(jnp.bfloat16)
     returned = lax.all_to_all(
-        updated.reshape(chunk_count * tp_count, width // tp_count),
+        updated.reshape(rows * tp_count, width // tp_count),
         ("req", "tp"),
         0,
         0,

time: 157 us -> 158 us (level)
  matrix products: 9.18 us -> 11.5 us
  local copies, waits for them, and re-layouts: 11.9 us -> 10 us
    reshape x1 -> x0, local copies, waits for them, and re-layouts: 1.6 us -> none  [on_device(): partial.reshape(chunk_count, tp_count, width)]
  transfers between devices with their start and end apart: 5 -> 5, of which waited for: 5 -> 5; matrix products, arithmetic and copies ran while one was open for 4% -> 3% of each run, Pallas kernels for 0% -> 0%
where the time goes in v4:
time: 158 us; the launch traced here: 157 us
  waiting for transfers between devices  70.6 us (45%)
  starting transfers between devices  29.2 us (18%)
  blocking collectives  28.6 us (18%)
  matrix products  11.5 us (7%)
  local copies, waits for them, and re-layouts  10 us (6%)
  other arithmetic  4.23 us (3%)
  between operations  2.96 us (2%)
    all_to_all x2, waiting for transfers between devices, reduce_tp(): lax.all_to_all(partial.reshape(tp_count, rows, -1), 'tp', 0, 0, tiled=True)  29.8 us
    all_to_all x1, blocking collectives, on_device(): lax.all_to_all(jnp.transpose(routed_in, (1, 0, 2)), 'req', split_axis=1,...  28.6 us
    all_to_all x2, waiting for transfers between devices, gather_tp(): got = lax.all_to_all(copies, 'tp', axis, axis, tiled=True)  24.4 us
    all_to_all x1, waiting for transfers between devices, on_device(): lax.all_to_all(updated.reshape(rows * tp_count, width // tp_count), ('req...  16.4 us
    all_to_all x2, starting transfers between devices, gather_tp(): got = lax.all_to_all(copies, 'tp', axis, axis, tiled=True)  11 us
    all_to_all x1, starting transfers between devices, on_device(): lax.all_to_all(updated.reshape(rows * tp_count, width // tp_count), ('req...  9.36 us
    all_to_all x2, starting transfers between devices, reduce_tp(): lax.all_to_all(partial.reshape(tp_count, rows, -1), 'tp', 0, 0, tiled=True)  8.84 us
    dot_general x1, matrix products, on_device(): jnp.dot(normed_all, widen_weight, preferred_element_type=jnp.float32)  4.28 us
  transfers between devices with their start and end apart: 5, of which 5 were waited for; matrix products, arithmetic and copies ran while one was open for 3% of the time, Pallas kernels for 0%

profile of v4, /device:TPU:1, one launch (start us, length us, event | category | flops | bytes accessed | tf_op | source)
XLA Modules:
  0.0 157.0 jit_solution(2075853976028216427)
XLA Ops:
  0.7 0.7 compare_select_fusion.1
  1.4 1.5 gather_fusion
  3.0 28.6 %all_to_all.35 = bf16[8,64,128]{2,0,1:T(8,128)(2,1)S(1)} all-to-all(bf16[8,64,128]{2,0,1:T(8,128)(2,1)S(1)} %bitcast.107), channel_id=1, replica_groups=mesh['req'=64,'tp'=8] {'req'}, dimensions={1} | all-to-all | bytes 262144 | tf_op jit(solution)/shard_map/all_to_all | solution.py:115
  31.6 1.1 broadcast_in_dim.72
  32.7 6.6 %all-to-all-start.1 = ((bf16[512,8,128]{2,0,1:T(8,128)(2,1)}), bf16[512,8,128]{2,0,1:T(8,128)(2,1)S(1)}, u32[]{:S(2)}, u32[]{:S(2)}) async-start(bf16[512,8,128]{2,0,1:T(8,128)(2,1)} %broadcast_in_dim.72), calls=%async_computation.1 | async-start | bytes 2097152 | tf_op jit(solution)/shard_map/all_to_all | solution.py:81
  39.3 0.6 dynamic_slice.14
  41.3 1.2 copy.55
  43.3 0.6 dynamic_slice.15
  43.9 0.6 iota_compare_fusion
  44.8 9.4 %all-to-all-done.1 = bf16[512,8,128]{2,0,1:T(8,128)(2,1)S(1)} async-done(((bf16[512,8,128]{2,0,1:T(8,128)(2,1)}), bf16[512,8,128]{2,0,1:T(8,128)(2,1)S(1)}, u32[]{:S(2)}, u32[]{:S(2)}) %all-to-all-start.1) | async-done | bytes 1048608 | tf_op jit(solution)/shard_map/all_to_all | solution.py:81
  54.2 1.7 %fusion.42 = f32[512,384]{0,1:S(1)} fusion(bf16[1024,384]{0,1:T(8,128)(2,1)} %bitcast.102, bf16[512,8,128]{2,0,1:T(8,128)(2,1)S(1)} %all-to-all-done.1), kind=kOutput, calls=%fused_computation.97 | convolution fusion | flops 402653184 | bytes 2621440
  56.2 0.5 select_reduce_fusion
  56.7 0.6 select_reduce_fusion.1
  57.3 0.6 convolution_bitcast_fusion
  57.8 0.9 fusion
  58.7 0.7 fusion.7
  59.7 1.4 convolution_convert_fusion
  61.1 4.4 %all-to-all-start.2 = ((bf16[8,64,1024]{2,1,0:T(8,128)(2,1)}), bf16[8,64,1024]{2,1,0:T(8,128)(2,1)S(1)}, u32[]{:S(2)}, u32[]{:S(2)}) async-start(bf16[8,64,1024]{2,1,0:T(8,128)(2,1)} %bitcast.97), calls=%async_computation.2 | async-start | bytes 2097152 | tf_op jit(solution)/shard_map/all_to_all | solution.py:87
  65.7 14.8 %all-to-all-done.2 = bf16[8,64,1024]{2,1,0:T(8,128)(2,1)S(1)} async-done(((bf16[8,64,1024]{2,1,0:T(8,128)(2,1)}), bf16[8,64,1024]{2,1,0:T(8,128)(2,1)S(1)}, u32[]{:S(2)}, u32[]{:S(2)}) %all-to-all-start.2) | async-done | bytes 1048608 | tf_op jit(solution)/shard_map/all_to_all | solution.py:87
  81.2 1.1 broadcast_in_dim.76
  82.3 4.4 %all-to-all-start.3 = ((bf16[8,64,1024]{2,1,0:T(8,128)(2,1)}), bf16[8,64,1024]{2,1,0:T(8,128)(2,1)S(1)}, u32[]{:S(2)}, u32[]{:S(2)}) async-start(bf16[8,64,1024]{2,1,0:T(8,128)(2,1)} %broadcast_in_dim.76), calls=%async_computation.3 | async-start | bytes 2097152 | tf_op jit(solution)/shard_map/all_to_all | solution.py:81
  86.7 15.0 %all-to-all-done.3 = bf16[8,64,1024]{2,1,0:T(8,128)(2,1)S(1)} async-done(((bf16[8,64,1024]{2,1,0:T(8,128)(2,1)}), bf16[8,64,1024]{2,1,0:T(8,128)(2,1)S(1)}, u32[]{:S(2)}, u32[]{:S(2)}) %all-to-all-start.3) | async-done | bytes 1048608 | tf_op jit(solution)/shard_map/all_to_all | solution.py:81
  101.7 4.3 %fusion.10 = bf16[512,512]{1,0:T(8,128)(2,1)S(1)} fusion(bf16[512,1024]{1,0:T(8,128)(2,1)S(1)} %bitcast.101, bf16[1024,512]{1,0:T(8,128)(2,1)} %param.28, f32[512]{0:T(512)S(1)} %convert_element_type.100), kind=kOutput, calls=%fused_computation.24 | convolution fusion | flops 554172416 | bytes 2623488 | tf_op jit(solution)/shard_map/dot_general | solution.py:152
  106.0 1.7 %convolution_convert_fusion.1 = bf16[512,1024]{1,0:T(8,128)(2,1)} fusion(bf16[512,512]{1,0:T(8,128)(2,1)S(1)} %fusion.10, bf16[512,1024]{1,0:T(8,128)(2,1)S(1)} %copy-done), kind=kOutput, calls=%fused_computation.14 | convolution fusion | flops 537395200 | bytes 2621440 | tf_op jit(solution)/shard_map/dot_general | solution.py:159
  107.7 4.4 %all-to-all-start.4 = ((bf16[8,64,1024]{2,1,0:T(8,128)(2,1)}), bf16[8,64,1024]{2,1,0:T(8,128)(2,1)S(1)}, u32[]{:S(2)}, u32[]{:S(2)}) async-start(bf16[8,64,1024]{2,1,0:T(8,128)(2,1)} %bitcast.28), calls=%async_computation.4 | async-start | bytes 2097152 | tf_op jit(solution)/shard_map/all_to_all | solution.py:87
  112.1 15.0 %all-to-all-done.4 = bf16[8,64,1024]{2,1,0:T(8,128)(2,1)S(1)} async-done(((bf16[8,64,1024]{2,1,0:T(8,128)(2,1)}), bf16[8,64,1024]{2,1,0:T(8,128)(2,1)S(1)}, u32[]{:S(2)}, u32[]{:S(2)}) %all-to-all-start.4) | async-done | bytes 1048608 | tf_op jit(solution)/shard_map/all_to_all | solution.py:87
  127.5 0.3 multiply_reduce_fusion
  128.0 0.8 all_to_all.28
  128.8 9.4 %all-to-all-start.5 = ((bf16[512,1,128]{2,1,0:T(2,128)(2,1)}), bf16[512,1,128]{2,1,0:T(2,128)(2,1)S(1)}, u32[]{:S(2)}, u32[]{:S(2)}) async-start(bf16[512,1,128]{2,1,0:T(2,128)(2,1)} %all_to_all.28), calls=%async_computation.5 | async-start | bytes 524288 | tf_op jit(solution)/shard_map/all_to_all | solution.py:167
  138.5 0.9 copy.73
  139.3 16.4 %all-to-all-done.5 = bf16[512,1,128]{2,1,0:T(2,128)(2,1)S(1)} async-done(((bf16[512,1,128]{2,1,0:T(2,128)(2,1)}), bf16[512,1,128]{2,1,0:T(2,128)(2,1)S(1)}, u32[]{:S(2)}, u32[]{:S(2)}) %all-to-all-start.5) | async-done | bytes 131104 | tf_op jit(solution)/shard_map/all_to_all | solution.py:167
  155.8 1.3 gather_fusion.1
  (64 shorter events, 2.7 us)
Async XLA Ops:
  0.6 105.4 %copy-start = (bf16[512,1024]{1,0:T(8,128)(2,1)S(1)}, bf16[512,1024]{1,0:T(8,128)(2,1)}, u32[]{:S(2)}) copy-start(bf16[512,1024]{1,0:T(8,128)(2,1)} %param.30) | copy-start | bytes 3145732
  0.6 38.6 %copy-start.11 = (s32[64]{0:T(128)S(1)}, s32[64]{0:T(128)}, u32[]{:S(2)}) copy-start(s32[64]{0:T(128)} %param.20) | copy-start | bytes 772
  0.7 40.5 %copy-start.7 = (bf16[1024]{0:T(1024)(128)(2,1)S(1)}, bf16[1024]{0:T(1024)(128)(2,1)}, u32[]{:S(2)}) copy-start(bf16[1024]{0:T(1024)(128)(2,1)} %param.25) | copy-start | bytes 6148
  0.7 40.5 %copy-start.3 = (bf16[1,512,128]{2,1,0:T(8,128)(2,1)S(1)}, bf16[1,512,128]{2,1,0:T(8,128)(2,1)}, u32[]{:S(2)}) copy-start(bf16[1,512,128]{2,1,0:T(8,128)(2,1)} %param.18) | copy-start | bytes 393220
  3.0 38.3 %copy-start.1 = (bf16[3,1024,128]{2,1,0:T(8,128)(2,1)S(1)}, bf16[3,1024,128]{2,1,0:T(8,128)(2,1)}, u32[]{:S(2)}) copy-start(bf16[3,1024,128]{2,1,0:T(8,128)(2,1)} %param.22) | copy-start | bytes 2359300
  32.7 9.9 %copy-start.9 = (bf16[3,128]{1,0:T(4,128)(2,1)S(1)}, bf16[3,128]{1,0:T(4,128)(2,1)}, u32[]{:S(2)}) copy-start(bf16[3,128]{1,0:T(4,128)(2,1)} %param.23) | copy-start | bytes 2308
  32.7 9.9 %copy-start.4 = (bf16[1,512,128]{2,1,0:T(8,128)(2,1)S(1)}, bf16[1,512,128]{2,1,0:T(8,128)(2,1)}, u32[]{:S(2)}) copy-start(bf16[1,512,128]{2,1,0:T(8,128)(2,1)} %param.17) | copy-start | bytes 393220
  32.7 10.6 %copy-start.12 = (s32[64]{0:T(128)S(1)}, s32[64]{0:T(128)}, u32[]{:S(2)}) copy-start(s32[64]{0:T(128)} %param.19) | copy-start | bytes 772
  32.7 21.6 %all-to-all-start.1 = ((bf16[512,8,128]{2,0,1:T(8,128)(2,1)}), bf16[512,8,128]{2,0,1:T(8,128)(2,1)S(1)}, u32[]{:S(2)}, u32[]{:S(2)}) async-start(bf16[512,8,128]{2,0,1:T(8,128)(2,1)} %broadcast_in_dim.72), calls=%async_computation.1 | async-start | bytes 2097152 | tf_op jit(solution)/shard_map/all_to_all | solution.py:81
  58.7 1.0 copy-start.2
  59.4 6.1 %copy-start.5 = (bf16[2,1024]{1,0:T(2,128)(2,1)S(1)}, bf16[2,1024]{1,0:T(2,128)(2,1)}, u32[]{:S(2)}) copy-start(bf16[2,1024]{1,0:T(2,128)(2,1)} %param.27) | copy-start | bytes 12292
  59.4 6.1 %copy-start.6 = (bf16[2,1024]{1,0:T(2,128)(2,1)S(1)}, bf16[2,1024]{1,0:T(2,128)(2,1)}, u32[]{:S(2)}) copy-start(bf16[2,1024]{1,0:T(2,128)(2,1)} %param.26) | copy-start | bytes 12292
  61.1 19.4 %all-to-all-start.2 = ((bf16[8,64,1024]{2,1,0:T(8,128)(2,1)}), bf16[8,64,1024]{2,1,0:T(8,128)(2,1)S(1)}, u32[]{:S(2)}, u32[]{:S(2)}) async-start(bf16[8,64,1024]{2,1,0:T(8,128)(2,1)} %bitcast.97), calls=%async_computation.2 | async-start | bytes 2097152 | tf_op jit(solution)/shard_map/all_to_all | solution.py:87
  80.8 5.9 %copy-start.10 = (bf16[512]{0:T(512)(128)(2,1)S(1)}, bf16[512]{0:T(512)(128)(2,1)}, u32[]{:S(2)}) copy-start(bf16[512]{0:T(512)(128)(2,1)} %param.29) | copy-start | bytes 3076
  82.3 19.4 %all-to-all-start.3 = ((bf16[8,64,1024]{2,1,0:T(8,128)(2,1)}), bf16[8,64,1024]{2,1,0:T(8,128)(2,1)S(1)}, u32[]{:S(2)}, u32[]{:S(2)}) async-start(bf16[8,64,1024]{2,1,0:T(8,128)(2,1)} %broadcast_in_dim.76), calls=%async_computation.3 | async-start | bytes 2097152 | tf_op jit(solution)/shard_map/all_to_all | solution.py:81
  106.0 6.1 %copy-start.8 = (bf16[1024]{0:T(1024)(128)(2,1)S(1)}, bf16[1024]{0:T(1024)(128)(2,1)}, u32[]{:S(2)}) copy-start(bf16[1024]{0:T(1024)(128)(2,1)} %param.31) | copy-start | bytes 6148
  107.7 19.4 %all-to-all-start.4 = ((bf16[8,64,1024]{2,1,0:T(8,128)(2,1)}), bf16[8,64,1024]{2,1,0:T(8,128)(2,1)S(1)}, u32[]{:S(2)}, u32[]{:S(2)}) async-start(bf16[8,64,1024]{2,1,0:T(8,128)(2,1)} %bitcast.28), calls=%async_computation.4 | async-start | bytes 2097152 | tf_op jit(solution)/shard_map/all_to_all | solution.py:87
  112.1 26.0 %copy-start.13 = (s32[64]{0:T(128)S(1)}, s32[64]{0:T(128)}, u32[]{:S(2)}) copy-start(s32[64]{0:T(128)} %param.21) | copy-start | bytes 772
  128.8 27.0 %all-to-all-start.5 = ((bf16[512,1,128]{2,1,0:T(2,128)(2,1)}), bf16[512,1,128]{2,1,0:T(2,128)(2,1)S(1)}, u32[]{:S(2)}, u32[]{:S(2)}) async-start(bf16[512,1,128]{2,1,0:T(2,128)(2,1)} %all_to_all.28), calls=%async_computation.5 | async-start | bytes 524288 | tf_op jit(solution)/shard_map/all_to_all | solution.py:167

commit v5 on v4

--- a/solution.py
+++ b/solution.py
@@ -86,6 +86,13 @@
     rows = partial.shape[0] // tp_count
     got = lax.all_to_all(partial.reshape(tp_count, rows, -1), "tp", 0, 0, tiled=True)
     return jnp.sum(got.astype(jnp.float32), axis=0)
+
+
+def permute_rows(order, table):
+    picks = (order[:, None] == jnp.arange(table.shape[0])[None, :]).astype(table.dtype)
+    flat = table.reshape(table.shape[0], -1)
+    moved = jnp.dot(picks, flat, preferred_element_type=jnp.float32).astype(table.dtype)
+    return moved.reshape(table.shape)
 
 
 def on_device(
@@ -110,7 +117,7 @@
     tp_index = lax.axis_index("tp")
     slot_index = lax.axis_index("req")
     length = cache_lengths[owner_order[slot_index]]
-    routed_in = hidden_in.at[owner_order].get(mode="promise_in_bounds", unique_indices=True)
+    routed_in = permute_rows(owner_order, hidden_in)
     chunk_len = routed_in.shape[1]
     own_cols = lax.all_to_all(
         jnp.transpose(routed_in, (1, 0, 2)), "req", split_axis=1, concat_axis=1, tiled=True
@@ -171,7 +178,7 @@
         0,
         tiled=True,
     ).reshape(-1, tp_count, width // tp_count)
-    hidden_out = returned.at[request_slot].get(mode="promise_in_bounds", unique_indices=True)
+    hidden_out = permute_rows(request_slot, returned)
     return (hidden_out, new_cache)
 
 

time: 158 us -> 157 us (level)
  local copies, waits for them, and re-layouts: 10 us -> 8.03 us
    gather x2 -> x0, local copies, waits for them, and re-layouts: 2.81 us -> none  [the longest x1 1.54 us: on_device(): hidden_in.at[owner_order].get(mode='promise_in_bounds', unique_indices=True)]
where the time goes in v5:
time: 157 us
  waiting for transfers between devices  70.6 us (45%)
  starting transfers between devices  29.2 us (19%)
  blocking collectives  28.6 us (18%)
  matrix products  12.9 us (8%)
  local copies, waits for them, and re-layouts  8.03 us (5%)
  other arithmetic  4.21 us (3%)
  between operations  2.98 us (2%)
    all_to_all x2, waiting for transfers between devices, reduce_tp(): lax.all_to_all(partial.reshape(tp_count, rows, -1), 'tp', 0, 0, tiled=True)  29.8 us
    all_to_all x1, blocking collectives, on_device(): lax.all_to_all(jnp.transpose(routed_in, (1, 0, 2)), 'req', split_axis=1,...  28.6 us
    all_to_all x2, waiting for transfers between devices, gather_tp(): got = lax.all_to_all(copies, 'tp', axis, axis, tiled=True)  24.4 us
    all_to_all x1, waiting for transfers between devices, on_device(): lax.all_to_all(updated.reshape(rows * tp_count, width // tp_count), ('req...  16.4 us
    all_to_all x2, starting transfers between devices, gather_tp(): got = lax.all_to_all(copies, 'tp', axis, axis, tiled=True)  11 us
    all_to_all x1, starting transfers between devices, on_device(): lax.all_to_all(updated.reshape(rows * tp_count, width // tp_count), ('req...  9.38 us
    all_to_all x2, starting transfers between devices, reduce_tp(): lax.all_to_all(partial.reshape(tp_count, rows, -1), 'tp', 0, 0, tiled=True)  8.85 us
    dot_general x1, matrix products, on_device(): jnp.dot(normed_all, widen_weight, preferred_element_type=jnp.float32)  4.28 us
  transfers between devices with their start and end apart: 5, of which 5 were waited for; matrix products, arithmetic and copies ran while one was open for 3% of the time, Pallas kernels for 0%

profile of v5, /device:TPU:1, one launch (start us, length us, event | category | flops | bytes accessed | tf_op | source)
XLA Modules:
  0.0 156.5 jit_solution(17630371864476680332)
XLA Ops:
  0.6 1.2 fusion.8
  2.0 28.6 %all_to_all.35 = bf16[8,64,128]{2,0,1:T(8,128)(2,1)S(1)} all-to-all(bf16[8,64,128]{2,0,1:T(8,128)(2,1)S(1)} %bitcast.115), channel_id=1, replica_groups=mesh['req'=64,'tp'=8] {'req'}, dimensions={1} | all-to-all | bytes 262144 | tf_op jit(solution)/shard_map/all_to_all | solution.py:122
  30.5 1.1 broadcast_in_dim.41
  31.7 6.6 %all-to-all-start.1 = ((bf16[512,8,128]{2,0,1:T(8,128)(2,1)}), bf16[512,8,128]{2,0,1:T(8,128)(2,1)S(1)}, u32[]{:S(2)}, u32[]{:S(2)}) async-start(bf16[512,8,128]{2,0,1:T(8,128)(2,1)} %broadcast_in_dim.41), calls=%async_computation.1 | async-start | bytes 2097152 | tf_op jit(solution)/shard_map/all_to_all | solution.py:81
  38.3 0.6 dynamic_slice.14
  40.3 1.2 copy.56
  42.3 0.6 dynamic_slice.15
  42.9 0.6 iota_compare_fusion.4
  43.8 9.4 %all-to-all-done.1 = bf16[512,8,128]{2,0,1:T(8,128)(2,1)S(1)} async-done(((bf16[512,8,128]{2,0,1:T(8,128)(2,1)}), bf16[512,8,128]{2,0,1:T(8,128)(2,1)S(1)}, u32[]{:S(2)}, u32[]{:S(2)}) %all-to-all-start.1) | async-done | bytes 1048608 | tf_op jit(solution)/shard_map/all_to_all | solution.py:81
  53.2 1.7 %fusion.48 = f32[512,384]{0,1:S(1)} fusion(bf16[1024,384]{0,1:T(8,128)(2,1)} %bitcast.111, bf16[512,8,128]{2,0,1:T(8,128)(2,1)S(1)} %all-to-all-done.1), kind=kOutput, calls=%fused_computation.100 | convolution fusion | flops 402653184 | bytes 2621440
  55.2 0.5 select_reduce_fusion
  55.7 0.6 select_reduce_fusion.1
  56.3 0.6 convolution_bitcast_fusion
  56.8 0.9 fusion
  57.7 0.7 fusion.7
  58.6 1.4 convolution_convert_fusion
  60.1 4.4 %all-to-all-start.2 = ((bf16[8,64,1024]{2,1,0:T(8,128)(2,1)}), bf16[8,64,1024]{2,1,0:T(8,128)(2,1)S(1)}, u32[]{:S(2)}, u32[]{:S(2)}) async-start(bf16[8,64,1024]{2,1,0:T(8,128)(2,1)} %bitcast.106), calls=%async_computation.2 | async-start | bytes 2097152 | tf_op jit(solution)/shard_map/all_to_all | solution.py:87
  64.8 14.8 %all-to-all-done.2 = bf16[8,64,1024]{2,1,0:T(8,128)(2,1)S(1)} async-done(((bf16[8,64,1024]{2,1,0:T(8,128)(2,1)}), bf16[8,64,1024]{2,1,0:T(8,128)(2,1)S(1)}, u32[]{:S(2)}, u32[]{:S(2)}) %all-to-all-start.2) | async-done | bytes 1048608 | tf_op jit(solution)/shard_map/all_to_all | solution.py:87
  80.2 1.1 broadcast_in_dim.45
  81.3 4.4 %all-to-all-start.3 = ((bf16[8,64,1024]{2,1,0:T(8,128)(2,1)}), bf16[8,64,1024]{2,1,0:T(8,128)(2,1)S(1)}, u32[]{:S(2)}, u32[]{:S(2)}) async-start(bf16[8,64,1024]{2,1,0:T(8,128)(2,1)} %broadcast_in_dim.45), calls=%async_computation.3 | async-start | bytes 2097152 | tf_op jit(solution)/shard_map/all_to_all | solution.py:81
  85.7 15.0 %all-to-all-done.3 = bf16[8,64,1024]{2,1,0:T(8,128)(2,1)S(1)} async-done(((bf16[8,64,1024]{2,1,0:T(8,128)(2,1)}), bf16[8,64,1024]{2,1,0:T(8,128)(2,1)S(1)}, u32[]{:S(2)}, u32[]{:S(2)}) %all-to-all-start.3) | async-done | bytes 1048608 | tf_op jit(solution)/shard_map/all_to_all | solution.py:81
  100.7 4.3 %fusion.12 = bf16[512,512]{1,0:T(8,128)(2,1)S(1)} fusion(bf16[512,1024]{1,0:T(8,128)(2,1)S(1)} %bitcast.110, bf16[1024,512]{1,0:T(8,128)(2,1)} %param.28, f32[512]{0:T(512)S(1)} %convert_element_type.109), kind=kOutput, calls=%fused_computation.26 | convolution fusion | flops 554172416 | bytes 2623488 | tf_op jit(solution)/shard_map/dot_general | solution.py:159
  105.0 1.7 %convolution_convert_fusion.1 = bf16[512,1024]{1,0:T(8,128)(2,1)} fusion(bf16[512,512]{1,0:T(8,128)(2,1)S(1)} %fusion.12, bf16[512,1024]{1,0:T(8,128)(2,1)S(1)} %copy-done), kind=kOutput, calls=%fused_computation.12 | convolution fusion | flops 537395200 | bytes 2621440 | tf_op jit(solution)/shard_map/dot_general | solution.py:166
  106.8 4.4 %all-to-all-start.4 = ((bf16[8,64,1024]{2,1,0:T(8,128)(2,1)}), bf16[8,64,1024]{2,1,0:T(8,128)(2,1)S(1)}, u32[]{:S(2)}, u32[]{:S(2)}) async-start(bf16[8,64,1024]{2,1,0:T(8,128)(2,1)} %bitcast.28), calls=%async_computation.4 | async-start | bytes 2097152 | tf_op jit(solution)/shard_map/all_to_all | solution.py:87
  111.2 15.0 %all-to-all-done.4 = bf16[8,64,1024]{2,1,0:T(8,128)(2,1)S(1)} async-done(((bf16[8,64,1024]{2,1,0:T(8,128)(2,1)}), bf16[8,64,1024]{2,1,0:T(8,128)(2,1)S(1)}, u32[]{:S(2)}, u32[]{:S(2)}) %all-to-all-start.4) | async-done | bytes 1048608 | tf_op jit(solution)/shard_map/all_to_all | solution.py:87
  126.6 0.2 multiply_reduce_fusion
  127.0 0.8 all_to_all.28
  127.8 9.4 %all-to-all-start.5 = ((bf16[512,1,128]{2,1,0:T(2,128)(2,1)}), bf16[512,1,128]{2,1,0:T(2,128)(2,1)S(1)}, u32[]{:S(2)}, u32[]{:S(2)}) async-start(bf16[512,1,128]{2,1,0:T(2,128)(2,1)} %all_to_all.28), calls=%async_computation.5 | async-start | bytes 524288 | tf_op jit(solution)/shard_map/all_to_all | solution.py:174
  137.5 0.9 copy.79
  138.4 16.4 %all-to-all-done.5 = bf16[512,1,128]{2,1,0:T(2,128)(2,1)S(1)} async-done(((bf16[512,1,128]{2,1,0:T(2,128)(2,1)}), bf16[512,1,128]{2,1,0:T(2,128)(2,1)S(1)}, u32[]{:S(2)}, u32[]{:S(2)}) %all-to-all-start.5) | async-done | bytes 131104 | tf_op jit(solution)/shard_map/all_to_all | solution.py:174
  154.8 0.8 reduce
  155.8 0.7 copy.71
  (63 shorter events, 3.0 us)
Async XLA Ops:
  0.6 104.4 %copy-start = (bf16[512,1024]{1,0:T(8,128)(2,1)S(1)}, bf16[512,1024]{1,0:T(8,128)(2,1)}, u32[]{:S(2)}) copy-start(bf16[512,1024]{1,0:T(8,128)(2,1)} %param.30) | copy-start | bytes 3145732
  1.9 36.4 %copy-start.11 = (s32[64]{0:T(128)S(1)}, s32[64]{0:T(128)}, u32[]{:S(2)}) copy-start(s32[64]{0:T(128)} %param.20) | copy-start | bytes 772
  1.9 38.3 %copy-start.7 = (bf16[1024]{0:T(1024)(128)(2,1)S(1)}, bf16[1024]{0:T(1024)(128)(2,1)}, u32[]{:S(2)}) copy-start(bf16[1024]{0:T(1024)(128)(2,1)} %param.25) | copy-start | bytes 6148
  1.9 38.3 %copy-start.3 = (bf16[1,512,128]{2,1,0:T(8,128)(2,1)S(1)}, bf16[1,512,128]{2,1,0:T(8,128)(2,1)}, u32[]{:S(2)}) copy-start(bf16[1,512,128]{2,1,0:T(8,128)(2,1)} %param.18) | copy-start | bytes 393220
  1.9 38.4 %copy-start.1 = (bf16[3,1024,128]{2,1,0:T(8,128)(2,1)S(1)}, bf16[3,1024,128]{2,1,0:T(8,128)(2,1)}, u32[]{:S(2)}) copy-start(bf16[3,1024,128]{2,1,0:T(8,128)(2,1)} %param.22) | copy-start | bytes 2359300
  31.7 9.9 %copy-start.9 = (bf16[3,128]{1,0:T(4,128)(2,1)S(1)}, bf16[3,128]{1,0:T(4,128)(2,1)}, u32[]{:S(2)}) copy-start(bf16[3,128]{1,0:T(4,128)(2,1)} %param.23) | copy-start | bytes 2308
  31.7 9.9 %copy-start.4 = (bf16[1,512,128]{2,1,0:T(8,128)(2,1)S(1)}, bf16[1,512,128]{2,1,0:T(8,128)(2,1)}, u32[]{:S(2)}) copy-start(bf16[1,512,128]{2,1,0:T(8,128)(2,1)} %param.17) | copy-start | bytes 393220
  31.7 10.6 %copy-start.13 = (s32[64]{0:T(128)S(1)}, s32[64]{0:T(128)}, u32[]{:S(2)}) copy-start(s32[64]{0:T(128)} %param.19) | copy-start | bytes 772
  31.7 21.6 %all-to-all-start.1 = ((bf16[512,8,128]{2,0,1:T(8,128)(2,1)}), bf16[512,8,128]{2,0,1:T(8,128)(2,1)S(1)}, u32[]{:S(2)}, u32[]{:S(2)}) async-start(bf16[512,8,128]{2,0,1:T(8,128)(2,1)} %broadcast_in_dim.41), calls=%async_computation.1 | async-start | bytes 2097152 | tf_op jit(solution)/shard_map/all_to_all | solution.py:81
  57.7 1.0 copy-start.2
  58.4 6.1 %copy-start.5 = (bf16[2,1024]{1,0:T(2,128)(2,1)S(1)}, bf16[2,1024]{1,0:T(2,128)(2,1)}, u32[]{:S(2)}) copy-start(bf16[2,1024]{1,0:T(2,128)(2,1)} %param.27) | copy-start | bytes 12292
  58.4 6.1 %copy-start.6 = (bf16[2,1024]{1,0:T(2,128)(2,1)S(1)}, bf16[2,1024]{1,0:T(2,128)(2,1)}, u32[]{:S(2)}) copy-start(bf16[2,1024]{1,0:T(2,128)(2,1)} %param.26) | copy-start | bytes 12292
  60.1 19.4 %all-to-all-start.2 = ((bf16[8,64,1024]{2,1,0:T(8,128)(2,1)}), bf16[8,64,1024]{2,1,0:T(8,128)(2,1)S(1)}, u32[]{:S(2)}, u32[]{:S(2)}) async-start(bf16[8,64,1024]{2,1,0:T(8,128)(2,1)} %bitcast.106), calls=%async_computation.2 | async-start | bytes 2097152 | tf_op jit(solution)/shard_map/all_to_all | solution.py:87
  79.8 5.9 %copy-start.10 = (bf16[512]{0:T(512)(128)(2,1)S(1)}, bf16[512]{0:T(512)(128)(2,1)}, u32[]{:S(2)}) copy-start(bf16[512]{0:T(512)(128)(2,1)} %param.29) | copy-start | bytes 3076
  81.3 19.4 %all-to-all-start.3 = ((bf16[8,64,1024]{2,1,0:T(8,128)(2,1)}), bf16[8,64,1024]{2,1,0:T(8,128)(2,1)S(1)}, u32[]{:S(2)}, u32[]{:S(2)}) async-start(bf16[8,64,1024]{2,1,0:T(8,128)(2,1)} %broadcast_in_dim.45), calls=%async_computation.3 | async-start | bytes 2097152 | tf_op jit(solution)/shard_map/all_to_all | solution.py:81
  105.0 6.1 %copy-start.8 = (bf16[1024]{0:T(1024)(128)(2,1)S(1)}, bf16[1024]{0:T(1024)(128)(2,1)}, u32[]{:S(2)}) copy-start(bf16[1024]{0:T(1024)(128)(2,1)} %param.31) | copy-start | bytes 6148
  106.8 19.4 %all-to-all-start.4 = ((bf16[8,64,1024]{2,1,0:T(8,128)(2,1)}), bf16[8,64,1024]{2,1,0:T(8,128)(2,1)S(1)}, u32[]{:S(2)}, u32[]{:S(2)}) async-start(bf16[8,64,1024]{2,1,0:T(8,128)(2,1)} %bitcast.28), calls=%async_computation.4 | async-start | bytes 2097152 | tf_op jit(solution)/shard_map/all_to_all | solution.py:87
  126.6 29.0 %copy-start.12 = (s32[64]{0:T(128)S(1)}, s32[64]{0:T(128)}, u32[]{:S(2)}) copy-start(s32[64]{0:T(128)} %param.21) | copy-start | bytes 772
  127.8 26.9 %all-to-all-start.5 = ((bf16[512,1,128]{2,1,0:T(2,128)(2,1)}), bf16[512,1,128]{2,1,0:T(2,128)(2,1)S(1)}, u32[]{:S(2)}, u32[]{:S(2)}) async-start(bf16[512,1,128]{2,1,0:T(2,128)(2,1)} %all_to_all.28), calls=%async_computation.5 | async-start | bytes 524288 | tf_op jit(solution)/shard_map/all_to_all | solution.py:174

commit v6 on v5

--- a/solution.py
+++ b/solution.py
@@ -1,7 +1,7 @@
 import jax
 import jax.numpy as jnp
 from jax import lax
-from jax.sharding import PartitionSpec as P
+from jax.sharding import Mesh, PartitionSpec as P
 
 HD = 64
 
@@ -74,18 +74,25 @@
     return context.reshape(fresh_len, -1).astype(jnp.bfloat16)
 
 
-def gather_tp(block, tp_count, axis):
+TP = ("x", "core")
+
+
+def gather_tp(block, tp_count, axis, names=TP):
     copies = jnp.broadcast_to(
         jnp.expand_dims(block, axis), block.shape[:axis] + (tp_count,) + block.shape[axis:]
     )
-    got = lax.all_to_all(copies, "tp", axis, axis, tiled=True)
+    got = lax.all_to_all(copies, names, axis, axis, tiled=True)
     return got.reshape(block.shape[:axis] + (-1,) + block.shape[axis + 1 :])
 
 
-def reduce_tp(partial, tp_count):
+def reduce_tp(partial, tp_count, names=TP):
     rows = partial.shape[0] // tp_count
-    got = lax.all_to_all(partial.reshape(tp_count, rows, -1), "tp", 0, 0, tiled=True)
+    got = lax.all_to_all(partial.reshape(tp_count, rows, -1), names, 0, 0, tiled=True)
     return jnp.sum(got.astype(jnp.float32), axis=0)
+
+
+def from_partner(block):
+    return lax.ppermute(block, "core", [(0, 1), (1, 0)])
 
 
 def permute_rows(order, table):
@@ -113,8 +120,12 @@
     narrow_weight,
     narrow_bias,
 ):
-    tp_count = lax.axis_size("tp")
-    tp_index = lax.axis_index("tp")
+    x_count = lax.axis_size("x")
+    tp_count = x_count * lax.axis_size("core")
+    tp_index = lax.axis_index(TP)
+    partner_widen = from_partner(widen_weight)
+    partner_widen_bias = from_partner(widen_bias)
+    partner_narrow = from_partner(narrow_weight)
     slot_index = lax.axis_index("req")
     length = cache_lengths[owner_order[slot_index]]
     routed_in = permute_rows(owner_order, hidden_in)
@@ -155,17 +166,20 @@
         norm_gains[0],
         norm_biases[0],
     ).astype(jnp.bfloat16)
-    normed_all = gather_tp(normed, tp_count, 0)
-    widened = jnp.dot(normed_all, widen_weight, preferred_element_type=jnp.float32) + widen_bias.astype(
-        jnp.float32
-    )
-    activated = lax.optimization_barrier(
-        jax.nn.gelu(widened, approximate=False).astype(jnp.bfloat16)
-    )
-    fed_total = reduce_tp(
-        jnp.dot(activated, narrow_weight, preferred_element_type=jnp.float32).astype(jnp.bfloat16),
-        tp_count,
-    )
+    normed_half = gather_tp(normed, x_count, 0, "x")
+
+    def unit_group(widen_block, bias_block, narrow_block):
+        widened = jnp.dot(normed_half, widen_block, preferred_element_type=jnp.float32)
+        activated = jax.nn.gelu(
+            widened + bias_block.astype(jnp.float32), approximate=False
+        ).astype(jnp.bfloat16)
+        partial = jnp.dot(activated, narrow_block, preferred_element_type=jnp.float32)
+        return partial.astype(jnp.bfloat16).astype(jnp.float32)
+
+    pair = unit_group(widen_weight, widen_bias, narrow_weight) + unit_group(
+        partner_widen, partner_widen_bias, partner_narrow
+    )
+    fed_total = reduce_tp(pair.astype(jnp.bfloat16), x_count, "x")
     updated = layer_norm(
         normed.astype(jnp.float32) + fed_total + narrow_bias.astype(jnp.float32),
         norm_gains[1],
@@ -173,7 +187,7 @@
     ).astype(jnp.bfloat16)
     returned = lax.all_to_all(
         updated.reshape(rows * tp_count, width // tp_count),
-        ("req", "tp"),
+        ("req",) + TP,
         0,
         0,
         tiled=True,
@@ -183,25 +197,27 @@
 
 
 def solution(mesh):
+    req_count, tp_count = mesh.devices.shape
+    split = Mesh(mesh.devices.reshape(req_count, tp_count // 2, 2), ("req",) + TP)
     in_specs = (
-        P(None, "req", "tp"),
-        P("req", None, "tp"),
-        P("req", None, "tp"),
-        P(),
-        P(),
-        P(),
-        P(None, None, "tp"),
-        P(None, "tp"),
-        P("tp", None),
-        P(),
-        P(),
-        P(),
-        P(None, "tp"),
-        P("tp"),
-        P("tp", None),
-        P(),
-    )
-    out_specs = (P(None, "req", "tp"), P(None, "req", None, "tp"))
+        P(None, "req", TP),
+        P("req", None, TP),
+        P("req", None, TP),
+        P(),
+        P(),
+        P(),
+        P(None, None, TP),
+        P(None, TP),
+        P(TP, None),
+        P(),
+        P(),
+        P(),
+        P(None, TP),
+        P(TP),
+        P(TP, None),
+        P(),
+    )
+    out_specs = (P(None, "req", TP), P(None, "req", None, TP))
     return jax.shard_map(
-        on_device, mesh=mesh, in_specs=in_specs, out_specs=out_specs, check_vma=False
-    )
+        on_device, mesh=split, in_specs=in_specs, out_specs=out_specs, check_vma=False
+    )

time: 157 us -> 143 us (0.911)
  waiting for transfers between devices: 70.6 us -> 49.6 us
  starting transfers between devices: 29.2 us -> 36.8 us
    all_to_all x4, waiting for transfers between devices: 54.2 us -> 32.4 us  [the longest x2 21.9 us: reduce_tp(): lax.all_to_all(partial.reshape(tp_count, rows, -1), names, 0, 0, tiled=True)]
    ppermute x0 -> x3, starting transfers between devices: none -> 7.19 us  [from_partner(): return lax.ppermute(block, 'core', [(0, 1), (1, 0)])]
    all_to_all x1, starting transfers between devices: 9.38 us -> 11.6 us  [on_device(): lax.all_to_all(updated.reshape(rows * tp_count, width // tp_count), ('req...]
    all_to_all x4, starting transfers between devices: 19.9 us -> 18 us  [the longest x2 10.1 us: gather_tp(): got = lax.all_to_all(copies, names, axis, axis, tiled=True)]
    dot_general x2, matrix products: 5.99 us -> 7.69 us  [unit_group(): jnp.dot(activated, narrow_block, preferred_element_type=jnp.float32)]
  transfers between devices with their start and end apart: 5 -> 8, of which waited for: 5 -> 6; matrix products, arithmetic and copies ran while one was open for 3% -> 10% of each run, Pallas kernels for 0% -> 0%
where the time goes in v6:
time: 143 us; the launch traced here: 142 us
  waiting for transfers between devices  49.6 us (35%)
  starting transfers between devices  36.8 us (26%)
  blocking collectives  28.6 us (20%)
  matrix products  13.5 us (9%)
  local copies, waits for them, and re-layouts  6.61 us (5%)
  other arithmetic  4.13 us (3%)
  between operations  3.09 us (2%)
    all_to_all x1, blocking collectives, on_device(): lax.all_to_all(jnp.transpose(routed_in, (1, 0, 2)), 'req', split_axis=1,...  28.6 us
    all_to_all x2, waiting for transfers between devices, reduce_tp(): lax.all_to_all(partial.reshape(tp_count, rows, -1), names, 0, 0, tiled=True)  21.9 us
    all_to_all x1, waiting for transfers between devices, on_device(): lax.all_to_all(updated.reshape(rows * tp_count, width // tp_count), ('req...  16.4 us
    all_to_all x1, starting transfers between devices, on_device(): lax.all_to_all(updated.reshape(rows * tp_count, width // tp_count), ('req...  11.6 us
    all_to_all x2, waiting for transfers between devices, gather_tp(): got = lax.all_to_all(copies, names, axis, axis, tiled=True)  10.6 us
    all_to_all x2, starting transfers between devices, gather_tp(): got = lax.all_to_all(copies, names, axis, axis, tiled=True)  10.1 us
    all_to_all x2, starting transfers between devices, reduce_tp(): lax.all_to_all(partial.reshape(tp_count, rows, -1), names, 0, 0, tiled=True)  7.9 us
    dot_general x2, matrix products, unit_group(): jnp.dot(activated, narrow_block, preferred_element_type=jnp.float32)  7.69 us
  transfers between devices with their start and end apart: 8, of which 6 were waited for; matrix products, arithmetic and copies ran while one was open for 10% of the time, Pallas kernels for 0%

profile of v6, /device:TPU:1, one launch (start us, length us, event | category | flops | bytes accessed | tf_op | source)
XLA Modules:
  0.0 142.3 jit_solution(3064983816698585424)
XLA Ops:
  0.6 1.2 fusion.12
  1.9 28.6 %all_to_all.35 = bf16[8,64,128]{2,0,1:T(8,128)(2,1)S(1)} all-to-all(bf16[8,64,128]{2,0,1:T(8,128)(2,1)S(1)} %bitcast.117), channel_id=1, replica_groups=mesh['req'=64,'x'=4,'core'=2] {'req'}, dimensions={1} | all-to-all | bytes 262144 | tf_op jit(solution)/shard_map/all_to_all | solution.py:133
  30.5 1.1 broadcast_in_dim.41
  31.6 6.6 %all-to-all-start.1 = ((bf16[512,8,128]{2,0,1:T(8,128)(2,1)}), bf16[512,8,128]{2,0,1:T(8,128)(2,1)S(1)}, u32[]{:S(2)}, u32[]{:S(2)}) async-start(bf16[512,8,128]{2,0,1:T(8,128)(2,1)} %broadcast_in_dim.41), calls=%async_computation.1 | async-start | bytes 2097152 | tf_op jit(solution)/shard_map/all_to_all | solution.py:84
  38.2 1.9 %collective-permute-start.2 = (bf16[512,1024]{1,0:T(8,128)(2,1)}, bf16[512,1024]{1,0:T(8,128)(2,1)}, u32[]{:S(2)}, u32[]{:S(2)}) collective-permute-start(bf16[512,1024]{1,0:T(8,128)(2,1)} %param.30), channel_id=1, source_target_pairs={{0,1},{1,0},{2,3},{3,2},{4,5},{5,4},{6,7},{7,6},{8,9},{9,8},{10,11... | collective-permute-start | bytes 3145736 | tf_op jit(solution)/shard_map/ppermute | solution.py:95
  40.1 2.4 %collective-permute-start = (bf16[1024,512]{1,0:T(8,128)(2,1)}, bf16[1024,512]{1,0:T(8,128)(2,1)}, u32[]{:S(2)}, u32[]{:S(2)}) collective-permute-start(bf16[1024,512]{1,0:T(8,128)(2,1)} %param.28), channel_id=1, source_target_pairs={{0,1},{1,0},{2,3},{3,2},{4,5},{5,4},{6,7},{7,6},{8,9},{9,8},{10,11... | collective-permute-start | bytes 3145736 | tf_op jit(solution)/shard_map/ppermute | solution.py:95
  42.6 0.6 dynamic_slice.14
  45.7 0.6 dynamic_slice.15
  46.3 0.6 iota_compare_fusion.4
  47.2 6.0 %all-to-all-done.1 = bf16[512,8,128]{2,0,1:T(8,128)(2,1)S(1)} async-done(((bf16[512,8,128]{2,0,1:T(8,128)(2,1)}), bf16[512,8,128]{2,0,1:T(8,128)(2,1)S(1)}, u32[]{:S(2)}, u32[]{:S(2)}) %all-to-all-start.1) | async-done | bytes 1048608 | tf_op jit(solution)/shard_map/all_to_all | solution.py:84
  53.2 0.6 fusion.184
  55.1 0.6 convolution_bitcast_fusion
  55.7 0.9 fusion
  56.6 0.7 fusion.11
  57.3 1.4 %convolution_convert_fusion = bf16[512,1024]{1,0:T(8,128)(2,1)} fusion(bf16[512,128]{0,1:T(8,128)(2,1)S(1)} %bitcast.125, bf16[128,1024]{1,0:T(8,128)(2,1)S(1)} %copy-done), kind=kOutput, calls=%fused_computation.9 | convolution fusion | flops 134742016 | bytes 1441792 | tf_op jit(solution)/shard_map/dot_general | solution.py:161
  58.7 4.4 %all-to-all-start.2 = ((bf16[8,64,1024]{2,1,0:T(8,128)(2,1)}), bf16[8,64,1024]{2,1,0:T(8,128)(2,1)S(1)}, u32[]{:S(2)}, u32[]{:S(2)}) async-start(bf16[8,64,1024]{2,1,0:T(8,128)(2,1)} %bitcast.24), calls=%async_computation.2 | async-start | bytes 2097152 | tf_op jit(solution)/shard_map/all_to_all | solution.py:90
  63.4 14.8 %all-to-all-done.2 = bf16[8,64,1024]{2,1,0:T(8,128)(2,1)S(1)} async-done(((bf16[8,64,1024]{2,1,0:T(8,128)(2,1)}), bf16[8,64,1024]{2,1,0:T(8,128)(2,1)S(1)}, u32[]{:S(2)}, u32[]{:S(2)}) %all-to-all-start.2) | async-done | bytes 1048608 | tf_op jit(solution)/shard_map/all_to_all | solution.py:90
  78.8 0.9 broadcast_in_dim.45
  79.6 3.5 %all-to-all-start.3 = ((bf16[4,64,1024]{2,1,0:T(8,128)(2,1)}), bf16[4,64,1024]{2,1,0:T(8,128)(2,1)S(1)}, u32[]{:S(2)}, u32[]{:S(2)}) async-start(bf16[4,64,1024]{2,1,0:T(8,128)(2,1)} %broadcast_in_dim.45), calls=%async_computation.3 | async-start | bytes 1048576 | tf_op jit(solution)/shard_map/all_to_all | solution.py:84
  83.1 2.9 %collective-permute-start.1 = (bf16[512]{0:T(512)(128)(2,1)S(1)}, bf16[512]{0:T(512)(128)(2,1)S(1)}, u32[]{:S(2)}, u32[]{:S(2)}) collective-permute-start(bf16[512]{0:T(512)(128)(2,1)S(1)} %copy-done.9), channel_id=1, source_target_pairs={{0,1},{1,0},{2,3},{3,2},{4,5},{5,4},{6,7},{7,6},{8,9},{9,8},{10,11... | collective-permute-start | bytes 3080 | tf_op jit(solution)/shard_map/ppermute | solution.py:95
  86.0 0.8 collective-permute-done.1
  86.8 4.6 %all-to-all-done.3 = bf16[4,64,1024]{2,1,0:T(8,128)(2,1)S(1)} async-done(((bf16[4,64,1024]{2,1,0:T(8,128)(2,1)}), bf16[4,64,1024]{2,1,0:T(8,128)(2,1)S(1)}, u32[]{:S(2)}, u32[]{:S(2)}) %all-to-all-start.3) | async-done | bytes 524320 | tf_op jit(solution)/shard_map/all_to_all | solution.py:84
  91.4 3.4 %fusion.6 = f32[256,1024]{1,0:T(8,128)S(1)} fusion(bf16[512,1024]{1,0:T(8,128)(2,1)} %param.30, bf16[256,1024]{1,0:T(8,128)(2,1)S(1)} %bitcast.115, bf16[1024,512]{1,0:T(8,128)(2,1)} %param.28, f32[512]{0:T(512)S(1)} %convert_element_type.127), kind=kOutput, calls=%fused_computation.14 | convolution fusion | flops 546045952 | bytes 3672064 | tf_op jit(solution)/shard_map/dot_general | solution.py:176
  94.9 4.2 %fusion.7 = bf16[256,1024]{1,0:T(8,128)(2,1)} fusion(f32[256,1024]{1,0:T(8,128)S(1)} %fusion.6, bf16[512,1024]{1,0:T(8,128)(2,1)} %collective-permute-done.2, bf16[256,1024]{1,0:T(8,128)(2,1)S(1)} %bitcast.116, bf16[1024,512]{1,0:T(8,128)(2,1)} %collective-permute-done, f32[512]{0:T(512)S(1)} %convert_element_type.131), kind=kOutput, calls=%fused_computation.15 | convolution fusion | flops 546570240 | bytes 4196352 | tf_op jit(solution)/shard_map/dot_general | solution.py:176
  99.1 3.5 %all-to-all-start.4 = ((bf16[4,64,1024]{2,1,0:T(8,128)(2,1)}), bf16[4,64,1024]{2,1,0:T(8,128)(2,1)S(1)}, u32[]{:S(2)}, u32[]{:S(2)}) async-start(bf16[4,64,1024]{2,1,0:T(8,128)(2,1)} %bitcast.28), calls=%async_computation.4 | async-start | bytes 1048576 | tf_op jit(solution)/shard_map/all_to_all | solution.py:90
  102.6 7.1 %all-to-all-done.4 = bf16[4,64,1024]{2,1,0:T(8,128)(2,1)S(1)} async-done(((bf16[4,64,1024]{2,1,0:T(8,128)(2,1)}), bf16[4,64,1024]{2,1,0:T(8,128)(2,1)S(1)}, u32[]{:S(2)}, u32[]{:S(2)}) %all-to-all-start.4) | async-done | bytes 524320 | tf_op jit(solution)/shard_map/all_to_all | solution.py:90
  110.5 0.8 all_to_all.28
  111.3 11.6 %all-to-all-start.5 = ((bf16[512,1,128]{2,1,0:T(2,128)(2,1)}), bf16[512,1,128]{2,1,0:T(2,128)(2,1)S(1)}, u32[]{:S(2)}, u32[]{:S(2)}) async-start(bf16[512,1,128]{2,1,0:T(2,128)(2,1)} %all_to_all.28), calls=%async_computation.5 | async-start | bytes 524288 | tf_op jit(solution)/shard_map/all_to_all | solution.py:188
  123.2 0.9 copy.79
  124.1 16.4 %all-to-all-done.5 = bf16[512,1,128]{2,1,0:T(2,128)(2,1)S(1)} async-done(((bf16[512,1,128]{2,1,0:T(2,128)(2,1)}), bf16[512,1,128]{2,1,0:T(2,128)(2,1)S(1)}, u32[]{:S(2)}, u32[]{:S(2)}) %all-to-all-start.5) | async-done | bytes 131104 | tf_op jit(solution)/shard_map/all_to_all | solution.py:188
  140.5 0.8 reduce
  141.6 0.7 copy.71
  (68 shorter events, 4.3 us)
Async XLA Ops:
  0.6 56.6 %copy-start = (bf16[128,1024]{1,0:T(8,128)(2,1)S(1)}, bf16[128,1024]{1,0:T(8,128)(2,1)}, u32[]{:S(2)}) copy-start(bf16[128,1024]{1,0:T(8,128)(2,1)} %param.24) | copy-start | bytes 786436
  1.8 40.7 %copy-start.10 = (s32[64]{0:T(128)S(1)}, s32[64]{0:T(128)}, u32[]{:S(2)}) copy-start(s32[64]{0:T(128)} %param.20) | copy-start | bytes 772
  1.8 42.6 %copy-start.6 = (bf16[1024]{0:T(1024)(128)(2,1)S(1)}, bf16[1024]{0:T(1024)(128)(2,1)}, u32[]{:S(2)}) copy-start(bf16[1024]{0:T(1024)(128)(2,1)} %param.25) | copy-start | bytes 6148
  1.9 42.6 %copy-start.2 = (bf16[1,512,128]{2,1,0:T(8,128)(2,1)S(1)}, bf16[1,512,128]{2,1,0:T(8,128)(2,1)}, u32[]{:S(2)}) copy-start(bf16[1,512,128]{2,1,0:T(8,128)(2,1)} %param.18) | copy-start | bytes 393220
  1.9 42.7 %copy-start.1 = (bf16[3,1024,128]{2,1,0:T(8,128)(2,1)S(1)}, bf16[3,1024,128]{2,1,0:T(8,128)(2,1)}, u32[]{:S(2)}) copy-start(bf16[3,1024,128]{2,1,0:T(8,128)(2,1)} %param.22) | copy-start | bytes 2359300
  31.6 13.3 %copy-start.8 = (bf16[3,128]{1,0:T(4,128)(2,1)S(1)}, bf16[3,128]{1,0:T(4,128)(2,1)}, u32[]{:S(2)}) copy-start(bf16[3,128]{1,0:T(4,128)(2,1)} %param.23) | copy-start | bytes 2308
  31.6 13.3 %copy-start.3 = (bf16[1,512,128]{2,1,0:T(8,128)(2,1)S(1)}, bf16[1,512,128]{2,1,0:T(8,128)(2,1)}, u32[]{:S(2)}) copy-start(bf16[1,512,128]{2,1,0:T(8,128)(2,1)} %param.17) | copy-start | bytes 393220
  31.6 14.1 %copy-start.12 = (s32[64]{0:T(128)S(1)}, s32[64]{0:T(128)}, u32[]{:S(2)}) copy-start(s32[64]{0:T(128)} %param.19) | copy-start | bytes 772
  31.6 21.6 %all-to-all-start.1 = ((bf16[512,8,128]{2,0,1:T(8,128)(2,1)}), bf16[512,8,128]{2,0,1:T(8,128)(2,1)S(1)}, u32[]{:S(2)}, u32[]{:S(2)}) async-start(bf16[512,8,128]{2,0,1:T(8,128)(2,1)} %broadcast_in_dim.41), calls=%async_computation.1 | async-start | bytes 2097152 | tf_op jit(solution)/shard_map/all_to_all | solution.py:84
  38.2 56.7 %collective-permute-start.2 = (bf16[512,1024]{1,0:T(8,128)(2,1)}, bf16[512,1024]{1,0:T(8,128)(2,1)}, u32[]{:S(2)}, u32[]{:S(2)}) collective-permute-start(bf16[512,1024]{1,0:T(8,128)(2,1)} %param.30), channel_id=1, source_target_pairs={{0,1},{1,0},{2,3},{3,2},{4,5},{5,4},{6,7},{7,6},{8,9},{9,8},{10,11... | collective-permute-start | bytes 3145736 | tf_op jit(solution)/shard_map/ppermute | solution.py:95
  40.1 54.7 %collective-permute-start = (bf16[1024,512]{1,0:T(8,128)(2,1)}, bf16[1024,512]{1,0:T(8,128)(2,1)}, u32[]{:S(2)}, u32[]{:S(2)}) collective-permute-start(bf16[1024,512]{1,0:T(8,128)(2,1)} %param.28), channel_id=1, source_target_pairs={{0,1},{1,0},{2,3},{3,2},{4,5},{5,4},{6,7},{7,6},{8,9},{9,8},{10,11... | collective-permute-start | bytes 3145736 | tf_op jit(solution)/shard_map/ppermute | solution.py:95
  57.2 5.9 %copy-start.4 = (bf16[2,1024]{1,0:T(2,128)(2,1)S(1)}, bf16[2,1024]{1,0:T(2,128)(2,1)}, u32[]{:S(2)}) copy-start(bf16[2,1024]{1,0:T(2,128)(2,1)} %param.27) | copy-start | bytes 12292
  57.2 5.9 %copy-start.5 = (bf16[2,1024]{1,0:T(2,128)(2,1)S(1)}, bf16[2,1024]{1,0:T(2,128)(2,1)}, u32[]{:S(2)}) copy-start(bf16[2,1024]{1,0:T(2,128)(2,1)} %param.26) | copy-start | bytes 12292
  58.7 19.4 %all-to-all-start.2 = ((bf16[8,64,1024]{2,1,0:T(8,128)(2,1)}), bf16[8,64,1024]{2,1,0:T(8,128)(2,1)S(1)}, u32[]{:S(2)}, u32[]{:S(2)}) async-start(bf16[8,64,1024]{2,1,0:T(8,128)(2,1)} %bitcast.24), calls=%async_computation.2 | async-start | bytes 2097152 | tf_op jit(solution)/shard_map/all_to_all | solution.py:90
  63.4 19.7 %copy-start.9 = (bf16[512]{0:T(512)(128)(2,1)S(1)}, bf16[512]{0:T(512)(128)(2,1)}, u32[]{:S(2)}) copy-start(bf16[512]{0:T(512)(128)(2,1)} %param.29) | copy-start | bytes 3076
  79.6 11.8 %all-to-all-start.3 = ((bf16[4,64,1024]{2,1,0:T(8,128)(2,1)}), bf16[4,64,1024]{2,1,0:T(8,128)(2,1)S(1)}, u32[]{:S(2)}, u32[]{:S(2)}) async-start(bf16[4,64,1024]{2,1,0:T(8,128)(2,1)} %broadcast_in_dim.45), calls=%async_computation.3 | async-start | bytes 1048576 | tf_op jit(solution)/shard_map/all_to_all | solution.py:84
  83.1 3.7 %collective-permute-start.1 = (bf16[512]{0:T(512)(128)(2,1)S(1)}, bf16[512]{0:T(512)(128)(2,1)S(1)}, u32[]{:S(2)}, u32[]{:S(2)}) collective-permute-start(bf16[512]{0:T(512)(128)(2,1)S(1)} %copy-done.9), channel_id=1, source_target_pairs={{0,1},{1,0},{2,3},{3,2},{4,5},{5,4},{6,7},{7,6},{8,9},{9,8},{10,11... | collective-permute-start | bytes 3080 | tf_op jit(solution)/shard_map/ppermute | solution.py:95
  94.9 7.8 %copy-start.7 = (bf16[1024]{0:T(1024)(128)(2,1)S(1)}, bf16[1024]{0:T(1024)(128)(2,1)}, u32[]{:S(2)}) copy-start(bf16[1024]{0:T(1024)(128)(2,1)} %param.31) | copy-start | bytes 6148
  99.1 10.6 %all-to-all-start.4 = ((bf16[4,64,1024]{2,1,0:T(8,128)(2,1)}), bf16[4,64,1024]{2,1,0:T(8,128)(2,1)S(1)}, u32[]{:S(2)}, u32[]{:S(2)}) async-start(bf16[4,64,1024]{2,1,0:T(8,128)(2,1)} %bitcast.28), calls=%async_computation.4 | async-start | bytes 1048576 | tf_op jit(solution)/shard_map/all_to_all | solution.py:90
  110.1 31.3 %copy-start.11 = (s32[64]{0:T(128)S(1)}, s32[64]{0:T(128)}, u32[]{:S(2)}) copy-start(s32[64]{0:T(128)} %param.21) | copy-start | bytes 772
  111.3 29.2 %all-to-all-start.5 = ((bf16[512,1,128]{2,1,0:T(2,128)(2,1)}), bf16[512,1,128]{2,1,0:T(2,128)(2,1)S(1)}, u32[]{:S(2)}, u32[]{:S(2)}) async-start(bf16[512,1,128]{2,1,0:T(2,128)(2,1)} %all_to_all.28), calls=%async_computation.5 | async-start | bytes 524288 | tf_op jit(solution)/shard_map/all_to_all | solution.py:188

commit v7 on v6

--- a/solution.py
+++ b/solution.py
@@ -126,6 +126,8 @@
     partner_widen = from_partner(widen_weight)
     partner_widen_bias = from_partner(widen_bias)
     partner_narrow = from_partner(narrow_weight)
+    partner_output = from_partner(output_weight)
+    core_index = lax.axis_index("core")
     slot_index = lax.axis_index("req")
     length = cache_lengths[owner_order[slot_index]]
     routed_in = permute_rows(owner_order, hidden_in)
@@ -157,9 +159,21 @@
         lax.dynamic_slice_in_dim(token_rows, tp_index * rows, rows).astype(jnp.float32)
         + output_bias.astype(jnp.float32)
     )
+    halves = context.reshape(x_count, 2, rows, -1)
+    kept = lax.dynamic_index_in_dim(halves, core_index, 1, keepdims=False)
+    sent = lax.dynamic_index_in_dim(halves, 1 - core_index, 1, keepdims=False)
+    got = from_partner(sent)
+
+    def head_group(context_rows, weight_block):
+        partial = jnp.dot(
+            context_rows.reshape(x_count * rows, -1), weight_block, preferred_element_type=jnp.float32
+        )
+        return partial.astype(jnp.bfloat16).astype(jnp.float32)
+
     attended = reduce_tp(
-        jnp.dot(context, output_weight, preferred_element_type=jnp.float32).astype(jnp.bfloat16),
-        tp_count,
+        (head_group(kept, output_weight) + head_group(got, partner_output)).astype(jnp.bfloat16),
+        x_count,
+        "x",
     )
     normed = layer_norm(
         own_rows + attended,

time: 143 us -> 141 us (0.986)
  waiting for transfers between devices: 49.6 us -> 41.6 us
  starting transfers between devices: 36.8 us -> 41.1 us
    all_to_all x2, waiting for transfers between devices: 21.9 us -> 15.7 us  [reduce_tp(): lax.all_to_all(partial.reshape(tp_count, rows, -1), names, 0, 0, tiled=True)]
    ppermute x3 -> x5, starting transfers between devices: 7.19 us -> 12.2 us  [from_partner(): return lax.ppermute(block, 'core', [(0, 1), (1, 0)])]
    all_to_all x2, waiting for transfers between devices: 10.6 us -> 8.09 us  [gather_tp(): got = lax.all_to_all(copies, names, axis, axis, tiled=True)]
  transfers between devices with their start and end apart: 8 -> 10, of which waited for: 6 -> 7; matrix products, arithmetic and copies ran while one was open for 10% -> 11% of each run, Pallas kernels for 0% -> 0%
where the time goes in v7:
time: 141 us; the launch traced here: 140 us
  waiting for transfers between devices  41.6 us (30%)
  starting transfers between devices  41.1 us (29%)
  blocking collectives  28.6 us (20%)
  matrix products  14.3 us (10%)
  local copies, waits for them, and re-layouts  7.61 us (5%)
  other arithmetic  4.05 us (3%)
  between operations  3.12 us (2%)
    all_to_all x1, blocking collectives, on_device(): lax.all_to_all(jnp.transpose(routed_in, (1, 0, 2)), 'req', split_axis=1,...  28.6 us
    all_to_all x1, waiting for transfers between devices, on_device(): lax.all_to_all(updated.reshape(rows * tp_count, width // tp_count), ('req...  16.4 us
    all_to_all x2, waiting for transfers between devices, reduce_tp(): lax.all_to_all(partial.reshape(tp_count, rows, -1), names, 0, 0, tiled=True)  15.7 us
    ppermute x5, starting transfers between devices, from_partner(): return lax.ppermute(block, 'core', [(0, 1), (1, 0)])  12.2 us
    all_to_all x1, starting transfers between devices, on_device(): lax.all_to_all(updated.reshape(rows * tp_count, width // tp_count), ('req...  11.6 us
    all_to_all x2, starting transfers between devices, gather_tp(): got = lax.all_to_all(copies, names, axis, axis, tiled=True)  10.1 us
    dot_general x2, matrix products, unit_group(): jnp.dot(activated, narrow_block, preferred_element_type=jnp.float32)  8.69 us
    all_to_all x2, waiting for transfers between devices, gather_tp(): got = lax.all_to_all(copies, names, axis, axis, tiled=True)  8.09 us
  transfers between devices with their start and end apart: 10, of which 7 were waited for; matrix products, arithmetic and copies ran while one was open for 11% of the time, Pallas kernels for 0%

profile of v7, /device:TPU:1, one launch (start us, length us, event | category | flops | bytes accessed | tf_op | source)
XLA Modules:
  0.0 140.3 jit_solution(529316309616871397)
XLA Ops:
  0.6 1.1 fusion.16
  1.9 28.6 %all_to_all.35 = bf16[8,64,128]{2,0,1:T(8,128)(2,1)S(1)} all-to-all(bf16[8,64,128]{2,0,1:T(8,128)(2,1)S(1)} %bitcast.123), channel_id=1, replica_groups=mesh['req'=64,'x'=4,'core'=2] {'req'}, dimensions={1} | all-to-all | bytes 262144 | tf_op jit(solution)/shard_map/all_to_all | solution.py:135
  30.4 1.1 broadcast_in_dim.41
  31.6 6.6 %all-to-all-start.1 = ((bf16[512,8,128]{2,0,1:T(8,128)(2,1)}), bf16[512,8,128]{2,0,1:T(8,128)(2,1)S(1)}, u32[]{:S(2)}, u32[]{:S(2)}) async-start(bf16[512,8,128]{2,0,1:T(8,128)(2,1)} %broadcast_in_dim.41), calls=%async_computation.1 | async-start | bytes 2097152 | tf_op jit(solution)/shard_map/all_to_all | solution.py:84
  38.2 1.9 %collective-permute-start.1 = (bf16[128,1024]{1,0:T(8,128)(2,1)S(1)}, bf16[128,1024]{1,0:T(8,128)(2,1)S(1)}, u32[]{:S(2)}, u32[]{:S(2)}) collective-permute-start(bf16[128,1024]{1,0:T(8,128)(2,1)S(1)} %copy-done.1), channel_id=1, source_target_pairs={{0,1},{1,0},{2,3},{3,2},{4,5},{5,4},{6,7},{7,6},{8,9},{9,8},{10,11... | collective-permute-start | bytes 786440 | tf_op jit(solution)/shard_map/ppermute | solution.py:95
  40.1 2.4 %collective-permute-start.4 = (bf16[512,1024]{1,0:T(8,128)(2,1)}, bf16[512,1024]{1,0:T(8,128)(2,1)}, u32[]{:S(2)}, u32[]{:S(2)}) collective-permute-start(bf16[512,1024]{1,0:T(8,128)(2,1)} %param.30), channel_id=1, source_target_pairs={{0,1},{1,0},{2,3},{3,2},{4,5},{5,4},{6,7},{7,6},{8,9},{9,8},{10,11... | collective-permute-start | bytes 3145736 | tf_op jit(solution)/shard_map/ppermute | solution.py:95
  42.5 1.9 %collective-permute-start.2 = (bf16[1024,512]{1,0:T(8,128)(2,1)}, bf16[1024,512]{1,0:T(8,128)(2,1)}, u32[]{:S(2)}, u32[]{:S(2)}) collective-permute-start(bf16[1024,512]{1,0:T(8,128)(2,1)} %param.28), channel_id=1, source_target_pairs={{0,1},{1,0},{2,3},{3,2},{4,5},{5,4},{6,7},{7,6},{8,9},{9,8},{10,11... | collective-permute-start | bytes 3145736 | tf_op jit(solution)/shard_map/ppermute | solution.py:95
  44.5 0.6 dynamic_slice.21
  48.2 0.6 iota_compare_fusion.4
  49.2 4.0 %all-to-all-done.1 = bf16[512,8,128]{2,0,1:T(8,128)(2,1)S(1)} async-done(((bf16[512,8,128]{2,0,1:T(8,128)(2,1)}), bf16[512,8,128]{2,0,1:T(8,128)(2,1)S(1)}, u32[]{:S(2)}, u32[]{:S(2)}) %all-to-all-start.1) | async-done | bytes 1048608 | tf_op jit(solution)/shard_map/all_to_all | solution.py:84
  53.2 0.6 fusion.188
  55.6 0.9 fusion
  56.5 0.7 fusion.15
  58.2 2.9 %collective-permute-start = (bf16[4,64,128]{2,1,0:T(8,128)(2,1)S(1)}, bf16[4,64,128]{2,1,0:T(8,128)(2,1)S(1)}, u32[]{:S(2)}, u32[]{:S(2)}) collective-permute-start(bf16[4,64,128]{2,1,0:T(8,128)(2,1)S(1)} %bitcast.140), channel_id=1, source_target_pairs={{0,1},{1,0},{2,3},{3,2},{4,5},{5,4},{6,7},{7,6},{8,9},{9,8},{10,11... | collective-permute-start | bytes 196616 | tf_op jit(solution)/shard_map/ppermute | solution.py:95
  62.0 1.1 fusion.10
  63.1 3.5 %all-to-all-start.2 = ((bf16[4,64,1024]{2,1,0:T(8,128)(2,1)}), bf16[4,64,1024]{2,1,0:T(8,128)(2,1)S(1)}, u32[]{:S(2)}, u32[]{:S(2)}) async-start(bf16[4,64,1024]{2,1,0:T(8,128)(2,1)} %bitcast.26), calls=%async_computation.2 | async-start | bytes 1048576 | tf_op jit(solution)/shard_map/all_to_all | solution.py:90
  66.8 9.0 %all-to-all-done.2 = bf16[4,64,1024]{2,1,0:T(8,128)(2,1)S(1)} async-done(((bf16[4,64,1024]{2,1,0:T(8,128)(2,1)}), bf16[4,64,1024]{2,1,0:T(8,128)(2,1)S(1)}, u32[]{:S(2)}, u32[]{:S(2)}) %all-to-all-start.2) | async-done | bytes 524320 | tf_op jit(solution)/shard_map/all_to_all | solution.py:90
  76.3 0.9 broadcast_in_dim.45
  77.1 3.5 %all-to-all-start.3 = ((bf16[4,64,1024]{2,1,0:T(8,128)(2,1)}), bf16[4,64,1024]{2,1,0:T(8,128)(2,1)S(1)}, u32[]{:S(2)}, u32[]{:S(2)}) async-start(bf16[4,64,1024]{2,1,0:T(8,128)(2,1)} %broadcast_in_dim.45), calls=%async_computation.3 | async-start | bytes 1048576 | tf_op jit(solution)/shard_map/all_to_all | solution.py:84
  80.6 3.1 %collective-permute-start.3 = (bf16[512]{0:T(512)(128)(2,1)S(1)}, bf16[512]{0:T(512)(128)(2,1)S(1)}, u32[]{:S(2)}, u32[]{:S(2)}) collective-permute-start(bf16[512]{0:T(512)(128)(2,1)S(1)} %copy-done.9), channel_id=1, source_target_pairs={{0,1},{1,0},{2,3},{3,2},{4,5},{5,4},{6,7},{7,6},{8,9},{9,8},{10,11... | collective-permute-start | bytes 3080 | tf_op jit(solution)/shard_map/ppermute | solution.py:95
  83.8 0.8 collective-permute-done.3
  84.6 4.1 %all-to-all-done.3 = bf16[4,64,1024]{2,1,0:T(8,128)(2,1)S(1)} async-done(((bf16[4,64,1024]{2,1,0:T(8,128)(2,1)}), bf16[4,64,1024]{2,1,0:T(8,128)(2,1)S(1)}, u32[]{:S(2)}, u32[]{:S(2)}) %all-to-all-start.3) | async-done | bytes 524320 | tf_op jit(solution)/shard_map/all_to_all | solution.py:84
  88.7 4.1 %fusion.6 = f32[256,1024]{1,0:T(8,128)} fusion(bf16[512,1024]{1,0:T(8,128)(2,1)S(1)} %copy-done.12, bf16[256,1024]{1,0:T(8,128)(2,1)S(1)} %bitcast.121, bf16[1024,512]{1,0:T(8,128)(2,1)} %param.28, f32[512]{0:T(512)S(1)} %convert_element_type.144), kind=kOutput, calls=%fused_computation.12 | convolution fusion | flops 546045952 | bytes 3672064 | tf_op jit(solution)/shard_map/dot_general | solution.py:190
  92.8 4.6 %fusion.7 = bf16[256,1024]{1,0:T(8,128)(2,1)} fusion(f32[256,1024]{1,0:T(8,128)} %fusion.6, bf16[512,1024]{1,0:T(8,128)(2,1)} %collective-permute-done.4, bf16[256,1024]{1,0:T(8,128)(2,1)S(1)} %bitcast.122, bf16[1024,512]{1,0:T(8,128)(2,1)} %collective-permute-done.2, f32[512]{0:T(512)S(1)} %convert_element_type.148), kind=kOutput, calls=%fused_computation.13 | convolution fusion | flops 546570240 | bytes 4196352 | tf_op jit(solution)/shard_map/dot_general | solution.py:190
  97.4 3.6 %all-to-all-start.4 = ((bf16[4,64,1024]{2,1,0:T(8,128)(2,1)}), bf16[4,64,1024]{2,1,0:T(8,128)(2,1)S(1)}, u32[]{:S(2)}, u32[]{:S(2)}) async-start(bf16[4,64,1024]{2,1,0:T(8,128)(2,1)} %bitcast.30), calls=%async_computation.4 | async-start | bytes 1048576 | tf_op jit(solution)/shard_map/all_to_all | solution.py:90
  101.0 6.7 %all-to-all-done.4 = bf16[4,64,1024]{2,1,0:T(8,128)(2,1)S(1)} async-done(((bf16[4,64,1024]{2,1,0:T(8,128)(2,1)}), bf16[4,64,1024]{2,1,0:T(8,128)(2,1)S(1)}, u32[]{:S(2)}, u32[]{:S(2)}) %all-to-all-start.4) | async-done | bytes 524320 | tf_op jit(solution)/shard_map/all_to_all | solution.py:90
  108.5 0.8 all_to_all.28
  109.3 11.6 %all-to-all-start.5 = ((bf16[512,1,128]{2,1,0:T(2,128)(2,1)}), bf16[512,1,128]{2,1,0:T(2,128)(2,1)S(1)}, u32[]{:S(2)}, u32[]{:S(2)}) async-start(bf16[512,1,128]{2,1,0:T(2,128)(2,1)} %all_to_all.28), calls=%async_computation.5 | async-start | bytes 524288 | tf_op jit(solution)/shard_map/all_to_all | solution.py:202
  121.3 0.9 copy.86
  122.1 16.4 %all-to-all-done.5 = bf16[512,1,128]{2,1,0:T(2,128)(2,1)S(1)} async-done(((bf16[512,1,128]{2,1,0:T(2,128)(2,1)}), bf16[512,1,128]{2,1,0:T(2,128)(2,1)S(1)}, u32[]{:S(2)}, u32[]{:S(2)}) %all-to-all-start.5) | async-done | bytes 131104 | tf_op jit(solution)/shard_map/all_to_all | solution.py:202
  138.6 0.8 reduce
  139.7 0.7 copy.78
  (79 shorter events, 7.2 us)
Async XLA Ops:
  1.8 36.4 %copy-start.1 = (bf16[128,1024]{1,0:T(8,128)(2,1)S(1)}, bf16[128,1024]{1,0:T(8,128)(2,1)}, u32[]{:S(2)}) copy-start(bf16[128,1024]{1,0:T(8,128)(2,1)} %param.24) | copy-start | bytes 786436
  1.8 42.7 %copy-start.10 = (s32[64]{0:T(128)S(1)}, s32[64]{0:T(128)}, u32[]{:S(2)}) copy-start(s32[64]{0:T(128)} %param.20) | copy-start | bytes 772
  1.8 44.6 %copy-start.6 = (bf16[1024]{0:T(1024)(128)(2,1)S(1)}, bf16[1024]{0:T(1024)(128)(2,1)}, u32[]{:S(2)}) copy-start(bf16[1024]{0:T(1024)(128)(2,1)} %param.25) | copy-start | bytes 6148
  1.8 44.6 %copy-start.2 = (bf16[1,512,128]{2,1,0:T(8,128)(2,1)S(1)}, bf16[1,512,128]{2,1,0:T(8,128)(2,1)}, u32[]{:S(2)}) copy-start(bf16[1,512,128]{2,1,0:T(8,128)(2,1)} %param.18) | copy-start | bytes 393220
  1.9 44.7 %copy-start = (bf16[3,1024,128]{2,1,0:T(8,128)(2,1)S(1)}, bf16[3,1024,128]{2,1,0:T(8,128)(2,1)}, u32[]{:S(2)}) copy-start(bf16[3,1024,128]{2,1,0:T(8,128)(2,1)} %param.22) | copy-start | bytes 2359300
  31.6 15.3 %copy-start.8 = (bf16[3,128]{1,0:T(4,128)(2,1)S(1)}, bf16[3,128]{1,0:T(4,128)(2,1)}, u32[]{:S(2)}) copy-start(bf16[3,128]{1,0:T(4,128)(2,1)} %param.23) | copy-start | bytes 2308
  31.6 15.3 %copy-start.3 = (bf16[1,512,128]{2,1,0:T(8,128)(2,1)S(1)}, bf16[1,512,128]{2,1,0:T(8,128)(2,1)}, u32[]{:S(2)}) copy-start(bf16[1,512,128]{2,1,0:T(8,128)(2,1)} %param.17) | copy-start | bytes 393220
  31.6 16.1 %copy-start.13 = (s32[64]{0:T(128)S(1)}, s32[64]{0:T(128)}, u32[]{:S(2)}) copy-start(s32[64]{0:T(128)} %param.19) | copy-start | bytes 772
  31.6 17.3 %copy-start.4 = (bf16[2,1024]{1,0:T(2,128)(2,1)S(1)}, bf16[2,1024]{1,0:T(2,128)(2,1)}, u32[]{:S(2)}) copy-start(bf16[2,1024]{1,0:T(2,128)(2,1)} %param.27) | copy-start | bytes 12292
  31.6 17.3 %copy-start.5 = (bf16[2,1024]{1,0:T(2,128)(2,1)S(1)}, bf16[2,1024]{1,0:T(2,128)(2,1)}, u32[]{:S(2)}) copy-start(bf16[2,1024]{1,0:T(2,128)(2,1)} %param.26) | copy-start | bytes 12292
  31.6 21.6 %all-to-all-start.1 = ((bf16[512,8,128]{2,0,1:T(8,128)(2,1)}), bf16[512,8,128]{2,0,1:T(8,128)(2,1)S(1)}, u32[]{:S(2)}, u32[]{:S(2)}) async-start(bf16[512,8,128]{2,0,1:T(8,128)(2,1)} %broadcast_in_dim.41), calls=%async_computation.1 | async-start | bytes 2097152 | tf_op jit(solution)/shard_map/all_to_all | solution.py:84
  38.2 23.2 %collective-permute-start.1 = (bf16[128,1024]{1,0:T(8,128)(2,1)S(1)}, bf16[128,1024]{1,0:T(8,128)(2,1)S(1)}, u32[]{:S(2)}, u32[]{:S(2)}) collective-permute-start(bf16[128,1024]{1,0:T(8,128)(2,1)S(1)} %copy-done.1), channel_id=1, source_target_pairs={{0,1},{1,0},{2,3},{3,2},{4,5},{5,4},{6,7},{7,6},{8,9},{9,8},{10,11... | collective-permute-start | bytes 786440 | tf_op jit(solution)/shard_map/ppermute | solution.py:95
  40.1 52.7 %collective-permute-start.4 = (bf16[512,1024]{1,0:T(8,128)(2,1)}, bf16[512,1024]{1,0:T(8,128)(2,1)}, u32[]{:S(2)}, u32[]{:S(2)}) collective-permute-start(bf16[512,1024]{1,0:T(8,128)(2,1)} %param.30), channel_id=1, source_target_pairs={{0,1},{1,0},{2,3},{3,2},{4,5},{5,4},{6,7},{7,6},{8,9},{9,8},{10,11... | collective-permute-start | bytes 3145736 | tf_op jit(solution)/shard_map/ppermute | solution.py:95
  42.5 50.2 %collective-permute-start.2 = (bf16[1024,512]{1,0:T(8,128)(2,1)}, bf16[1024,512]{1,0:T(8,128)(2,1)}, u32[]{:S(2)}, u32[]{:S(2)}) collective-permute-start(bf16[1024,512]{1,0:T(8,128)(2,1)} %param.28), channel_id=1, source_target_pairs={{0,1},{1,0},{2,3},{3,2},{4,5},{5,4},{6,7},{7,6},{8,9},{9,8},{10,11... | collective-permute-start | bytes 3145736 | tf_op jit(solution)/shard_map/ppermute | solution.py:95
  58.2 3.8 %collective-permute-start = (bf16[4,64,128]{2,1,0:T(8,128)(2,1)S(1)}, bf16[4,64,128]{2,1,0:T(8,128)(2,1)S(1)}, u32[]{:S(2)}, u32[]{:S(2)}) collective-permute-start(bf16[4,64,128]{2,1,0:T(8,128)(2,1)S(1)} %bitcast.140), channel_id=1, source_target_pairs={{0,1},{1,0},{2,3},{3,2},{4,5},{5,4},{6,7},{7,6},{8,9},{9,8},{10,11... | collective-permute-start | bytes 196616 | tf_op jit(solution)/shard_map/ppermute | solution.py:95
  63.1 12.7 %all-to-all-start.2 = ((bf16[4,64,1024]{2,1,0:T(8,128)(2,1)}), bf16[4,64,1024]{2,1,0:T(8,128)(2,1)S(1)}, u32[]{:S(2)}, u32[]{:S(2)}) async-start(bf16[4,64,1024]{2,1,0:T(8,128)(2,1)} %bitcast.26), calls=%async_computation.2 | async-start | bytes 1048576 | tf_op jit(solution)/shard_map/all_to_all | solution.py:90
  66.7 13.9 %copy-start.9 = (bf16[512]{0:T(512)(128)(2,1)S(1)}, bf16[512]{0:T(512)(128)(2,1)}, u32[]{:S(2)}) copy-start(bf16[512]{0:T(512)(128)(2,1)} %param.29) | copy-start | bytes 3076
  66.7 21.9 %copy-start.12 = (bf16[512,1024]{1,0:T(8,128)(2,1)S(1)}, bf16[512,1024]{1,0:T(8,128)(2,1)}, u32[]{:S(2)}) copy-start(bf16[512,1024]{1,0:T(8,128)(2,1)} %param.30) | copy-start | bytes 3145732
  77.1 11.5 %all-to-all-start.3 = ((bf16[4,64,1024]{2,1,0:T(8,128)(2,1)}), bf16[4,64,1024]{2,1,0:T(8,128)(2,1)S(1)}, u32[]{:S(2)}, u32[]{:S(2)}) async-start(bf16[4,64,1024]{2,1,0:T(8,128)(2,1)} %broadcast_in_dim.45), calls=%async_computation.3 | async-start | bytes 1048576 | tf_op jit(solution)/shard_map/all_to_all | solution.py:84
  80.6 3.9 %collective-permute-start.3 = (bf16[512]{0:T(512)(128)(2,1)S(1)}, bf16[512]{0:T(512)(128)(2,1)S(1)}, u32[]{:S(2)}, u32[]{:S(2)}) collective-permute-start(bf16[512]{0:T(512)(128)(2,1)S(1)} %copy-done.9), channel_id=1, source_target_pairs={{0,1},{1,0},{2,3},{3,2},{4,5},{5,4},{6,7},{7,6},{8,9},{9,8},{10,11... | collective-permute-start | bytes 3080 | tf_op jit(solution)/shard_map/ppermute | solution.py:95
  92.8 8.2 %copy-start.7 = (bf16[1024]{0:T(1024)(128)(2,1)S(1)}, bf16[1024]{0:T(1024)(128)(2,1)}, u32[]{:S(2)}) copy-start(bf16[1024]{0:T(1024)(128)(2,1)} %param.31) | copy-start | bytes 6148
  97.4 10.4 %all-to-all-start.4 = ((bf16[4,64,1024]{2,1,0:T(8,128)(2,1)}), bf16[4,64,1024]{2,1,0:T(8,128)(2,1)S(1)}, u32[]{:S(2)}, u32[]{:S(2)}) async-start(bf16[4,64,1024]{2,1,0:T(8,128)(2,1)} %bitcast.30), calls=%async_computation.4 | async-start | bytes 1048576 | tf_op jit(solution)/shard_map/all_to_all | solution.py:90
  108.1 31.3 %copy-start.11 = (s32[64]{0:T(128)S(1)}, s32[64]{0:T(128)}, u32[]{:S(2)}) copy-start(s32[64]{0:T(128)} %param.21) | copy-start | bytes 772
  109.3 29.2 %all-to-all-start.5 = ((bf16[512,1,128]{2,1,0:T(2,128)(2,1)}), bf16[512,1,128]{2,1,0:T(2,128)(2,1)S(1)}, u32[]{:S(2)}, u32[]{:S(2)}) async-start(bf16[512,1,128]{2,1,0:T(2,128)(2,1)} %all_to_all.28), calls=%async_computation.5 | async-start | bytes 524288 | tf_op jit(solution)/shard_map/all_to_all | solution.py:202

commit v8 on v7

--- a/solution.py
+++ b/solution.py
@@ -182,16 +182,22 @@
     ).astype(jnp.bfloat16)
     normed_half = gather_tp(normed, x_count, 0, "x")
 
-    def unit_group(widen_block, bias_block, narrow_block):
-        widened = jnp.dot(normed_half, widen_block, preferred_element_type=jnp.float32)
-        activated = jax.nn.gelu(
-            widened + bias_block.astype(jnp.float32), approximate=False
-        ).astype(jnp.bfloat16)
-        partial = jnp.dot(activated, narrow_block, preferred_element_type=jnp.float32)
+    unit_count = widen_weight.shape[1]
+    widened = jnp.dot(
+        normed_half,
+        jnp.concatenate([widen_weight, partner_widen], axis=1),
+        preferred_element_type=jnp.float32,
+    ) + jnp.concatenate([widen_bias, partner_widen_bias]).astype(jnp.float32)
+    activated = lax.optimization_barrier(
+        jax.nn.gelu(widened, approximate=False).astype(jnp.bfloat16)
+    )
+
+    def unit_group(activated_block, narrow_block):
+        partial = jnp.dot(activated_block, narrow_block, preferred_element_type=jnp.float32)
         return partial.astype(jnp.bfloat16).astype(jnp.float32)
 
-    pair = unit_group(widen_weight, widen_bias, narrow_weight) + unit_group(
-        partner_widen, partner_widen_bias, partner_narrow
+    pair = unit_group(activated[:, :unit_count], narrow_weight) + unit_group(
+        activated[:, unit_count:], partner_narrow
     )
     fed_total = reduce_tp(pair.astype(jnp.bfloat16), x_count, "x")
     updated = layer_norm(

time: 141 us -> 138 us (0.979)
  matrix products: 14.3 us -> 11.8 us
    dot_general x2 -> x3, matrix products: 8.69 us -> 6.13 us  [the longest x1 4.43 us: on_device(): jnp.dot(normed_half, jnp.concatenate([widen_weight, partner_widen], axis=...]
  transfers between devices with their start and end apart: 10 -> 10, of which waited for: 7 -> 6; matrix products, arithmetic and copies ran while one was open for 11% -> 12% of each run, Pallas kernels for 0% -> 0%
where the time goes in v8:
time: 138 us
  waiting for transfers between devices  41.6 us (30%)
  starting transfers between devices  41 us (30%)
  blocking collectives  28.6 us (21%)
  matrix products  11.8 us (9%)
  local copies, waits for them, and re-layouts  7.67 us (6%)
  other arithmetic  4.05 us (3%)
  between operations  3.17 us (2%)
    all_to_all x1, blocking collectives, on_device(): lax.all_to_all(jnp.transpose(routed_in, (1, 0, 2)), 'req', split_axis=1,...  28.6 us
    all_to_all x1, waiting for transfers between devices, on_device(): lax.all_to_all(updated.reshape(rows * tp_count, width // tp_count), ('req...  16.4 us
    all_to_all x2, waiting for transfers between devices, reduce_tp(): lax.all_to_all(partial.reshape(tp_count, rows, -1), names, 0, 0, tiled=True)  15.7 us
    ppermute x5, starting transfers between devices, from_partner(): return lax.ppermute(block, 'core', [(0, 1), (1, 0)])  12.2 us
    all_to_all x1, starting transfers between devices, on_device(): lax.all_to_all(updated.reshape(rows * tp_count, width // tp_count), ('req...  11.6 us
    all_to_all x2, starting transfers between devices, gather_tp(): got = lax.all_to_all(copies, names, axis, axis, tiled=True)  10.1 us
    all_to_all x2, waiting for transfers between devices, gather_tp(): got = lax.all_to_all(copies, names, axis, axis, tiled=True)  8.85 us
    all_to_all x2, starting transfers between devices, reduce_tp(): lax.all_to_all(partial.reshape(tp_count, rows, -1), names, 0, 0, tiled=True)  7.12 us
  transfers between devices with their start and end apart: 10, of which 6 were waited for; matrix products, arithmetic and copies ran while one was open for 12% of the time, Pallas kernels for 0%

profile of v8, /device:TPU:1, one launch (start us, length us, event | category | flops | bytes accessed | tf_op | source)
XLA Modules:
  0.0 137.9 jit_solution(11157739695759337240)
XLA Ops:
  0.6 1.1 fusion.23
  1.9 28.6 %all_to_all.35 = bf16[8,64,128]{2,0,1:T(8,128)(2,1)S(1)} all-to-all(bf16[8,64,128]{2,0,1:T(8,128)(2,1)S(1)} %bitcast.119), channel_id=1, replica_groups=mesh['req'=64,'x'=4,'core'=2] {'req'}, dimensions={1} | all-to-all | bytes 262144 | tf_op jit(solution)/shard_map/all_to_all | solution.py:135
  30.4 1.2 broadcast_in_dim.41
  31.6 6.6 %all-to-all-start.1 = ((bf16[512,8,128]{2,0,1:T(8,128)(2,1)}), bf16[512,8,128]{2,0,1:T(8,128)(2,1)S(1)}, u32[]{:S(2)}, u32[]{:S(2)}) async-start(bf16[512,8,128]{2,0,1:T(8,128)(2,1)} %broadcast_in_dim.41), calls=%async_computation.1 | async-start | bytes 2097152 | tf_op jit(solution)/shard_map/all_to_all | solution.py:84
  38.2 1.9 %collective-permute-start.1 = (bf16[128,1024]{1,0:T(8,128)(2,1)S(1)}, bf16[128,1024]{1,0:T(8,128)(2,1)S(1)}, u32[]{:S(2)}, u32[]{:S(2)}) collective-permute-start(bf16[128,1024]{1,0:T(8,128)(2,1)S(1)} %copy-done.2), channel_id=1, source_target_pairs={{0,1},{1,0},{2,3},{3,2},{4,5},{5,4},{6,7},{7,6},{8,9},{9,8},{10,11... | collective-permute-start | bytes 786440 | tf_op jit(solution)/shard_map/ppermute | solution.py:95
  40.2 2.4 %collective-permute-start.2 = (bf16[1024,512]{1,0:T(8,128)(2,1)}, bf16[1024,512]{1,0:T(8,128)(2,1)}, u32[]{:S(2)}, u32[]{:S(2)}) collective-permute-start(bf16[1024,512]{1,0:T(8,128)(2,1)} %param.28), channel_id=1, source_target_pairs={{0,1},{1,0},{2,3},{3,2},{4,5},{5,4},{6,7},{7,6},{8,9},{9,8},{10,11... | collective-permute-start | bytes 3145736 | tf_op jit(solution)/shard_map/ppermute | solution.py:95
  42.6 0.6 dynamic_slice.21
  45.7 0.6 dynamic_slice.22
  46.3 0.6 iota_compare_fusion.4
  47.3 5.9 %all-to-all-done.1 = bf16[512,8,128]{2,0,1:T(8,128)(2,1)S(1)} async-done(((bf16[512,8,128]{2,0,1:T(8,128)(2,1)}), bf16[512,8,128]{2,0,1:T(8,128)(2,1)S(1)}, u32[]{:S(2)}, u32[]{:S(2)}) %all-to-all-start.1) | async-done | bytes 1048608 | tf_op jit(solution)/shard_map/all_to_all | solution.py:84
  53.2 0.6 fusion.68
  55.7 0.9 fusion.4
  56.6 0.7 fusion.22
  58.3 2.9 %collective-permute-start = (bf16[4,64,128]{2,1,0:T(8,128)(2,1)S(1)}, bf16[4,64,128]{2,1,0:T(8,128)(2,1)S(1)}, u32[]{:S(2)}, u32[]{:S(2)}) collective-permute-start(bf16[4,64,128]{2,1,0:T(8,128)(2,1)S(1)} %bitcast.136), channel_id=1, source_target_pairs={{0,1},{1,0},{2,3},{3,2},{4,5},{5,4},{6,7},{7,6},{8,9},{9,8},{10,11... | collective-permute-start | bytes 196616 | tf_op jit(solution)/shard_map/ppermute | solution.py:95
  62.0 1.1 fusion.17
  63.1 3.5 %all-to-all-start.2 = ((bf16[4,64,1024]{2,1,0:T(8,128)(2,1)}), bf16[4,64,1024]{2,1,0:T(8,128)(2,1)S(1)}, u32[]{:S(2)}, u32[]{:S(2)}) async-start(bf16[4,64,1024]{2,1,0:T(8,128)(2,1)} %bitcast.26), calls=%async_computation.2 | async-start | bytes 1048576 | tf_op jit(solution)/shard_map/all_to_all | solution.py:90
  66.8 9.0 %all-to-all-done.2 = bf16[4,64,1024]{2,1,0:T(8,128)(2,1)S(1)} async-done(((bf16[4,64,1024]{2,1,0:T(8,128)(2,1)}), bf16[4,64,1024]{2,1,0:T(8,128)(2,1)S(1)}, u32[]{:S(2)}, u32[]{:S(2)}) %all-to-all-start.2) | async-done | bytes 524320 | tf_op jit(solution)/shard_map/all_to_all | solution.py:90
  76.3 0.9 broadcast_in_dim.45
  77.2 3.5 %all-to-all-start.3 = ((bf16[4,64,1024]{2,1,0:T(8,128)(2,1)}), bf16[4,64,1024]{2,1,0:T(8,128)(2,1)S(1)}, u32[]{:S(2)}, u32[]{:S(2)}) async-start(bf16[4,64,1024]{2,1,0:T(8,128)(2,1)} %broadcast_in_dim.45), calls=%async_computation.3 | async-start | bytes 1048576 | tf_op jit(solution)/shard_map/all_to_all | solution.py:84
  80.7 3.1 %collective-permute-start.3 = (bf16[512]{0:T(512)(128)(2,1)S(1)}, bf16[512]{0:T(512)(128)(2,1)S(1)}, u32[]{:S(2)}, u32[]{:S(2)}) collective-permute-start(bf16[512]{0:T(512)(128)(2,1)S(1)} %copy-done.10), channel_id=1, source_target_pairs={{0,1},{1,0},{2,3},{3,2},{4,5},{5,4},{6,7},{7,6},{8,9},{9,8},{10,11... | collective-permute-start | bytes 3080 | tf_op jit(solution)/shard_map/ppermute | solution.py:95
  83.8 1.9 %collective-permute-start.4 = (bf16[512,1024]{1,0:T(8,128)(2,1)S(1)}, bf16[512,1024]{1,0:T(8,128)(2,1)S(1)}, u32[]{:S(2)}, u32[]{:S(2)}) collective-permute-start(bf16[512,1024]{1,0:T(8,128)(2,1)S(1)} %copy-done), channel_id=1, source_target_pairs={{0,1},{1,0},{2,3},{3,2},{4,5},{5,4},{6,7},{7,6},{8,9},{9,8},{10,11... | collective-permute-start | bytes 3145736 | tf_op jit(solution)/shard_map/ppermute | solution.py:95
  85.8 2.9 %all-to-all-done.3 = bf16[4,64,1024]{2,1,0:T(8,128)(2,1)S(1)} async-done(((bf16[4,64,1024]{2,1,0:T(8,128)(2,1)}), bf16[4,64,1024]{2,1,0:T(8,128)(2,1)S(1)}, u32[]{:S(2)}, u32[]{:S(2)}) %all-to-all-start.3) | async-done | bytes 524320 | tf_op jit(solution)/shard_map/all_to_all | solution.py:84
  88.7 4.4 %fusion.27 = bf16[256,1024]{1,0:T(8,128)(2,1)S(1)} fusion(bf16[256,1024]{1,0:T(8,128)(2,1)S(1)} %bitcast.118, bf16[1024,512]{1,0:T(8,128)(2,1)} %collective-permute-done.2, bf16[1024,512]{1,0:T(8,128)(2,1)} %param.28, f32[1024]{0:T(1024)S(1)} %maximum_convert_fusion), kind=kOutput, calls=%fused_computation.38 | convolution fusion | flops 558366720 | bytes 3149824 | tf_op jit(solution)/shard_map/dot_general | solution.py:186
  93.6 1.3 fusion.14
  94.9 3.6 %all-to-all-start.4 = ((bf16[4,64,1024]{2,1,0:T(8,128)(2,1)}), bf16[4,64,1024]{2,1,0:T(8,128)(2,1)S(1)}, u32[]{:S(2)}, u32[]{:S(2)}) async-start(bf16[4,64,1024]{2,1,0:T(8,128)(2,1)} %bitcast.30), calls=%async_computation.4 | async-start | bytes 1048576 | tf_op jit(solution)/shard_map/all_to_all | solution.py:90
  98.6 6.7 %all-to-all-done.4 = bf16[4,64,1024]{2,1,0:T(8,128)(2,1)S(1)} async-done(((bf16[4,64,1024]{2,1,0:T(8,128)(2,1)}), bf16[4,64,1024]{2,1,0:T(8,128)(2,1)S(1)}, u32[]{:S(2)}, u32[]{:S(2)}) %all-to-all-start.4) | async-done | bytes 524320 | tf_op jit(solution)/shard_map/all_to_all | solution.py:90
  106.1 0.8 all_to_all.28
  106.9 11.6 %all-to-all-start.5 = ((bf16[512,1,128]{2,1,0:T(2,128)(2,1)}), bf16[512,1,128]{2,1,0:T(2,128)(2,1)S(1)}, u32[]{:S(2)}, u32[]{:S(2)}) async-start(bf16[512,1,128]{2,1,0:T(2,128)(2,1)} %all_to_all.28), calls=%async_computation.5 | async-start | bytes 524288 | tf_op jit(solution)/shard_map/all_to_all | solution.py:208
  118.8 0.9 copy.86
  119.7 16.4 %all-to-all-done.5 = bf16[512,1,128]{2,1,0:T(2,128)(2,1)S(1)} async-done(((bf16[512,1,128]{2,1,0:T(2,128)(2,1)}), bf16[512,1,128]{2,1,0:T(2,128)(2,1)S(1)}, u32[]{:S(2)}, u32[]{:S(2)}) %all-to-all-start.5) | async-done | bytes 131104 | tf_op jit(solution)/shard_map/all_to_all | solution.py:208
  136.1 0.8 reduce
  137.2 0.7 copy.78
  (79 shorter events, 7.1 us)
Async XLA Ops:
  1.8 36.5 %copy-start.2 = (bf16[128,1024]{1,0:T(8,128)(2,1)S(1)}, bf16[128,1024]{1,0:T(8,128)(2,1)}, u32[]{:S(2)}) copy-start(bf16[128,1024]{1,0:T(8,128)(2,1)} %param.24) | copy-start | bytes 786436
  1.8 40.8 %copy-start.11 = (s32[64]{0:T(128)S(1)}, s32[64]{0:T(128)}, u32[]{:S(2)}) copy-start(s32[64]{0:T(128)} %param.20) | copy-start | bytes 772
  1.8 42.7 %copy-start.7 = (bf16[1024]{0:T(1024)(128)(2,1)S(1)}, bf16[1024]{0:T(1024)(128)(2,1)}, u32[]{:S(2)}) copy-start(bf16[1024]{0:T(1024)(128)(2,1)} %param.25) | copy-start | bytes 6148
  1.8 42.7 %copy-start.3 = (bf16[1,512,128]{2,1,0:T(8,128)(2,1)S(1)}, bf16[1,512,128]{2,1,0:T(8,128)(2,1)}, u32[]{:S(2)}) copy-start(bf16[1,512,128]{2,1,0:T(8,128)(2,1)} %param.18) | copy-start | bytes 393220
  1.9 42.8 %copy-start.1 = (bf16[3,1024,128]{2,1,0:T(8,128)(2,1)S(1)}, bf16[3,1024,128]{2,1,0:T(8,128)(2,1)}, u32[]{:S(2)}) copy-start(bf16[3,1024,128]{2,1,0:T(8,128)(2,1)} %param.22) | copy-start | bytes 2359300
  31.6 13.3 %copy-start.9 = (bf16[3,128]{1,0:T(4,128)(2,1)S(1)}, bf16[3,128]{1,0:T(4,128)(2,1)}, u32[]{:S(2)}) copy-start(bf16[3,128]{1,0:T(4,128)(2,1)} %param.23) | copy-start | bytes 2308
  31.6 13.3 %copy-start.4 = (bf16[1,512,128]{2,1,0:T(8,128)(2,1)S(1)}, bf16[1,512,128]{2,1,0:T(8,128)(2,1)}, u32[]{:S(2)}) copy-start(bf16[1,512,128]{2,1,0:T(8,128)(2,1)} %param.17) | copy-start | bytes 393220
  31.6 14.1 %copy-start.13 = (s32[64]{0:T(128)S(1)}, s32[64]{0:T(128)}, u32[]{:S(2)}) copy-start(s32[64]{0:T(128)} %param.19) | copy-start | bytes 772
  31.6 15.4 %copy-start.5 = (bf16[2,1024]{1,0:T(2,128)(2,1)S(1)}, bf16[2,1024]{1,0:T(2,128)(2,1)}, u32[]{:S(2)}) copy-start(bf16[2,1024]{1,0:T(2,128)(2,1)} %param.27) | copy-start | bytes 12292
  31.6 15.4 %copy-start.6 = (bf16[2,1024]{1,0:T(2,128)(2,1)S(1)}, bf16[2,1024]{1,0:T(2,128)(2,1)}, u32[]{:S(2)}) copy-start(bf16[2,1024]{1,0:T(2,128)(2,1)} %param.26) | copy-start | bytes 12292
  31.6 21.6 %all-to-all-start.1 = ((bf16[512,8,128]{2,0,1:T(8,128)(2,1)}), bf16[512,8,128]{2,0,1:T(8,128)(2,1)S(1)}, u32[]{:S(2)}, u32[]{:S(2)}) async-start(bf16[512,8,128]{2,0,1:T(8,128)(2,1)} %broadcast_in_dim.41), calls=%async_computation.1 | async-start | bytes 2097152 | tf_op jit(solution)/shard_map/all_to_all | solution.py:84
  38.2 23.2 %collective-permute-start.1 = (bf16[128,1024]{1,0:T(8,128)(2,1)S(1)}, bf16[128,1024]{1,0:T(8,128)(2,1)S(1)}, u32[]{:S(2)}, u32[]{:S(2)}) collective-permute-start(bf16[128,1024]{1,0:T(8,128)(2,1)S(1)} %copy-done.2), channel_id=1, source_target_pairs={{0,1},{1,0},{2,3},{3,2},{4,5},{5,4},{6,7},{7,6},{8,9},{9,8},{10,11... | collective-permute-start | bytes 786440 | tf_op jit(solution)/shard_map/ppermute | solution.py:95
  40.2 45.6 %collective-permute-start.2 = (bf16[1024,512]{1,0:T(8,128)(2,1)}, bf16[1024,512]{1,0:T(8,128)(2,1)}, u32[]{:S(2)}, u32[]{:S(2)}) collective-permute-start(bf16[1024,512]{1,0:T(8,128)(2,1)} %param.28), channel_id=1, source_target_pairs={{0,1},{1,0},{2,3},{3,2},{4,5},{5,4},{6,7},{7,6},{8,9},{9,8},{10,11... | collective-permute-start | bytes 3145736 | tf_op jit(solution)/shard_map/ppermute | solution.py:95
  58.3 3.8 %collective-permute-start = (bf16[4,64,128]{2,1,0:T(8,128)(2,1)S(1)}, bf16[4,64,128]{2,1,0:T(8,128)(2,1)S(1)}, u32[]{:S(2)}, u32[]{:S(2)}) collective-permute-start(bf16[4,64,128]{2,1,0:T(8,128)(2,1)S(1)} %bitcast.136), channel_id=1, source_target_pairs={{0,1},{1,0},{2,3},{3,2},{4,5},{5,4},{6,7},{7,6},{8,9},{9,8},{10,11... | collective-permute-start | bytes 196616 | tf_op jit(solution)/shard_map/ppermute | solution.py:95
  63.1 12.7 %all-to-all-start.2 = ((bf16[4,64,1024]{2,1,0:T(8,128)(2,1)}), bf16[4,64,1024]{2,1,0:T(8,128)(2,1)S(1)}, u32[]{:S(2)}, u32[]{:S(2)}) async-start(bf16[4,64,1024]{2,1,0:T(8,128)(2,1)} %bitcast.26), calls=%async_computation.2 | async-start | bytes 1048576 | tf_op jit(solution)/shard_map/all_to_all | solution.py:90
  66.8 13.9 %copy-start.10 = (bf16[512]{0:T(512)(128)(2,1)S(1)}, bf16[512]{0:T(512)(128)(2,1)}, u32[]{:S(2)}) copy-start(bf16[512]{0:T(512)(128)(2,1)} %param.29) | copy-start | bytes 3076
  66.8 17.1 %copy-start = (bf16[512,1024]{1,0:T(8,128)(2,1)S(1)}, bf16[512,1024]{1,0:T(8,128)(2,1)}, u32[]{:S(2)}) copy-start(bf16[512,1024]{1,0:T(8,128)(2,1)} %param.30) | copy-start | bytes 3145732
  77.2 11.5 %all-to-all-start.3 = ((bf16[4,64,1024]{2,1,0:T(8,128)(2,1)}), bf16[4,64,1024]{2,1,0:T(8,128)(2,1)S(1)}, u32[]{:S(2)}, u32[]{:S(2)}) async-start(bf16[4,64,1024]{2,1,0:T(8,128)(2,1)} %broadcast_in_dim.45), calls=%async_computation.3 | async-start | bytes 1048576 | tf_op jit(solution)/shard_map/all_to_all | solution.py:84
  80.7 5.1 %collective-permute-start.3 = (bf16[512]{0:T(512)(128)(2,1)S(1)}, bf16[512]{0:T(512)(128)(2,1)S(1)}, u32[]{:S(2)}, u32[]{:S(2)}) collective-permute-start(bf16[512]{0:T(512)(128)(2,1)S(1)} %copy-done.10), channel_id=1, source_target_pairs={{0,1},{1,0},{2,3},{3,2},{4,5},{5,4},{6,7},{7,6},{8,9},{9,8},{10,11... | collective-permute-start | bytes 3080 | tf_op jit(solution)/shard_map/ppermute | solution.py:95
  83.8 9.8 %collective-permute-start.4 = (bf16[512,1024]{1,0:T(8,128)(2,1)S(1)}, bf16[512,1024]{1,0:T(8,128)(2,1)S(1)}, u32[]{:S(2)}, u32[]{:S(2)}) collective-permute-start(bf16[512,1024]{1,0:T(8,128)(2,1)S(1)} %copy-done), channel_id=1, source_target_pairs={{0,1},{1,0},{2,3},{3,2},{4,5},{5,4},{6,7},{7,6},{8,9},{9,8},{10,11... | collective-permute-start | bytes 3145736 | tf_op jit(solution)/shard_map/ppermute | solution.py:95
  93.6 4.9 %copy-start.8 = (bf16[1024]{0:T(1024)(128)(2,1)S(1)}, bf16[1024]{0:T(1024)(128)(2,1)}, u32[]{:S(2)}) copy-start(bf16[1024]{0:T(1024)(128)(2,1)} %param.31) | copy-start | bytes 6148
  94.9 10.4 %all-to-all-start.4 = ((bf16[4,64,1024]{2,1,0:T(8,128)(2,1)}), bf16[4,64,1024]{2,1,0:T(8,128)(2,1)S(1)}, u32[]{:S(2)}, u32[]{:S(2)}) async-start(bf16[4,64,1024]{2,1,0:T(8,128)(2,1)} %bitcast.30), calls=%async_computation.4 | async-start | bytes 1048576 | tf_op jit(solution)/shard_map/all_to_all | solution.py:90
  105.6 31.3 %copy-start.12 = (s32[64]{0:T(128)S(1)}, s32[64]{0:T(128)}, u32[]{:S(2)}) copy-start(s32[64]{0:T(128)} %param.21) | copy-start | bytes 772
  106.9 29.2 %all-to-all-start.5 = ((bf16[512,1,128]{2,1,0:T(2,128)(2,1)}), bf16[512,1,128]{2,1,0:T(2,128)(2,1)S(1)}, u32[]{:S(2)}, u32[]{:S(2)}) async-start(bf16[512,1,128]{2,1,0:T(2,128)(2,1)} %all_to_all.28), calls=%async_computation.5 | async-start | bytes 524288 | tf_op jit(solution)/shard_map/all_to_all | solution.py:208

commit v9 on v8

--- a/solution.py
+++ b/solution.py
@@ -175,13 +175,18 @@
         x_count,
         "x",
     )
-    normed = layer_norm(
-        own_rows + attended,
-        norm_gains[0],
-        norm_biases[0],
+    pre_norm = own_rows + attended
+    average = jnp.mean(pre_norm, axis=-1, keepdims=True)
+    centred = pre_norm - average
+    spread = jnp.mean(centred * centred, axis=-1, keepdims=True)
+    normed_copies = (
+        jnp.broadcast_to(centred[None], (x_count,) + centred.shape)
+        * lax.rsqrt(spread + 1e-05)
+        * norm_gains[0].astype(jnp.float32)
+        + norm_biases[0].astype(jnp.float32)
     ).astype(jnp.bfloat16)
-    normed_half = gather_tp(normed, x_count, 0, "x")
-
+    normed = normed_copies[0]
+    normed_half = lax.all_to_all(normed_copies, "x", 0, 0, tiled=True).reshape(-1, width)
     unit_count = widen_weight.shape[1]
     widened = jnp.dot(
         normed_half,
@@ -212,7 +217,7 @@
         0,
         tiled=True,
     ).reshape(-1, tp_count, width // tp_count)
-    hidden_out = permute_rows(request_slot, returned)
+    hidden_out = returned.at[request_slot].get(mode="promise_in_bounds", unique_indices=True)
     return (hidden_out, new_cache)
 
 

time: 138 us -> 142 us (1.029)
  other arithmetic: 4.05 us -> 9.18 us
    all_to_all x2 -> x1, starting transfers between devices: 10.1 us -> 6.6 us  [gather_tp(): got = lax.all_to_all(copies, names, axis, axis, tiled=True)]
    all_to_all x0 -> x1, starting transfers between devices: none -> 3.47 us  [on_device(): lax.all_to_all(normed_copies, 'x', 0, 0, tiled=True).reshape(-1, width)]
    all_to_all x0 -> x1, waiting for transfers between devices: none -> 2.93 us  [on_device(): lax.all_to_all(normed_copies, 'x', 0, 0, tiled=True).reshape(-1, width)]
    all_to_all x2 -> x1, waiting for transfers between devices: 8.85 us -> 5.93 us  [gather_tp(): got = lax.all_to_all(copies, names, axis, axis, tiled=True)]
    convert_element_type x1, other arithmetic: 0.18 us -> 2.64 us  [on_device(): updated = layer_norm(normed.astype(jnp.float32) + fed_total + narrow_bias...]
    convert_element_type x1 -> x4, other arithmetic: 0.12 us -> 1.9 us  [the longest x1 0.96 us: on_device(): normed_copies = (jnp.broadcast_to(centred[None], (x_count,) + centred.sha...]
  transfers between devices with their start and end apart: 10 -> 10, of which waited for: 6 -> 6; matrix products, arithmetic and copies ran while one was open for 12% -> 13% of each run, Pallas kernels for 0% -> 0%
where the time goes in v9:
time: 142 us
  starting transfers between devices  41.1 us (29%)
  waiting for transfers between devices  40.3 us (28%)
  blocking collectives  28.6 us (20%)
  matrix products  11.6 us (8%)
  other arithmetic  9.18 us (6%)
  local copies, waits for them, and re-layouts  7.57 us (5%)
  between operations  3.22 us (2%)
    all_to_all x1, blocking collectives, on_device(): lax.all_to_all(jnp.transpose(routed_in, (1, 0, 2)), 'req', split_axis=1,...  28.6 us
    all_to_all x1, waiting for transfers between devices, on_device(): lax.all_to_all(updated.reshape(rows * tp_count, width // tp_count), ('req...  16.4 us
    all_to_all x2, waiting for transfers between devices, reduce_tp(): lax.all_to_all(partial.reshape(tp_count, rows, -1), names, 0, 0, tiled=True)  14.4 us
    ppermute x5, starting transfers between devices, from_partner(): return lax.ppermute(block, 'core', [(0, 1), (1, 0)])  12.2 us
    all_to_all x1, starting transfers between devices, on_device(): lax.all_to_all(updated.reshape(rows * tp_count, width // tp_count), ('req...  11.7 us
    all_to_all x2, starting transfers between devices, reduce_tp(): lax.all_to_all(partial.reshape(tp_count, rows, -1), names, 0, 0, tiled=True)  7.12 us
    all_to_all x1, starting transfers between devices, gather_tp(): got = lax.all_to_all(copies, names, axis, axis, tiled=True)  6.6 us
    all_to_all x1, waiting for transfers between devices, gather_tp(): got = lax.all_to_all(copies, names, axis, axis, tiled=True)  5.93 us
  transfers between devices with their start and end apart: 10, of which 6 were waited for; matrix products, arithmetic and copies ran while one was open for 13% of the time, Pallas kernels for 0%

profile of v9, /device:TPU:1, one launch (start us, length us, event | category | flops | bytes accessed | tf_op | source)
XLA Modules:
  0.0 141.5 jit_solution(12398605318920637968)
XLA Ops:
  0.6 1.1 fusion.23
  1.8 28.6 %all_to_all.31 = bf16[8,64,128]{2,0,1:T(8,128)(2,1)S(1)} all-to-all(bf16[8,64,128]{2,0,1:T(8,128)(2,1)S(1)} %bitcast.135), channel_id=1, replica_groups=mesh['req'=64,'x'=4,'core'=2] {'req'}, dimensions={1} | all-to-all | bytes 262144 | tf_op jit(solution)/shard_map/all_to_all | solution.py:135
  30.4 1.2 broadcast_in_dim.43
  31.6 6.6 %all-to-all-start.1 = ((bf16[512,8,128]{2,0,1:T(8,128)(2,1)}), bf16[512,8,128]{2,0,1:T(8,128)(2,1)S(1)}, u32[]{:S(2)}, u32[]{:S(2)}) async-start(bf16[512,8,128]{2,0,1:T(8,128)(2,1)} %broadcast_in_dim.43), calls=%async_computation.1 | async-start | bytes 2097152 | tf_op jit(solution)/shard_map/all_to_all | solution.py:84
  38.2 1.9 %collective-permute-start.1 = (bf16[128,1024]{1,0:T(8,128)(2,1)S(1)}, bf16[128,1024]{1,0:T(8,128)(2,1)S(1)}, u32[]{:S(2)}, u32[]{:S(2)}) collective-permute-start(bf16[128,1024]{1,0:T(8,128)(2,1)S(1)} %copy-done.2), channel_id=1, source_target_pairs={{0,1},{1,0},{2,3},{3,2},{4,5},{5,4},{6,7},{7,6},{8,9},{9,8},{10,11... | collective-permute-start | bytes 786440 | tf_op jit(solution)/shard_map/ppermute | solution.py:95
  40.2 2.4 %collective-permute-start.2 = (bf16[1024,512]{1,0:T(8,128)(2,1)}, bf16[1024,512]{1,0:T(8,128)(2,1)}, u32[]{:S(2)}, u32[]{:S(2)}) collective-permute-start(bf16[1024,512]{1,0:T(8,128)(2,1)} %param.28), channel_id=1, source_target_pairs={{0,1},{1,0},{2,3},{3,2},{4,5},{5,4},{6,7},{7,6},{8,9},{9,8},{10,11... | collective-permute-start | bytes 3145736 | tf_op jit(solution)/shard_map/ppermute | solution.py:95
  46.3 0.6 iota_compare_fusion.2
  47.3 5.9 %all-to-all-done.1 = bf16[512,8,128]{2,0,1:T(8,128)(2,1)S(1)} async-done(((bf16[512,8,128]{2,0,1:T(8,128)(2,1)}), bf16[512,8,128]{2,0,1:T(8,128)(2,1)S(1)}, u32[]{:S(2)}, u32[]{:S(2)}) %all-to-all-start.1) | async-done | bytes 1048608 | tf_op jit(solution)/shard_map/all_to_all | solution.py:84
  53.2 0.6 fusion.67
  55.1 0.9 fusion.4
  56.6 0.7 fusion.22
  58.3 2.9 %collective-permute-start = (bf16[4,64,128]{2,1,0:T(8,128)(2,1)S(1)}, bf16[4,64,128]{2,1,0:T(8,128)(2,1)S(1)}, u32[]{:S(2)}, u32[]{:S(2)}) collective-permute-start(bf16[4,64,128]{2,1,0:T(8,128)(2,1)S(1)} %bitcast.143), channel_id=1, source_target_pairs={{0,1},{1,0},{2,3},{3,2},{4,5},{5,4},{6,7},{7,6},{8,9},{9,8},{10,11... | collective-permute-start | bytes 196616 | tf_op jit(solution)/shard_map/ppermute | solution.py:95
  62.0 1.1 fusion.17
  63.2 3.5 %all-to-all-start.2 = ((bf16[4,64,1024]{2,1,0:T(8,128)(2,1)}), bf16[4,64,1024]{2,1,0:T(8,128)(2,1)S(1)}, u32[]{:S(2)}, u32[]{:S(2)}) async-start(bf16[4,64,1024]{2,1,0:T(8,128)(2,1)} %bitcast.26), calls=%async_computation.2 | async-start | bytes 1048576 | tf_op jit(solution)/shard_map/all_to_all | solution.py:90
  66.9 9.0 %all-to-all-done.2 = bf16[4,64,1024]{2,1,0:T(8,128)(2,1)S(1)} async-done(((bf16[4,64,1024]{2,1,0:T(8,128)(2,1)}), bf16[4,64,1024]{2,1,0:T(8,128)(2,1)S(1)}, u32[]{:S(2)}, u32[]{:S(2)}) %all-to-all-start.2) | async-done | bytes 524320 | tf_op jit(solution)/shard_map/all_to_all | solution.py:90
  76.3 1.0 add_convert_fusion
  77.2 3.5 %all-to-all-start.3 = ((bf16[4,64,1024]{2,1,0:T(8,128)(2,1)}), bf16[4,64,1024]{2,1,0:T(8,128)(2,1)S(1)}, u32[]{:S(2)}, u32[]{:S(2)}) async-start(bf16[4,64,1024]{2,1,0:T(8,128)(2,1)} %add_convert_fusion), calls=%async_computation.3 | async-start | bytes 1048576 | tf_op jit(solution)/shard_map/all_to_all | solution.py:189
  80.7 3.1 %collective-permute-start.3 = (bf16[512]{0:T(512)(128)(2,1)S(1)}, bf16[512]{0:T(512)(128)(2,1)S(1)}, u32[]{:S(2)}, u32[]{:S(2)}) collective-permute-start(bf16[512]{0:T(512)(128)(2,1)S(1)} %copy-done.10), channel_id=1, source_target_pairs={{0,1},{1,0},{2,3},{3,2},{4,5},{5,4},{6,7},{7,6},{8,9},{9,8},{10,11... | collective-permute-start | bytes 3080 | tf_op jit(solution)/shard_map/ppermute | solution.py:95
  83.8 1.9 %collective-permute-start.4 = (bf16[512,1024]{1,0:T(8,128)(2,1)S(1)}, bf16[512,1024]{1,0:T(8,128)(2,1)S(1)}, u32[]{:S(2)}, u32[]{:S(2)}) collective-permute-start(bf16[512,1024]{1,0:T(8,128)(2,1)S(1)} %copy-done), channel_id=1, source_target_pairs={{0,1},{1,0},{2,3},{3,2},{4,5},{5,4},{6,7},{7,6},{8,9},{9,8},{10,11... | collective-permute-start | bytes 3145736 | tf_op jit(solution)/shard_map/ppermute | solution.py:95
  85.8 2.9 %all-to-all-done.3 = bf16[4,64,1024]{2,1,0:T(8,128)(2,1)S(1)} async-done(((bf16[4,64,1024]{2,1,0:T(8,128)(2,1)}), bf16[4,64,1024]{2,1,0:T(8,128)(2,1)S(1)}, u32[]{:S(2)}, u32[]{:S(2)}) %all-to-all-start.3) | async-done | bytes 524320 | tf_op jit(solution)/shard_map/all_to_all | solution.py:189
  88.7 4.4 %fusion.26 = bf16[256,1024]{1,0:T(8,128)(2,1)S(1)} fusion(bf16[256,1024]{1,0:T(8,128)(2,1)S(1)} %bitcast.134, bf16[1024,512]{1,0:T(8,128)(2,1)} %collective-permute-done.2, bf16[1024,512]{1,0:T(8,128)(2,1)} %param.28, f32[1024]{0:T(1024)S(1)} %maximum_convert_fusion), kind=kOutput, calls=%fused_computation.37 | convolution fusion | flops 558366720 | bytes 3149824 | tf_op jit(solution)/shard_map/dot_general | solution.py:191
  93.6 1.3 fusion.14
  94.9 3.6 %all-to-all-start.4 = ((bf16[4,64,1024]{2,1,0:T(8,128)(2,1)}), bf16[4,64,1024]{2,1,0:T(8,128)(2,1)S(1)}, u32[]{:S(2)}, u32[]{:S(2)}) async-start(bf16[4,64,1024]{2,1,0:T(8,128)(2,1)} %bitcast.30), calls=%async_computation.4 | async-start | bytes 1048576 | tf_op jit(solution)/shard_map/all_to_all | solution.py:90
  98.6 0.9 slice_convert_fusion.2
  99.8 5.5 %all-to-all-done.4 = bf16[4,64,1024]{2,1,0:T(8,128)(2,1)S(1)} async-done(((bf16[4,64,1024]{2,1,0:T(8,128)(2,1)}), bf16[4,64,1024]{2,1,0:T(8,128)(2,1)S(1)}, u32[]{:S(2)}, u32[]{:S(2)}) %all-to-all-start.4) | async-done | bytes 524320 | tf_op jit(solution)/shard_map/all_to_all | solution.py:90
  105.7 1.0 fusion.50
  106.8 1.1 multiply_reduce_fusion
  108.3 2.6 %add_convert_fusion.1 = bf16[512,1,128]{2,1,0:T(2,128)(2,1)} fusion(f32[512,1,128]{2,1,0:T(1,128)S(1)} %bitcast.128, f32[512,1,128]{2,1,0:T(1,128)S(1)} %bitcast.127, f32[512,1,128]{2,1,0:T(1,128)S(1)} %bitcast.126, f32[512,1,128]{2,1,0:T(1,128)S(1)} %reshape.395, f32[512,1,128]{2,1,0:T(1,128)S(1)} %reduce_sum.87, f32[512]{0:T(512)S(1)} %mul.157, f32[512]{0:T(512)S(1)} %sub.87), kind=kLoop, calls=%fused_computation.75 | loop fusion | flops 458752 | bytes 1445888 | tf_op jit(solution)/shard_map/convert_element_type | solution.py:212
  111.0 11.7 %all-to-all-start.5 = ((bf16[512,1,128]{2,1,0:T(2,128)(2,1)}), bf16[512,1,128]{2,1,0:T(2,128)(2,1)S(1)}, u32[]{:S(2)}, u32[]{:S(2)}) async-start(bf16[512,1,128]{2,1,0:T(2,128)(2,1)} %add_convert_fusion.1), calls=%async_computation.5 | async-start | bytes 524288 | tf_op jit(solution)/shard_map/all_to_all | solution.py:213
  122.9 0.9 copy.85
  123.8 16.4 %all-to-all-done.5 = bf16[512,1,128]{2,1,0:T(2,128)(2,1)S(1)} async-done(((bf16[512,1,128]{2,1,0:T(2,128)(2,1)}), bf16[512,1,128]{2,1,0:T(2,128)(2,1)S(1)}, u32[]{:S(2)}, u32[]{:S(2)}) %all-to-all-start.5) | async-done | bytes 131104 | tf_op jit(solution)/shard_map/all_to_all | solution.py:213
  140.2 1.3 gather_fusion
  (87 shorter events, 8.2 us)
Async XLA Ops:
  1.8 36.5 %copy-start.2 = (bf16[128,1024]{1,0:T(8,128)(2,1)S(1)}, bf16[128,1024]{1,0:T(8,128)(2,1)}, u32[]{:S(2)}) copy-start(bf16[128,1024]{1,0:T(8,128)(2,1)} %param.24) | copy-start | bytes 786436
  1.8 40.8 %copy-start.11 = (s32[64]{0:T(128)S(1)}, s32[64]{0:T(128)}, u32[]{:S(2)}) copy-start(s32[64]{0:T(128)} %param.20) | copy-start | bytes 772
  1.8 42.7 %copy-start.1 = (bf16[3,1024,128]{2,1,0:T(8,128)(2,1)S(1)}, bf16[3,1024,128]{2,1,0:T(8,128)(2,1)}, u32[]{:S(2)}) copy-start(bf16[3,1024,128]{2,1,0:T(8,128)(2,1)} %param.22) | copy-start | bytes 2359300
  31.6 13.2 %copy-start.9 = (bf16[3,128]{1,0:T(4,128)(2,1)S(1)}, bf16[3,128]{1,0:T(4,128)(2,1)}, u32[]{:S(2)}) copy-start(bf16[3,128]{1,0:T(4,128)(2,1)} %param.23) | copy-start | bytes 2308
  31.6 13.2 %copy-start.3 = (bf16[1,512,128]{2,1,0:T(8,128)(2,1)S(1)}, bf16[1,512,128]{2,1,0:T(8,128)(2,1)}, u32[]{:S(2)}) copy-start(bf16[1,512,128]{2,1,0:T(8,128)(2,1)} %param.17) | copy-start | bytes 393220
  31.6 13.3 %copy-start.4 = (bf16[1,512,128]{2,1,0:T(8,128)(2,1)S(1)}, bf16[1,512,128]{2,1,0:T(8,128)(2,1)}, u32[]{:S(2)}) copy-start(bf16[1,512,128]{2,1,0:T(8,128)(2,1)} %param.18) | copy-start | bytes 393220
  31.6 13.5 %copy-start.7 = (bf16[1024]{0:T(1024)(128)(2,1)S(1)}, bf16[1024]{0:T(1024)(128)(2,1)}, u32[]{:S(2)}) copy-start(bf16[1024]{0:T(1024)(128)(2,1)} %param.25) | copy-start | bytes 6148
  31.6 14.1 %copy-start.12 = (s32[64]{0:T(128)S(1)}, s32[64]{0:T(128)}, u32[]{:S(2)}) copy-start(s32[64]{0:T(128)} %param.19) | copy-start | bytes 772
  31.6 15.4 %copy-start.5 = (bf16[2,1024]{1,0:T(2,128)(2,1)S(1)}, bf16[2,1024]{1,0:T(2,128)(2,1)}, u32[]{:S(2)}) copy-start(bf16[2,1024]{1,0:T(2,128)(2,1)} %param.26) | copy-start | bytes 12292
  31.6 15.4 %copy-start.6 = (bf16[2,1024]{1,0:T(2,128)(2,1)S(1)}, bf16[2,1024]{1,0:T(2,128)(2,1)}, u32[]{:S(2)}) copy-start(bf16[2,1024]{1,0:T(2,128)(2,1)} %param.27) | copy-start | bytes 12292
  31.6 21.6 %all-to-all-start.1 = ((bf16[512,8,128]{2,0,1:T(8,128)(2,1)}), bf16[512,8,128]{2,0,1:T(8,128)(2,1)S(1)}, u32[]{:S(2)}, u32[]{:S(2)}) async-start(bf16[512,8,128]{2,0,1:T(8,128)(2,1)} %broadcast_in_dim.43), calls=%async_computation.1 | async-start | bytes 2097152 | tf_op jit(solution)/shard_map/all_to_all | solution.py:84
  38.2 23.2 %collective-permute-start.1 = (bf16[128,1024]{1,0:T(8,128)(2,1)S(1)}, bf16[128,1024]{1,0:T(8,128)(2,1)S(1)}, u32[]{:S(2)}, u32[]{:S(2)}) collective-permute-start(bf16[128,1024]{1,0:T(8,128)(2,1)S(1)} %copy-done.2), channel_id=1, source_target_pairs={{0,1},{1,0},{2,3},{3,2},{4,5},{5,4},{6,7},{7,6},{8,9},{9,8},{10,11... | collective-permute-start | bytes 786440 | tf_op jit(solution)/shard_map/ppermute | solution.py:95
  40.2 45.6 %collective-permute-start.2 = (bf16[1024,512]{1,0:T(8,128)(2,1)}, bf16[1024,512]{1,0:T(8,128)(2,1)}, u32[]{:S(2)}, u32[]{:S(2)}) collective-permute-start(bf16[1024,512]{1,0:T(8,128)(2,1)} %param.28), channel_id=1, source_target_pairs={{0,1},{1,0},{2,3},{3,2},{4,5},{5,4},{6,7},{7,6},{8,9},{9,8},{10,11... | collective-permute-start | bytes 3145736 | tf_op jit(solution)/shard_map/ppermute | solution.py:95
  58.3 3.8 %collective-permute-start = (bf16[4,64,128]{2,1,0:T(8,128)(2,1)S(1)}, bf16[4,64,128]{2,1,0:T(8,128)(2,1)S(1)}, u32[]{:S(2)}, u32[]{:S(2)}) collective-permute-start(bf16[4,64,128]{2,1,0:T(8,128)(2,1)S(1)} %bitcast.143), channel_id=1, source_target_pairs={{0,1},{1,0},{2,3},{3,2},{4,5},{5,4},{6,7},{7,6},{8,9},{9,8},{10,11... | collective-permute-start | bytes 196616 | tf_op jit(solution)/shard_map/ppermute | solution.py:95
  63.2 12.7 %all-to-all-start.2 = ((bf16[4,64,1024]{2,1,0:T(8,128)(2,1)}), bf16[4,64,1024]{2,1,0:T(8,128)(2,1)S(1)}, u32[]{:S(2)}, u32[]{:S(2)}) async-start(bf16[4,64,1024]{2,1,0:T(8,128)(2,1)} %bitcast.26), calls=%async_computation.2 | async-start | bytes 1048576 | tf_op jit(solution)/shard_map/all_to_all | solution.py:90
  66.8 13.9 %copy-start.10 = (bf16[512]{0:T(512)(128)(2,1)S(1)}, bf16[512]{0:T(512)(128)(2,1)}, u32[]{:S(2)}) copy-start(bf16[512]{0:T(512)(128)(2,1)} %param.29) | copy-start | bytes 3076
  66.8 17.0 %copy-start = (bf16[512,1024]{1,0:T(8,128)(2,1)S(1)}, bf16[512,1024]{1,0:T(8,128)(2,1)}, u32[]{:S(2)}) copy-start(bf16[512,1024]{1,0:T(8,128)(2,1)} %param.30) | copy-start | bytes 3145732
  77.2 11.5 %all-to-all-start.3 = ((bf16[4,64,1024]{2,1,0:T(8,128)(2,1)}), bf16[4,64,1024]{2,1,0:T(8,128)(2,1)S(1)}, u32[]{:S(2)}, u32[]{:S(2)}) async-start(bf16[4,64,1024]{2,1,0:T(8,128)(2,1)} %add_convert_fusion), calls=%async_computation.3 | async-start | bytes 1048576 | tf_op jit(solution)/shard_map/all_to_all | solution.py:189
  80.7 5.1 %collective-permute-start.3 = (bf16[512]{0:T(512)(128)(2,1)S(1)}, bf16[512]{0:T(512)(128)(2,1)S(1)}, u32[]{:S(2)}, u32[]{:S(2)}) collective-permute-start(bf16[512]{0:T(512)(128)(2,1)S(1)} %copy-done.10), channel_id=1, source_target_pairs={{0,1},{1,0},{2,3},{3,2},{4,5},{5,4},{6,7},{7,6},{8,9},{9,8},{10,11... | collective-permute-start | bytes 3080 | tf_op jit(solution)/shard_map/ppermute | solution.py:95
  83.8 9.8 %collective-permute-start.4 = (bf16[512,1024]{1,0:T(8,128)(2,1)S(1)}, bf16[512,1024]{1,0:T(8,128)(2,1)S(1)}, u32[]{:S(2)}, u32[]{:S(2)}) collective-permute-start(bf16[512,1024]{1,0:T(8,128)(2,1)S(1)} %copy-done), channel_id=1, source_target_pairs={{0,1},{1,0},{2,3},{3,2},{4,5},{5,4},{6,7},{7,6},{8,9},{9,8},{10,11... | collective-permute-start | bytes 3145736 | tf_op jit(solution)/shard_map/ppermute | solution.py:95
  93.6 4.9 %copy-start.8 = (bf16[1024]{0:T(1024)(128)(2,1)S(1)}, bf16[1024]{0:T(1024)(128)(2,1)}, u32[]{:S(2)}) copy-start(bf16[1024]{0:T(1024)(128)(2,1)} %param.31) | copy-start | bytes 6148
  94.9 10.4 %all-to-all-start.4 = ((bf16[4,64,1024]{2,1,0:T(8,128)(2,1)}), bf16[4,64,1024]{2,1,0:T(8,128)(2,1)S(1)}, u32[]{:S(2)}, u32[]{:S(2)}) async-start(bf16[4,64,1024]{2,1,0:T(8,128)(2,1)} %bitcast.30), calls=%async_computation.4 | async-start | bytes 1048576 | tf_op jit(solution)/shard_map/all_to_all | solution.py:90
  105.4 17.2 %copy-start.13 = (s32[64]{0:T(128)S(1)}, s32[64]{0:T(128)}, u32[]{:S(2)}) copy-start(s32[64]{0:T(128)} %param.21) | copy-start | bytes 772
  111.0 29.3 %all-to-all-start.5 = ((bf16[512,1,128]{2,1,0:T(2,128)(2,1)}), bf16[512,1,128]{2,1,0:T(2,128)(2,1)S(1)}, u32[]{:S(2)}, u32[]{:S(2)}) async-start(bf16[512,1,128]{2,1,0:T(2,128)(2,1)} %add_convert_fusion.1), calls=%async_computation.5 | async-start | bytes 524288 | tf_op jit(solution)/shard_map/all_to_all | solution.py:213

commit v10 on v9

--- a/solution.py
+++ b/solution.py
@@ -176,6 +176,7 @@
         "x",
     )
     pre_norm = own_rows + attended
+    normed = layer_norm(pre_norm, norm_gains[0], norm_biases[0]).astype(jnp.bfloat16)
     average = jnp.mean(pre_norm, axis=-1, keepdims=True)
     centred = pre_norm - average
     spread = jnp.mean(centred * centred, axis=-1, keepdims=True)
@@ -185,7 +186,6 @@
         * norm_gains[0].astype(jnp.float32)
         + norm_biases[0].astype(jnp.float32)
     ).astype(jnp.bfloat16)
-    normed = normed_copies[0]
     normed_half = lax.all_to_all(normed_copies, "x", 0, 0, tiled=True).reshape(-1, width)
     unit_count = widen_weight.shape[1]
     widened = jnp.dot(
@@ -217,7 +217,7 @@
         0,
         tiled=True,
     ).reshape(-1, tp_count, width // tp_count)
-    hidden_out = returned.at[request_slot].get(mode="promise_in_bounds", unique_indices=True)
+    hidden_out = permute_rows(request_slot, returned)
     return (hidden_out, new_cache)
 
 

time: 142 us -> 138 us (0.972)
  other arithmetic: 9.18 us -> 4.75 us
    convert_element_type x1, other arithmetic: 2.64 us -> 0.12 us  [on_device(): updated = layer_norm(normed.astype(jnp.float32) + fed_total + narrow_bias...]
  transfers between devices with their start and end apart: 10 -> 10, of which waited for: 6 -> 6; matrix products, arithmetic and copies ran while one was open for 13% -> 12% of each run, Pallas kernels for 0% -> 0%
where the time goes in v10:
time: 138 us
  waiting for transfers between devices  41.5 us (30%)
  starting transfers between devices  41.1 us (30%)
  blocking collectives  28.6 us (21%)
  matrix products  11.8 us (9%)
  local copies, waits for them, and re-layouts  6.81 us (5%)
  other arithmetic  4.75 us (3%)
  between operations  3.16 us (2%)
    all_to_all x1, blocking collectives, on_device(): lax.all_to_all(jnp.transpose(routed_in, (1, 0, 2)), 'req', split_axis=1,...  28.6 us
    all_to_all x1, waiting for transfers between devices, on_device(): lax.all_to_all(updated.reshape(rows * tp_count, width // tp_count), ('req...  16.4 us
    all_to_all x2, waiting for transfers between devices, reduce_tp(): lax.all_to_all(partial.reshape(tp_count, rows, -1), names, 0, 0, tiled=True)  15.7 us
    ppermute x5, starting transfers between devices, from_partner(): return lax.ppermute(block, 'core', [(0, 1), (1, 0)])  12.2 us
    all_to_all x1, starting transfers between devices, on_device(): lax.all_to_all(updated.reshape(rows * tp_count, width // tp_count), ('req...  11.6 us
    all_to_all x2, starting transfers between devices, reduce_tp(): lax.all_to_all(partial.reshape(tp_count, rows, -1), names, 0, 0, tiled=True)  7.12 us
    all_to_all x1, starting transfers between devices, gather_tp(): got = lax.all_to_all(copies, names, axis, axis, tiled=True)  6.6 us
    all_to_all x1, waiting for transfers between devices, gather_tp(): got = lax.all_to_all(copies, names, axis, axis, tiled=True)  5.93 us
  transfers between devices with their start and end apart: 10, of which 6 were waited for; matrix products, arithmetic and copies ran while one was open for 12% of the time, Pallas kernels for 0%

profile of v10, /device:TPU:1, one launch (start us, length us, event | category | flops | bytes accessed | tf_op | source)
XLA Modules:
  0.0 137.7 jit_solution(8693430909652054444)
XLA Ops:
  0.6 1.1 fusion.23
  1.9 28.6 %all_to_all.35 = bf16[8,64,128]{2,0,1:T(8,128)(2,1)S(1)} all-to-all(bf16[8,64,128]{2,0,1:T(8,128)(2,1)S(1)} %bitcast.119), channel_id=1, replica_groups=mesh['req'=64,'x'=4,'core'=2] {'req'}, dimensions={1} | all-to-all | bytes 262144 | tf_op jit(solution)/shard_map/all_to_all | solution.py:135
  30.4 1.2 broadcast_in_dim.41
  31.6 6.6 %all-to-all-start.1 = ((bf16[512,8,128]{2,0,1:T(8,128)(2,1)}), bf16[512,8,128]{2,0,1:T(8,128)(2,1)S(1)}, u32[]{:S(2)}, u32[]{:S(2)}) async-start(bf16[512,8,128]{2,0,1:T(8,128)(2,1)} %broadcast_in_dim.41), calls=%async_computation.1 | async-start | bytes 2097152 | tf_op jit(solution)/shard_map/all_to_all | solution.py:84
  38.2 1.9 %collective-permute-start.1 = (bf16[128,1024]{1,0:T(8,128)(2,1)S(1)}, bf16[128,1024]{1,0:T(8,128)(2,1)S(1)}, u32[]{:S(2)}, u32[]{:S(2)}) collective-permute-start(bf16[128,1024]{1,0:T(8,128)(2,1)S(1)} %copy-done.2), channel_id=1, source_target_pairs={{0,1},{1,0},{2,3},{3,2},{4,5},{5,4},{6,7},{7,6},{8,9},{9,8},{10,11... | collective-permute-start | bytes 786440 | tf_op jit(solution)/shard_map/ppermute | solution.py:95
  40.2 2.4 %collective-permute-start.2 = (bf16[1024,512]{1,0:T(8,128)(2,1)}, bf16[1024,512]{1,0:T(8,128)(2,1)}, u32[]{:S(2)}, u32[]{:S(2)}) collective-permute-start(bf16[1024,512]{1,0:T(8,128)(2,1)} %param.28), channel_id=1, source_target_pairs={{0,1},{1,0},{2,3},{3,2},{4,5},{5,4},{6,7},{7,6},{8,9},{9,8},{10,11... | collective-permute-start | bytes 3145736 | tf_op jit(solution)/shard_map/ppermute | solution.py:95
  42.6 0.6 dynamic_slice.21
  45.8 0.6 dynamic_slice.22
  46.3 0.6 iota_compare_fusion.4
  47.3 5.9 %all-to-all-done.1 = bf16[512,8,128]{2,0,1:T(8,128)(2,1)S(1)} async-done(((bf16[512,8,128]{2,0,1:T(8,128)(2,1)}), bf16[512,8,128]{2,0,1:T(8,128)(2,1)S(1)}, u32[]{:S(2)}, u32[]{:S(2)}) %all-to-all-start.1) | async-done | bytes 1048608 | tf_op jit(solution)/shard_map/all_to_all | solution.py:84
  53.2 0.6 fusion.67
  55.7 0.9 fusion.4
  56.6 0.7 fusion.22
  58.3 2.9 %collective-permute-start = (bf16[4,64,128]{2,1,0:T(8,128)(2,1)S(1)}, bf16[4,64,128]{2,1,0:T(8,128)(2,1)S(1)}, u32[]{:S(2)}, u32[]{:S(2)}) collective-permute-start(bf16[4,64,128]{2,1,0:T(8,128)(2,1)S(1)} %bitcast.128), channel_id=1, source_target_pairs={{0,1},{1,0},{2,3},{3,2},{4,5},{5,4},{6,7},{7,6},{8,9},{9,8},{10,11... | collective-permute-start | bytes 196616 | tf_op jit(solution)/shard_map/ppermute | solution.py:95
  62.0 1.1 fusion.17
  63.1 3.5 %all-to-all-start.2 = ((bf16[4,64,1024]{2,1,0:T(8,128)(2,1)}), bf16[4,64,1024]{2,1,0:T(8,128)(2,1)S(1)}, u32[]{:S(2)}, u32[]{:S(2)}) async-start(bf16[4,64,1024]{2,1,0:T(8,128)(2,1)} %bitcast.26), calls=%async_computation.2 | async-start | bytes 1048576 | tf_op jit(solution)/shard_map/all_to_all | solution.py:90
  66.8 9.0 %all-to-all-done.2 = bf16[4,64,1024]{2,1,0:T(8,128)(2,1)S(1)} async-done(((bf16[4,64,1024]{2,1,0:T(8,128)(2,1)}), bf16[4,64,1024]{2,1,0:T(8,128)(2,1)S(1)}, u32[]{:S(2)}, u32[]{:S(2)}) %all-to-all-start.2) | async-done | bytes 524320 | tf_op jit(solution)/shard_map/all_to_all | solution.py:90
  76.2 0.9 add_convert_fusion
  77.2 3.5 %all-to-all-start.3 = ((bf16[4,64,1024]{2,1,0:T(8,128)(2,1)}), bf16[4,64,1024]{2,1,0:T(8,128)(2,1)S(1)}, u32[]{:S(2)}, u32[]{:S(2)}) async-start(bf16[4,64,1024]{2,1,0:T(8,128)(2,1)} %add_convert_fusion), calls=%async_computation.3 | async-start | bytes 1048576 | tf_op jit(solution)/shard_map/all_to_all | solution.py:189
  80.7 3.1 %collective-permute-start.3 = (bf16[512]{0:T(512)(128)(2,1)S(1)}, bf16[512]{0:T(512)(128)(2,1)S(1)}, u32[]{:S(2)}, u32[]{:S(2)}) collective-permute-start(bf16[512]{0:T(512)(128)(2,1)S(1)} %copy-done.10), channel_id=1, source_target_pairs={{0,1},{1,0},{2,3},{3,2},{4,5},{5,4},{6,7},{7,6},{8,9},{9,8},{10,11... | collective-permute-start | bytes 3080 | tf_op jit(solution)/shard_map/ppermute | solution.py:95
  83.8 1.9 %collective-permute-start.4 = (bf16[512,1024]{1,0:T(8,128)(2,1)S(1)}, bf16[512,1024]{1,0:T(8,128)(2,1)S(1)}, u32[]{:S(2)}, u32[]{:S(2)}) collective-permute-start(bf16[512,1024]{1,0:T(8,128)(2,1)S(1)} %copy-done), channel_id=1, source_target_pairs={{0,1},{1,0},{2,3},{3,2},{4,5},{5,4},{6,7},{7,6},{8,9},{9,8},{10,11... | collective-permute-start | bytes 3145736 | tf_op jit(solution)/shard_map/ppermute | solution.py:95
  85.8 2.9 %all-to-all-done.3 = bf16[4,64,1024]{2,1,0:T(8,128)(2,1)S(1)} async-done(((bf16[4,64,1024]{2,1,0:T(8,128)(2,1)}), bf16[4,64,1024]{2,1,0:T(8,128)(2,1)S(1)}, u32[]{:S(2)}, u32[]{:S(2)}) %all-to-all-start.3) | async-done | bytes 524320 | tf_op jit(solution)/shard_map/all_to_all | solution.py:189
  88.7 4.4 %fusion.27 = bf16[256,1024]{1,0:T(8,128)(2,1)S(1)} fusion(bf16[256,1024]{1,0:T(8,128)(2,1)S(1)} %bitcast.118, bf16[1024,512]{1,0:T(8,128)(2,1)} %collective-permute-done.2, bf16[1024,512]{1,0:T(8,128)(2,1)} %param.28, f32[1024]{0:T(1024)S(1)} %maximum_convert_fusion), kind=kOutput, calls=%fused_computation.38 | convolution fusion | flops 558366720 | bytes 3149824 | tf_op jit(solution)/shard_map/dot_general | solution.py:191
  93.6 1.3 fusion.14
  94.9 3.6 %all-to-all-start.4 = ((bf16[4,64,1024]{2,1,0:T(8,128)(2,1)}), bf16[4,64,1024]{2,1,0:T(8,128)(2,1)S(1)}, u32[]{:S(2)}, u32[]{:S(2)}) async-start(bf16[4,64,1024]{2,1,0:T(8,128)(2,1)} %bitcast.30), calls=%async_computation.4 | async-start | bytes 1048576 | tf_op jit(solution)/shard_map/all_to_all | solution.py:90
  98.5 6.7 %all-to-all-done.4 = bf16[4,64,1024]{2,1,0:T(8,128)(2,1)S(1)} async-done(((bf16[4,64,1024]{2,1,0:T(8,128)(2,1)}), bf16[4,64,1024]{2,1,0:T(8,128)(2,1)S(1)}, u32[]{:S(2)}, u32[]{:S(2)}) %all-to-all-start.4) | async-done | bytes 524320 | tf_op jit(solution)/shard_map/all_to_all | solution.py:90
  105.9 0.8 all_to_all.28
  106.7 11.6 %all-to-all-start.5 = ((bf16[512,1,128]{2,1,0:T(2,128)(2,1)}), bf16[512,1,128]{2,1,0:T(2,128)(2,1)S(1)}, u32[]{:S(2)}, u32[]{:S(2)}) async-start(bf16[512,1,128]{2,1,0:T(2,128)(2,1)} %all_to_all.28), calls=%async_computation.5 | async-start | bytes 524288 | tf_op jit(solution)/shard_map/all_to_all | solution.py:213
  118.6 0.9 copy.86
  119.5 16.4 %all-to-all-done.5 = bf16[512,1,128]{2,1,0:T(2,128)(2,1)S(1)} async-done(((bf16[512,1,128]{2,1,0:T(2,128)(2,1)}), bf16[512,1,128]{2,1,0:T(2,128)(2,1)S(1)}, u32[]{:S(2)}, u32[]{:S(2)}) %all-to-all-start.5) | async-done | bytes 131104 | tf_op jit(solution)/shard_map/all_to_all | solution.py:213
  135.9 0.8 reduce
  137.0 0.7 copy.78
  (78 shorter events, 6.8 us)
Async XLA Ops:
  1.8 36.5 %copy-start.2 = (bf16[128,1024]{1,0:T(8,128)(2,1)S(1)}, bf16[128,1024]{1,0:T(8,128)(2,1)}, u32[]{:S(2)}) copy-start(bf16[128,1024]{1,0:T(8,128)(2,1)} %param.24) | copy-start | bytes 786436
  1.8 40.8 %copy-start.11 = (s32[64]{0:T(128)S(1)}, s32[64]{0:T(128)}, u32[]{:S(2)}) copy-start(s32[64]{0:T(128)} %param.20) | copy-start | bytes 772
  1.8 42.7 %copy-start.7 = (bf16[1024]{0:T(1024)(128)(2,1)S(1)}, bf16[1024]{0:T(1024)(128)(2,1)}, u32[]{:S(2)}) copy-start(bf16[1024]{0:T(1024)(128)(2,1)} %param.25) | copy-start | bytes 6148
  1.8 42.7 %copy-start.3 = (bf16[1,512,128]{2,1,0:T(8,128)(2,1)S(1)}, bf16[1,512,128]{2,1,0:T(8,128)(2,1)}, u32[]{:S(2)}) copy-start(bf16[1,512,128]{2,1,0:T(8,128)(2,1)} %param.18) | copy-start | bytes 393220
  1.9 42.8 %copy-start.1 = (bf16[3,1024,128]{2,1,0:T(8,128)(2,1)S(1)}, bf16[3,1024,128]{2,1,0:T(8,128)(2,1)}, u32[]{:S(2)}) copy-start(bf16[3,1024,128]{2,1,0:T(8,128)(2,1)} %param.22) | copy-start | bytes 2359300
  31.6 13.3 %copy-start.9 = (bf16[3,128]{1,0:T(4,128)(2,1)S(1)}, bf16[3,128]{1,0:T(4,128)(2,1)}, u32[]{:S(2)}) copy-start(bf16[3,128]{1,0:T(4,128)(2,1)} %param.23) | copy-start | bytes 2308
  31.6 13.3 %copy-start.4 = (bf16[1,512,128]{2,1,0:T(8,128)(2,1)S(1)}, bf16[1,512,128]{2,1,0:T(8,128)(2,1)}, u32[]{:S(2)}) copy-start(bf16[1,512,128]{2,1,0:T(8,128)(2,1)} %param.17) | copy-start | bytes 393220
  31.6 14.1 %copy-start.13 = (s32[64]{0:T(128)S(1)}, s32[64]{0:T(128)}, u32[]{:S(2)}) copy-start(s32[64]{0:T(128)} %param.19) | copy-start | bytes 772
  31.6 15.4 %copy-start.5 = (bf16[2,1024]{1,0:T(2,128)(2,1)S(1)}, bf16[2,1024]{1,0:T(2,128)(2,1)}, u32[]{:S(2)}) copy-start(bf16[2,1024]{1,0:T(2,128)(2,1)} %param.27) | copy-start | bytes 12292
  31.6 15.4 %copy-start.6 = (bf16[2,1024]{1,0:T(2,128)(2,1)S(1)}, bf16[2,1024]{1,0:T(2,128)(2,1)}, u32[]{:S(2)}) copy-start(bf16[2,1024]{1,0:T(2,128)(2,1)} %param.26) | copy-start | bytes 12292
  31.6 21.6 %all-to-all-start.1 = ((bf16[512,8,128]{2,0,1:T(8,128)(2,1)}), bf16[512,8,128]{2,0,1:T(8,128)(2,1)S(1)}, u32[]{:S(2)}, u32[]{:S(2)}) async-start(bf16[512,8,128]{2,0,1:T(8,128)(2,1)} %broadcast_in_dim.41), calls=%async_computation.1 | async-start | bytes 2097152 | tf_op jit(solution)/shard_map/all_to_all | solution.py:84
  38.2 23.2 %collective-permute-start.1 = (bf16[128,1024]{1,0:T(8,128)(2,1)S(1)}, bf16[128,1024]{1,0:T(8,128)(2,1)S(1)}, u32[]{:S(2)}, u32[]{:S(2)}) collective-permute-start(bf16[128,1024]{1,0:T(8,128)(2,1)S(1)} %copy-done.2), channel_id=1, source_target_pairs={{0,1},{1,0},{2,3},{3,2},{4,5},{5,4},{6,7},{7,6},{8,9},{9,8},{10,11... | collective-permute-start | bytes 786440 | tf_op jit(solution)/shard_map/ppermute | solution.py:95
  40.2 45.6 %collective-permute-start.2 = (bf16[1024,512]{1,0:T(8,128)(2,1)}, bf16[1024,512]{1,0:T(8,128)(2,1)}, u32[]{:S(2)}, u32[]{:S(2)}) collective-permute-start(bf16[1024,512]{1,0:T(8,128)(2,1)} %param.28), channel_id=1, source_target_pairs={{0,1},{1,0},{2,3},{3,2},{4,5},{5,4},{6,7},{7,6},{8,9},{9,8},{10,11... | collective-permute-start | bytes 3145736 | tf_op jit(solution)/shard_map/ppermute | solution.py:95
  58.3 3.8 %collective-permute-start = (bf16[4,64,128]{2,1,0:T(8,128)(2,1)S(1)}, bf16[4,64,128]{2,1,0:T(8,128)(2,1)S(1)}, u32[]{:S(2)}, u32[]{:S(2)}) collective-permute-start(bf16[4,64,128]{2,1,0:T(8,128)(2,1)S(1)} %bitcast.128), channel_id=1, source_target_pairs={{0,1},{1,0},{2,3},{3,2},{4,5},{5,4},{6,7},{7,6},{8,9},{9,8},{10,11... | collective-permute-start | bytes 196616 | tf_op jit(solution)/shard_map/ppermute | solution.py:95
  63.1 12.7 %all-to-all-start.2 = ((bf16[4,64,1024]{2,1,0:T(8,128)(2,1)}), bf16[4,64,1024]{2,1,0:T(8,128)(2,1)S(1)}, u32[]{:S(2)}, u32[]{:S(2)}) async-start(bf16[4,64,1024]{2,1,0:T(8,128)(2,1)} %bitcast.26), calls=%async_computation.2 | async-start | bytes 1048576 | tf_op jit(solution)/shard_map/all_to_all | solution.py:90
  66.8 13.9 %copy-start.10 = (bf16[512]{0:T(512)(128)(2,1)S(1)}, bf16[512]{0:T(512)(128)(2,1)}, u32[]{:S(2)}) copy-start(bf16[512]{0:T(512)(128)(2,1)} %param.29) | copy-start | bytes 3076
  66.8 17.0 %copy-start = (bf16[512,1024]{1,0:T(8,128)(2,1)S(1)}, bf16[512,1024]{1,0:T(8,128)(2,1)}, u32[]{:S(2)}) copy-start(bf16[512,1024]{1,0:T(8,128)(2,1)} %param.30) | copy-start | bytes 3145732
  77.2 11.5 %all-to-all-start.3 = ((bf16[4,64,1024]{2,1,0:T(8,128)(2,1)}), bf16[4,64,1024]{2,1,0:T(8,128)(2,1)S(1)}, u32[]{:S(2)}, u32[]{:S(2)}) async-start(bf16[4,64,1024]{2,1,0:T(8,128)(2,1)} %add_convert_fusion), calls=%async_computation.3 | async-start | bytes 1048576 | tf_op jit(solution)/shard_map/all_to_all | solution.py:189
  80.7 5.1 %collective-permute-start.3 = (bf16[512]{0:T(512)(128)(2,1)S(1)}, bf16[512]{0:T(512)(128)(2,1)S(1)}, u32[]{:S(2)}, u32[]{:S(2)}) collective-permute-start(bf16[512]{0:T(512)(128)(2,1)S(1)} %copy-done.10), channel_id=1, source_target_pairs={{0,1},{1,0},{2,3},{3,2},{4,5},{5,4},{6,7},{7,6},{8,9},{9,8},{10,11... | collective-permute-start | bytes 3080 | tf_op jit(solution)/shard_map/ppermute | solution.py:95
  83.8 9.8 %collective-permute-start.4 = (bf16[512,1024]{1,0:T(8,128)(2,1)S(1)}, bf16[512,1024]{1,0:T(8,128)(2,1)S(1)}, u32[]{:S(2)}, u32[]{:S(2)}) collective-permute-start(bf16[512,1024]{1,0:T(8,128)(2,1)S(1)} %copy-done), channel_id=1, source_target_pairs={{0,1},{1,0},{2,3},{3,2},{4,5},{5,4},{6,7},{7,6},{8,9},{9,8},{10,11... | collective-permute-start | bytes 3145736 | tf_op jit(solution)/shard_map/ppermute | solution.py:95
  93.6 4.9 %copy-start.8 = (bf16[1024]{0:T(1024)(128)(2,1)S(1)}, bf16[1024]{0:T(1024)(128)(2,1)}, u32[]{:S(2)}) copy-start(bf16[1024]{0:T(1024)(128)(2,1)} %param.31) | copy-start | bytes 6148
  94.9 10.4 %all-to-all-start.4 = ((bf16[4,64,1024]{2,1,0:T(8,128)(2,1)}), bf16[4,64,1024]{2,1,0:T(8,128)(2,1)S(1)}, u32[]{:S(2)}, u32[]{:S(2)}) async-start(bf16[4,64,1024]{2,1,0:T(8,128)(2,1)} %bitcast.30), calls=%async_computation.4 | async-start | bytes 1048576 | tf_op jit(solution)/shard_map/all_to_all | solution.py:90
  105.6 31.2 %copy-start.12 = (s32[64]{0:T(128)S(1)}, s32[64]{0:T(128)}, u32[]{:S(2)}) copy-start(s32[64]{0:T(128)} %param.21) | copy-start | bytes 772
  106.7 29.2 %all-to-all-start.5 = ((bf16[512,1,128]{2,1,0:T(2,128)(2,1)}), bf16[512,1,128]{2,1,0:T(2,128)(2,1)S(1)}, u32[]{:S(2)}, u32[]{:S(2)}) async-start(bf16[512,1,128]{2,1,0:T(2,128)(2,1)} %all_to_all.28), calls=%async_computation.5 | async-start | bytes 524288 | tf_op jit(solution)/shard_map/all_to_all | solution.py:213

commit v11 on v8

--- a/solution.py
+++ b/solution.py
@@ -200,10 +200,14 @@
         activated[:, unit_count:], partner_narrow
     )
     fed_total = reduce_tp(pair.astype(jnp.bfloat16), x_count, "x")
-    updated = layer_norm(
-        normed.astype(jnp.float32) + fed_total + narrow_bias.astype(jnp.float32),
-        norm_gains[1],
-        norm_biases[1],
+    pieces = (rows, tp_count, width // tp_count)
+    pre_out = (normed.astype(jnp.float32) + fed_total + narrow_bias.astype(jnp.float32)).reshape(pieces)
+    average = jnp.mean(pre_out, axis=(1, 2), keepdims=True)
+    centred = pre_out - average
+    spread = jnp.mean(centred * centred, axis=(1, 2), keepdims=True)
+    updated = (
+        centred * lax.rsqrt(spread + 1e-05) * norm_gains[1].astype(jnp.float32).reshape(pieces[1:])
+        + norm_biases[1].astype(jnp.float32).reshape(pieces[1:])
     ).astype(jnp.bfloat16)
     returned = lax.all_to_all(
         updated.reshape(rows * tp_count, width // tp_count),

time: 138 us -> 141 us (1.022)
  other arithmetic: 4.05 us -> 6.45 us
    convert_element_type x1, other arithmetic: 0.18 us -> 2.64 us  [on_device(): updated = (centred * lax.rsqrt(spread + 1e-05) * norm_gains[1].astype(jnp...]
where the time goes in v11:
time: 141 us; the launch traced here: 140 us
  waiting for transfers between devices  41.5 us (29%)
  starting transfers between devices  41.1 us (29%)
  blocking collectives  28.6 us (20%)
  matrix products  11.8 us (8%)
  local copies, waits for them, and re-layouts  7.31 us (5%)
  other arithmetic  6.45 us (5%)
  between operations  3.2 us (2%)
    all_to_all x1, blocking collectives, on_device(): lax.all_to_all(jnp.transpose(routed_in, (1, 0, 2)), 'req', split_axis=1,...  28.6 us
    all_to_all x1, waiting for transfers between devices, on_device(): lax.all_to_all(updated.reshape(rows * tp_count, width // tp_count), ('req...  16.4 us
    all_to_all x2, waiting for transfers between devices, reduce_tp(): lax.all_to_all(partial.reshape(tp_count, rows, -1), names, 0, 0, tiled=True)  15.7 us
    ppermute x5, starting transfers between devices, from_partner(): return lax.ppermute(block, 'core', [(0, 1), (1, 0)])  12.2 us
    all_to_all x1, starting transfers between devices, on_device(): lax.all_to_all(updated.reshape(rows * tp_count, width // tp_count), ('req...  11.7 us
    all_to_all x2, starting transfers between devices, gather_tp(): got = lax.all_to_all(copies, names, axis, axis, tiled=True)  10.1 us
    all_to_all x2, waiting for transfers between devices, gather_tp(): got = lax.all_to_all(copies, names, axis, axis, tiled=True)  8.85 us
    all_to_all x2, starting transfers between devices, reduce_tp(): lax.all_to_all(partial.reshape(tp_count, rows, -1), names, 0, 0, tiled=True)  7.12 us
  transfers between devices with their start and end apart: 10, of which 6 were waited for; matrix products, arithmetic and copies ran while one was open for 12% of the time, Pallas kernels for 0%

profile of v11, /device:TPU:1, one launch (start us, length us, event | category | flops | bytes accessed | tf_op | source)
XLA Modules:
  0.0 140.0 jit_solution(10866694910103515696)
XLA Ops:
  0.6 1.1 fusion.23
  1.9 28.6 %all_to_all.31 = bf16[8,64,128]{2,0,1:T(8,128)(2,1)S(1)} all-to-all(bf16[8,64,128]{2,0,1:T(8,128)(2,1)S(1)} %bitcast.125), channel_id=1, replica_groups=mesh['req'=64,'x'=4,'core'=2] {'req'}, dimensions={1} | all-to-all | bytes 262144 | tf_op jit(solution)/shard_map/all_to_all | solution.py:135
  30.4 1.2 broadcast_in_dim.41
  31.6 6.6 %all-to-all-start.1 = ((bf16[512,8,128]{2,0,1:T(8,128)(2,1)}), bf16[512,8,128]{2,0,1:T(8,128)(2,1)S(1)}, u32[]{:S(2)}, u32[]{:S(2)}) async-start(bf16[512,8,128]{2,0,1:T(8,128)(2,1)} %broadcast_in_dim.41), calls=%async_computation.1 | async-start | bytes 2097152 | tf_op jit(solution)/shard_map/all_to_all | solution.py:84
  38.3 1.9 %collective-permute-start.1 = (bf16[128,1024]{1,0:T(8,128)(2,1)S(1)}, bf16[128,1024]{1,0:T(8,128)(2,1)S(1)}, u32[]{:S(2)}, u32[]{:S(2)}) collective-permute-start(bf16[128,1024]{1,0:T(8,128)(2,1)S(1)} %copy-done.2), channel_id=1, source_target_pairs={{0,1},{1,0},{2,3},{3,2},{4,5},{5,4},{6,7},{7,6},{8,9},{9,8},{10,11... | collective-permute-start | bytes 786440 | tf_op jit(solution)/shard_map/ppermute | solution.py:95
  40.2 2.4 %collective-permute-start.2 = (bf16[1024,512]{1,0:T(8,128)(2,1)}, bf16[1024,512]{1,0:T(8,128)(2,1)}, u32[]{:S(2)}, u32[]{:S(2)}) collective-permute-start(bf16[1024,512]{1,0:T(8,128)(2,1)} %param.28), channel_id=1, source_target_pairs={{0,1},{1,0},{2,3},{3,2},{4,5},{5,4},{6,7},{7,6},{8,9},{9,8},{10,11... | collective-permute-start | bytes 3145736 | tf_op jit(solution)/shard_map/ppermute | solution.py:95
  42.6 0.6 dynamic_slice.21
  45.8 0.6 dynamic_slice.22
  46.3 0.6 iota_compare_fusion.4
  47.3 5.9 %all-to-all-done.1 = bf16[512,8,128]{2,0,1:T(8,128)(2,1)S(1)} async-done(((bf16[512,8,128]{2,0,1:T(8,128)(2,1)}), bf16[512,8,128]{2,0,1:T(8,128)(2,1)S(1)}, u32[]{:S(2)}, u32[]{:S(2)}) %all-to-all-start.1) | async-done | bytes 1048608 | tf_op jit(solution)/shard_map/all_to_all | solution.py:84
  53.2 0.6 fusion.67
  55.7 0.9 fusion.4
  56.6 0.7 fusion.22
  58.3 2.9 %collective-permute-start = (bf16[4,64,128]{2,1,0:T(8,128)(2,1)S(1)}, bf16[4,64,128]{2,1,0:T(8,128)(2,1)S(1)}, u32[]{:S(2)}, u32[]{:S(2)}) collective-permute-start(bf16[4,64,128]{2,1,0:T(8,128)(2,1)S(1)} %bitcast.134), channel_id=1, source_target_pairs={{0,1},{1,0},{2,3},{3,2},{4,5},{5,4},{6,7},{7,6},{8,9},{9,8},{10,11... | collective-permute-start | bytes 196616 | tf_op jit(solution)/shard_map/ppermute | solution.py:95
  62.0 1.1 fusion.17
  63.1 3.5 %all-to-all-start.2 = ((bf16[4,64,1024]{2,1,0:T(8,128)(2,1)}), bf16[4,64,1024]{2,1,0:T(8,128)(2,1)S(1)}, u32[]{:S(2)}, u32[]{:S(2)}) async-start(bf16[4,64,1024]{2,1,0:T(8,128)(2,1)} %bitcast.26), calls=%async_computation.2 | async-start | bytes 1048576 | tf_op jit(solution)/shard_map/all_to_all | solution.py:90
  66.8 9.0 %all-to-all-done.2 = bf16[4,64,1024]{2,1,0:T(8,128)(2,1)S(1)} async-done(((bf16[4,64,1024]{2,1,0:T(8,128)(2,1)}), bf16[4,64,1024]{2,1,0:T(8,128)(2,1)S(1)}, u32[]{:S(2)}, u32[]{:S(2)}) %all-to-all-start.2) | async-done | bytes 524320 | tf_op jit(solution)/shard_map/all_to_all | solution.py:90
  76.3 0.9 broadcast_in_dim.45
  77.2 3.5 %all-to-all-start.3 = ((bf16[4,64,1024]{2,1,0:T(8,128)(2,1)}), bf16[4,64,1024]{2,1,0:T(8,128)(2,1)S(1)}, u32[]{:S(2)}, u32[]{:S(2)}) async-start(bf16[4,64,1024]{2,1,0:T(8,128)(2,1)} %broadcast_in_dim.45), calls=%async_computation.3 | async-start | bytes 1048576 | tf_op jit(solution)/shard_map/all_to_all | solution.py:84
  80.7 3.1 %collective-permute-start.3 = (bf16[512]{0:T(512)(128)(2,1)S(1)}, bf16[512]{0:T(512)(128)(2,1)S(1)}, u32[]{:S(2)}, u32[]{:S(2)}) collective-permute-start(bf16[512]{0:T(512)(128)(2,1)S(1)} %copy-done.10), channel_id=1, source_target_pairs={{0,1},{1,0},{2,3},{3,2},{4,5},{5,4},{6,7},{7,6},{8,9},{9,8},{10,11... | collective-permute-start | bytes 3080 | tf_op jit(solution)/shard_map/ppermute | solution.py:95
  83.8 1.9 %collective-permute-start.4 = (bf16[512,1024]{1,0:T(8,128)(2,1)S(1)}, bf16[512,1024]{1,0:T(8,128)(2,1)S(1)}, u32[]{:S(2)}, u32[]{:S(2)}) collective-permute-start(bf16[512,1024]{1,0:T(8,128)(2,1)S(1)} %copy-done), channel_id=1, source_target_pairs={{0,1},{1,0},{2,3},{3,2},{4,5},{5,4},{6,7},{7,6},{8,9},{9,8},{10,11... | collective-permute-start | bytes 3145736 | tf_op jit(solution)/shard_map/ppermute | solution.py:95
  85.8 2.9 %all-to-all-done.3 = bf16[4,64,1024]{2,1,0:T(8,128)(2,1)S(1)} async-done(((bf16[4,64,1024]{2,1,0:T(8,128)(2,1)}), bf16[4,64,1024]{2,1,0:T(8,128)(2,1)S(1)}, u32[]{:S(2)}, u32[]{:S(2)}) %all-to-all-start.3) | async-done | bytes 524320 | tf_op jit(solution)/shard_map/all_to_all | solution.py:84
  88.7 4.4 %fusion.27 = bf16[256,1024]{1,0:T(8,128)(2,1)S(1)} fusion(bf16[256,1024]{1,0:T(8,128)(2,1)S(1)} %bitcast.124, bf16[1024,512]{1,0:T(8,128)(2,1)} %collective-permute-done.2, bf16[1024,512]{1,0:T(8,128)(2,1)} %param.28, f32[1024]{0:T(1024)S(1)} %maximum_convert_fusion), kind=kOutput, calls=%fused_computation.38 | convolution fusion | flops 558366720 | bytes 3149824 | tf_op jit(solution)/shard_map/dot_general | solution.py:186
  93.6 1.3 fusion.14
  94.9 3.6 %all-to-all-start.4 = ((bf16[4,64,1024]{2,1,0:T(8,128)(2,1)}), bf16[4,64,1024]{2,1,0:T(8,128)(2,1)S(1)}, u32[]{:S(2)}, u32[]{:S(2)}) async-start(bf16[4,64,1024]{2,1,0:T(8,128)(2,1)} %bitcast.30), calls=%async_computation.4 | async-start | bytes 1048576 | tf_op jit(solution)/shard_map/all_to_all | solution.py:90
  98.6 6.7 %all-to-all-done.4 = bf16[4,64,1024]{2,1,0:T(8,128)(2,1)S(1)} async-done(((bf16[4,64,1024]{2,1,0:T(8,128)(2,1)}), bf16[4,64,1024]{2,1,0:T(8,128)(2,1)S(1)}, u32[]{:S(2)}, u32[]{:S(2)}) %all-to-all-start.4) | async-done | bytes 524320 | tf_op jit(solution)/shard_map/all_to_all | solution.py:90
  106.3 2.6 %add_convert_fusion = bf16[512,1,128]{2,1,0:T(2,128)(2,1)} fusion(f32[512,1,128]{2,1,0:T(1,128)S(1)} %bitcast.118, f32[512,1,128]{2,1,0:T(1,128)S(1)} %bitcast.119, f32[512,1,128]{2,1,0:T(1,128)S(1)} %bitcast.117, f32[512]{0:T(512)S(1)} %mul.161, f32[512]{0:T(512)S(1)} %sub.88), kind=kLoop, calls=%fused_computation.73 | loop fusion | flops 327680 | bytes 921600 | tf_op jit(solution)/shard_map/convert_element_type | solution.py:211
  108.9 11.7 %all-to-all-start.5 = ((bf16[512,1,128]{2,1,0:T(2,128)(2,1)}), bf16[512,1,128]{2,1,0:T(2,128)(2,1)S(1)}, u32[]{:S(2)}, u32[]{:S(2)}) async-start(bf16[512,1,128]{2,1,0:T(2,128)(2,1)} %add_convert_fusion), calls=%async_computation.5 | async-start | bytes 524288 | tf_op jit(solution)/shard_map/all_to_all | solution.py:212
  120.9 0.9 copy.86
  121.8 16.4 %all-to-all-done.5 = bf16[512,1,128]{2,1,0:T(2,128)(2,1)S(1)} async-done(((bf16[512,1,128]{2,1,0:T(2,128)(2,1)}), bf16[512,1,128]{2,1,0:T(2,128)(2,1)S(1)}, u32[]{:S(2)}, u32[]{:S(2)}) %all-to-all-start.5) | async-done | bytes 131104 | tf_op jit(solution)/shard_map/all_to_all | solution.py:212
  138.2 0.8 reduce.2
  139.3 0.7 copy.78
  (85 shorter events, 7.3 us)
Async XLA Ops:
  1.8 36.5 %copy-start.2 = (bf16[128,1024]{1,0:T(8,128)(2,1)S(1)}, bf16[128,1024]{1,0:T(8,128)(2,1)}, u32[]{:S(2)}) copy-start(bf16[128,1024]{1,0:T(8,128)(2,1)} %param.24) | copy-start | bytes 786436
  1.8 40.8 %copy-start.11 = (s32[64]{0:T(128)S(1)}, s32[64]{0:T(128)}, u32[]{:S(2)}) copy-start(s32[64]{0:T(128)} %param.20) | copy-start | bytes 772
  1.8 42.7 %copy-start.7 = (bf16[1024]{0:T(1024)(128)(2,1)S(1)}, bf16[1024]{0:T(1024)(128)(2,1)}, u32[]{:S(2)}) copy-start(bf16[1024]{0:T(1024)(128)(2,1)} %param.25) | copy-start | bytes 6148
  1.8 42.7 %copy-start.3 = (bf16[1,512,128]{2,1,0:T(8,128)(2,1)S(1)}, bf16[1,512,128]{2,1,0:T(8,128)(2,1)}, u32[]{:S(2)}) copy-start(bf16[1,512,128]{2,1,0:T(8,128)(2,1)} %param.18) | copy-start | bytes 393220
  1.9 42.8 %copy-start.1 = (bf16[3,1024,128]{2,1,0:T(8,128)(2,1)S(1)}, bf16[3,1024,128]{2,1,0:T(8,128)(2,1)}, u32[]{:S(2)}) copy-start(bf16[3,1024,128]{2,1,0:T(8,128)(2,1)} %param.22) | copy-start | bytes 2359300
  31.6 13.3 %copy-start.9 = (bf16[3,128]{1,0:T(4,128)(2,1)S(1)}, bf16[3,128]{1,0:T(4,128)(2,1)}, u32[]{:S(2)}) copy-start(bf16[3,128]{1,0:T(4,128)(2,1)} %param.23) | copy-start | bytes 2308
  31.6 13.3 %copy-start.4 = (bf16[1,512,128]{2,1,0:T(8,128)(2,1)S(1)}, bf16[1,512,128]{2,1,0:T(8,128)(2,1)}, u32[]{:S(2)}) copy-start(bf16[1,512,128]{2,1,0:T(8,128)(2,1)} %param.17) | copy-start | bytes 393220
  31.6 14.1 %copy-start.13 = (s32[64]{0:T(128)S(1)}, s32[64]{0:T(128)}, u32[]{:S(2)}) copy-start(s32[64]{0:T(128)} %param.19) | copy-start | bytes 772
  31.6 15.4 %copy-start.5 = (bf16[2,1024]{1,0:T(2,128)(2,1)S(1)}, bf16[2,1024]{1,0:T(2,128)(2,1)}, u32[]{:S(2)}) copy-start(bf16[2,1024]{1,0:T(2,128)(2,1)} %param.27) | copy-start | bytes 12292
  31.6 15.4 %copy-start.6 = (bf16[2,1024]{1,0:T(2,128)(2,1)S(1)}, bf16[2,1024]{1,0:T(2,128)(2,1)}, u32[]{:S(2)}) copy-start(bf16[2,1024]{1,0:T(2,128)(2,1)} %param.26) | copy-start | bytes 12292
  31.6 21.6 %all-to-all-start.1 = ((bf16[512,8,128]{2,0,1:T(8,128)(2,1)}), bf16[512,8,128]{2,0,1:T(8,128)(2,1)S(1)}, u32[]{:S(2)}, u32[]{:S(2)}) async-start(bf16[512,8,128]{2,0,1:T(8,128)(2,1)} %broadcast_in_dim.41), calls=%async_computation.1 | async-start | bytes 2097152 | tf_op jit(solution)/shard_map/all_to_all | solution.py:84
  38.3 23.2 %collective-permute-start.1 = (bf16[128,1024]{1,0:T(8,128)(2,1)S(1)}, bf16[128,1024]{1,0:T(8,128)(2,1)S(1)}, u32[]{:S(2)}, u32[]{:S(2)}) collective-permute-start(bf16[128,1024]{1,0:T(8,128)(2,1)S(1)} %copy-done.2), channel_id=1, source_target_pairs={{0,1},{1,0},{2,3},{3,2},{4,5},{5,4},{6,7},{7,6},{8,9},{9,8},{10,11... | collective-permute-start | bytes 786440 | tf_op jit(solution)/shard_map/ppermute | solution.py:95
  40.2 45.6 %collective-permute-start.2 = (bf16[1024,512]{1,0:T(8,128)(2,1)}, bf16[1024,512]{1,0:T(8,128)(2,1)}, u32[]{:S(2)}, u32[]{:S(2)}) collective-permute-start(bf16[1024,512]{1,0:T(8,128)(2,1)} %param.28), channel_id=1, source_target_pairs={{0,1},{1,0},{2,3},{3,2},{4,5},{5,4},{6,7},{7,6},{8,9},{9,8},{10,11... | collective-permute-start | bytes 3145736 | tf_op jit(solution)/shard_map/ppermute | solution.py:95
  58.3 3.8 %collective-permute-start = (bf16[4,64,128]{2,1,0:T(8,128)(2,1)S(1)}, bf16[4,64,128]{2,1,0:T(8,128)(2,1)S(1)}, u32[]{:S(2)}, u32[]{:S(2)}) collective-permute-start(bf16[4,64,128]{2,1,0:T(8,128)(2,1)S(1)} %bitcast.134), channel_id=1, source_target_pairs={{0,1},{1,0},{2,3},{3,2},{4,5},{5,4},{6,7},{7,6},{8,9},{9,8},{10,11... | collective-permute-start | bytes 196616 | tf_op jit(solution)/shard_map/ppermute | solution.py:95
  63.1 12.7 %all-to-all-start.2 = ((bf16[4,64,1024]{2,1,0:T(8,128)(2,1)}), bf16[4,64,1024]{2,1,0:T(8,128)(2,1)S(1)}, u32[]{:S(2)}, u32[]{:S(2)}) async-start(bf16[4,64,1024]{2,1,0:T(8,128)(2,1)} %bitcast.26), calls=%async_computation.2 | async-start | bytes 1048576 | tf_op jit(solution)/shard_map/all_to_all | solution.py:90
  66.8 13.9 %copy-start.10 = (bf16[512]{0:T(512)(128)(2,1)S(1)}, bf16[512]{0:T(512)(128)(2,1)}, u32[]{:S(2)}) copy-start(bf16[512]{0:T(512)(128)(2,1)} %param.29) | copy-start | bytes 3076
  66.8 17.0 %copy-start = (bf16[512,1024]{1,0:T(8,128)(2,1)S(1)}, bf16[512,1024]{1,0:T(8,128)(2,1)}, u32[]{:S(2)}) copy-start(bf16[512,1024]{1,0:T(8,128)(2,1)} %param.30) | copy-start | bytes 3145732
  77.2 11.5 %all-to-all-start.3 = ((bf16[4,64,1024]{2,1,0:T(8,128)(2,1)}), bf16[4,64,1024]{2,1,0:T(8,128)(2,1)S(1)}, u32[]{:S(2)}, u32[]{:S(2)}) async-start(bf16[4,64,1024]{2,1,0:T(8,128)(2,1)} %broadcast_in_dim.45), calls=%async_computation.3 | async-start | bytes 1048576 | tf_op jit(solution)/shard_map/all_to_all | solution.py:84
  80.7 5.1 %collective-permute-start.3 = (bf16[512]{0:T(512)(128)(2,1)S(1)}, bf16[512]{0:T(512)(128)(2,1)S(1)}, u32[]{:S(2)}, u32[]{:S(2)}) collective-permute-start(bf16[512]{0:T(512)(128)(2,1)S(1)} %copy-done.10), channel_id=1, source_target_pairs={{0,1},{1,0},{2,3},{3,2},{4,5},{5,4},{6,7},{7,6},{8,9},{9,8},{10,11... | collective-permute-start | bytes 3080 | tf_op jit(solution)/shard_map/ppermute | solution.py:95
  83.8 9.8 %collective-permute-start.4 = (bf16[512,1024]{1,0:T(8,128)(2,1)S(1)}, bf16[512,1024]{1,0:T(8,128)(2,1)S(1)}, u32[]{:S(2)}, u32[]{:S(2)}) collective-permute-start(bf16[512,1024]{1,0:T(8,128)(2,1)S(1)} %copy-done), channel_id=1, source_target_pairs={{0,1},{1,0},{2,3},{3,2},{4,5},{5,4},{6,7},{7,6},{8,9},{9,8},{10,11... | collective-permute-start | bytes 3145736 | tf_op jit(solution)/shard_map/ppermute | solution.py:95
  93.6 4.9 %copy-start.8 = (bf16[1024]{0:T(1024)(128)(2,1)S(1)}, bf16[1024]{0:T(1024)(128)(2,1)}, u32[]{:S(2)}) copy-start(bf16[1024]{0:T(1024)(128)(2,1)} %param.31) | copy-start | bytes 6148
  94.9 10.4 %all-to-all-start.4 = ((bf16[4,64,1024]{2,1,0:T(8,128)(2,1)}), bf16[4,64,1024]{2,1,0:T(8,128)(2,1)S(1)}, u32[]{:S(2)}, u32[]{:S(2)}) async-start(bf16[4,64,1024]{2,1,0:T(8,128)(2,1)} %bitcast.30), calls=%async_computation.4 | async-start | bytes 1048576 | tf_op jit(solution)/shard_map/all_to_all | solution.py:90
  106.3 32.8 %copy-start.12 = (s32[64]{0:T(128)S(1)}, s32[64]{0:T(128)}, u32[]{:S(2)}) copy-start(s32[64]{0:T(128)} %param.21) | copy-start | bytes 772
  108.9 29.3 %all-to-all-start.5 = ((bf16[512,1,128]{2,1,0:T(2,128)(2,1)}), bf16[512,1,128]{2,1,0:T(2,128)(2,1)S(1)}, u32[]{:S(2)}, u32[]{:S(2)}) async-start(bf16[512,1,128]{2,1,0:T(2,128)(2,1)} %add_convert_fusion), calls=%async_computation.5 | async-start | bytes 524288 | tf_op jit(solution)/shard_map/all_to_all | solution.py:212

commit v12 on v8

--- a/solution.py
+++ b/solution.py
@@ -212,7 +212,7 @@
         0,
         tiled=True,
     ).reshape(-1, tp_count, width // tp_count)
-    hidden_out = permute_rows(request_slot, returned)
+    hidden_out = returned.at[request_slot].get(mode="promise_in_bounds", unique_indices=True)
     return (hidden_out, new_cache)
 
 

time: 138 us -> 138 us (level)
  no operation moved by 1% of the time
where the time goes in v12:
time: 138 us
  waiting for transfers between devices  41.5 us (30%)
  starting transfers between devices  41.3 us (30%)
  blocking collectives  28.6 us (21%)
  matrix products  11.6 us (8%)
  local copies, waits for them, and re-layouts  8.22 us (6%)
  other arithmetic  3.3 us (2%)
  between operations  3.16 us (2%)
    all_to_all x1, blocking collectives, on_device(): lax.all_to_all(jnp.transpose(routed_in, (1, 0, 2)), 'req', split_axis=1,...  28.6 us
    all_to_all x1, waiting for transfers between devices, on_device(): lax.all_to_all(updated.reshape(rows * tp_count, width // tp_count), ('req...  16.3 us
    all_to_all x2, waiting for transfers between devices, reduce_tp(): lax.all_to_all(partial.reshape(tp_count, rows, -1), names, 0, 0, tiled=True)  15.7 us
    ppermute x5, starting transfers between devices, from_partner(): return lax.ppermute(block, 'core', [(0, 1), (1, 0)])  12.2 us
    all_to_all x1, starting transfers between devices, on_device(): lax.all_to_all(updated.reshape(rows * tp_count, width // tp_count), ('req...  11.7 us
    all_to_all x2, starting transfers between devices, gather_tp(): got = lax.all_to_all(copies, names, axis, axis, tiled=True)  10.1 us
    all_to_all x2, waiting for transfers between devices, gather_tp(): got = lax.all_to_all(copies, names, axis, axis, tiled=True)  8.85 us
    all_to_all x2, starting transfers between devices, reduce_tp(): lax.all_to_all(partial.reshape(tp_count, rows, -1), names, 0, 0, tiled=True)  7.25 us
  transfers between devices with their start and end apart: 10, of which 6 were waited for; matrix products, arithmetic and copies ran while one was open for 12% of the time, Pallas kernels for 0%

profile of v12, /device:TPU:1, one launch (start us, length us, event | category | flops | bytes accessed | tf_op | source)
XLA Modules:
  0.0 137.5 jit_solution(3660880440500721495)
XLA Ops:
  0.6 1.1 fusion.23
  1.9 28.6 %all_to_all.35 = bf16[8,64,128]{2,0,1:T(8,128)(2,1)S(1)} all-to-all(bf16[8,64,128]{2,0,1:T(8,128)(2,1)S(1)} %bitcast.119), channel_id=1, replica_groups=mesh['req'=64,'x'=4,'core'=2] {'req'}, dimensions={1} | all-to-all | bytes 262144 | tf_op jit(solution)/shard_map/all_to_all | solution.py:135
  30.4 1.2 broadcast_in_dim.43
  31.6 6.6 %all-to-all-start.1 = ((bf16[512,8,128]{2,0,1:T(8,128)(2,1)}), bf16[512,8,128]{2,0,1:T(8,128)(2,1)S(1)}, u32[]{:S(2)}, u32[]{:S(2)}) async-start(bf16[512,8,128]{2,0,1:T(8,128)(2,1)} %broadcast_in_dim.43), calls=%async_computation.1 | async-start | bytes 2097152 | tf_op jit(solution)/shard_map/all_to_all | solution.py:84
  38.2 1.9 %collective-permute-start.1 = (bf16[128,1024]{1,0:T(8,128)(2,1)S(1)}, bf16[128,1024]{1,0:T(8,128)(2,1)S(1)}, u32[]{:S(2)}, u32[]{:S(2)}) collective-permute-start(bf16[128,1024]{1,0:T(8,128)(2,1)S(1)} %copy-done.2), channel_id=1, source_target_pairs={{0,1},{1,0},{2,3},{3,2},{4,5},{5,4},{6,7},{7,6},{8,9},{9,8},{10,11... | collective-permute-start | bytes 786440 | tf_op jit(solution)/shard_map/ppermute | solution.py:95
  40.2 2.4 %collective-permute-start.2 = (bf16[1024,512]{1,0:T(8,128)(2,1)}, bf16[1024,512]{1,0:T(8,128)(2,1)}, u32[]{:S(2)}, u32[]{:S(2)}) collective-permute-start(bf16[1024,512]{1,0:T(8,128)(2,1)} %param.28), channel_id=1, source_target_pairs={{0,1},{1,0},{2,3},{3,2},{4,5},{5,4},{6,7},{7,6},{8,9},{9,8},{10,11... | collective-permute-start | bytes 3145736 | tf_op jit(solution)/shard_map/ppermute | solution.py:95
  42.6 0.6 dynamic_slice.21
  45.7 0.6 dynamic_slice.22
  46.3 0.6 iota_compare_fusion.2
  47.3 5.9 %all-to-all-done.1 = bf16[512,8,128]{2,0,1:T(8,128)(2,1)S(1)} async-done(((bf16[512,8,128]{2,0,1:T(8,128)(2,1)}), bf16[512,8,128]{2,0,1:T(8,128)(2,1)S(1)}, u32[]{:S(2)}, u32[]{:S(2)}) %all-to-all-start.1) | async-done | bytes 1048608 | tf_op jit(solution)/shard_map/all_to_all | solution.py:84
  53.2 0.6 fusion.66
  55.7 0.9 fusion.4
  56.6 0.7 fusion.22
  58.3 2.9 %collective-permute-start = (bf16[4,64,128]{2,1,0:T(8,128)(2,1)S(1)}, bf16[4,64,128]{2,1,0:T(8,128)(2,1)S(1)}, u32[]{:S(2)}, u32[]{:S(2)}) collective-permute-start(bf16[4,64,128]{2,1,0:T(8,128)(2,1)S(1)} %bitcast.135), channel_id=1, source_target_pairs={{0,1},{1,0},{2,3},{3,2},{4,5},{5,4},{6,7},{7,6},{8,9},{9,8},{10,11... | collective-permute-start | bytes 196616 | tf_op jit(solution)/shard_map/ppermute | solution.py:95
  61.4 0.6 collective-permute-done
  62.0 1.1 fusion.17
  63.1 3.5 %all-to-all-start.2 = ((bf16[4,64,1024]{2,1,0:T(8,128)(2,1)}), bf16[4,64,1024]{2,1,0:T(8,128)(2,1)S(1)}, u32[]{:S(2)}, u32[]{:S(2)}) async-start(bf16[4,64,1024]{2,1,0:T(8,128)(2,1)} %bitcast.26), calls=%async_computation.2 | async-start | bytes 1048576 | tf_op jit(solution)/shard_map/all_to_all | solution.py:90
  66.8 9.0 %all-to-all-done.2 = bf16[4,64,1024]{2,1,0:T(8,128)(2,1)S(1)} async-done(((bf16[4,64,1024]{2,1,0:T(8,128)(2,1)}), bf16[4,64,1024]{2,1,0:T(8,128)(2,1)S(1)}, u32[]{:S(2)}, u32[]{:S(2)}) %all-to-all-start.2) | async-done | bytes 524320 | tf_op jit(solution)/shard_map/all_to_all | solution.py:90
  76.3 0.9 broadcast_in_dim.74
  77.2 3.5 %all-to-all-start.3 = ((bf16[4,64,1024]{2,1,0:T(8,128)(2,1)}), bf16[4,64,1024]{2,1,0:T(8,128)(2,1)S(1)}, u32[]{:S(2)}, u32[]{:S(2)}) async-start(bf16[4,64,1024]{2,1,0:T(8,128)(2,1)} %broadcast_in_dim.74), calls=%async_computation.3 | async-start | bytes 1048576 | tf_op jit(solution)/shard_map/all_to_all | solution.py:84
  80.7 3.1 %collective-permute-start.3 = (bf16[512]{0:T(512)(128)(2,1)S(1)}, bf16[512]{0:T(512)(128)(2,1)S(1)}, u32[]{:S(2)}, u32[]{:S(2)}) collective-permute-start(bf16[512]{0:T(512)(128)(2,1)S(1)} %copy-done.10), channel_id=1, source_target_pairs={{0,1},{1,0},{2,3},{3,2},{4,5},{5,4},{6,7},{7,6},{8,9},{9,8},{10,11... | collective-permute-start | bytes 3080 | tf_op jit(solution)/shard_map/ppermute | solution.py:95
  83.8 1.9 %collective-permute-start.4 = (bf16[512,1024]{1,0:T(8,128)(2,1)S(1)}, bf16[512,1024]{1,0:T(8,128)(2,1)S(1)}, u32[]{:S(2)}, u32[]{:S(2)}) collective-permute-start(bf16[512,1024]{1,0:T(8,128)(2,1)S(1)} %copy-done), channel_id=1, source_target_pairs={{0,1},{1,0},{2,3},{3,2},{4,5},{5,4},{6,7},{7,6},{8,9},{9,8},{10,11... | collective-permute-start | bytes 3145736 | tf_op jit(solution)/shard_map/ppermute | solution.py:95
  85.8 2.9 %all-to-all-done.3 = bf16[4,64,1024]{2,1,0:T(8,128)(2,1)S(1)} async-done(((bf16[4,64,1024]{2,1,0:T(8,128)(2,1)}), bf16[4,64,1024]{2,1,0:T(8,128)(2,1)S(1)}, u32[]{:S(2)}, u32[]{:S(2)}) %all-to-all-start.3) | async-done | bytes 524320 | tf_op jit(solution)/shard_map/all_to_all | solution.py:84
  88.7 4.4 %fusion.26 = bf16[256,1024]{1,0:T(8,128)(2,1)S(1)} fusion(bf16[256,1024]{1,0:T(8,128)(2,1)S(1)} %bitcast.118, bf16[1024,512]{1,0:T(8,128)(2,1)} %collective-permute-done.2, bf16[1024,512]{1,0:T(8,128)(2,1)} %param.28, f32[1024]{0:T(1024)S(1)} %maximum_convert_fusion), kind=kOutput, calls=%fused_computation.37 | convolution fusion | flops 558366720 | bytes 3149824 | tf_op jit(solution)/shard_map/dot_general | solution.py:186
  93.6 1.3 fusion.14
  94.9 3.8 %all-to-all-start.4 = ((bf16[4,64,1024]{2,1,0:T(8,128)(2,1)}), bf16[4,64,1024]{2,1,0:T(8,128)(2,1)S(1)}, u32[]{:S(2)}, u32[]{:S(2)}) async-start(bf16[4,64,1024]{2,1,0:T(8,128)(2,1)} %bitcast.30), calls=%async_computation.4 | async-start | bytes 1048576 | tf_op jit(solution)/shard_map/all_to_all | solution.py:90
  98.7 6.7 %all-to-all-done.4 = bf16[4,64,1024]{2,1,0:T(8,128)(2,1)S(1)} async-done(((bf16[4,64,1024]{2,1,0:T(8,128)(2,1)}), bf16[4,64,1024]{2,1,0:T(8,128)(2,1)S(1)}, u32[]{:S(2)}, u32[]{:S(2)}) %all-to-all-start.4) | async-done | bytes 524320 | tf_op jit(solution)/shard_map/all_to_all | solution.py:90
  106.2 0.8 all_to_all.28
  107.0 11.7 %all-to-all-start.5 = ((bf16[512,1,128]{2,1,0:T(2,128)(2,1)}), bf16[512,1,128]{2,1,0:T(2,128)(2,1)S(1)}, u32[]{:S(2)}, u32[]{:S(2)}) async-start(bf16[512,1,128]{2,1,0:T(2,128)(2,1)} %all_to_all.28), calls=%async_computation.5 | async-start | bytes 524288 | tf_op jit(solution)/shard_map/all_to_all | solution.py:208
  119.0 0.9 copy.87
  119.9 16.3 %all-to-all-done.5 = bf16[512,1,128]{2,1,0:T(2,128)(2,1)S(1)} async-done(((bf16[512,1,128]{2,1,0:T(2,128)(2,1)}), bf16[512,1,128]{2,1,0:T(2,128)(2,1)S(1)}, u32[]{:S(2)}, u32[]{:S(2)}) %all-to-all-start.5) | async-done | bytes 131104 | tf_op jit(solution)/shard_map/all_to_all | solution.py:208
  136.3 1.3 gather_fusion
  (79 shorter events, 6.2 us)
Async XLA Ops:
  1.8 36.5 %copy-start.2 = (bf16[128,1024]{1,0:T(8,128)(2,1)S(1)}, bf16[128,1024]{1,0:T(8,128)(2,1)}, u32[]{:S(2)}) copy-start(bf16[128,1024]{1,0:T(8,128)(2,1)} %param.24) | copy-start | bytes 786436
  1.8 40.8 %copy-start.11 = (s32[64]{0:T(128)S(1)}, s32[64]{0:T(128)}, u32[]{:S(2)}) copy-start(s32[64]{0:T(128)} %param.20) | copy-start | bytes 772
  1.8 42.7 %copy-start.7 = (bf16[1024]{0:T(1024)(128)(2,1)S(1)}, bf16[1024]{0:T(1024)(128)(2,1)}, u32[]{:S(2)}) copy-start(bf16[1024]{0:T(1024)(128)(2,1)} %param.25) | copy-start | bytes 6148
  1.8 42.7 %copy-start.3 = (bf16[1,512,128]{2,1,0:T(8,128)(2,1)S(1)}, bf16[1,512,128]{2,1,0:T(8,128)(2,1)}, u32[]{:S(2)}) copy-start(bf16[1,512,128]{2,1,0:T(8,128)(2,1)} %param.18) | copy-start | bytes 393220
  1.9 42.8 %copy-start.1 = (bf16[3,1024,128]{2,1,0:T(8,128)(2,1)S(1)}, bf16[3,1024,128]{2,1,0:T(8,128)(2,1)}, u32[]{:S(2)}) copy-start(bf16[3,1024,128]{2,1,0:T(8,128)(2,1)} %param.22) | copy-start | bytes 2359300
  31.6 13.3 %copy-start.9 = (bf16[3,128]{1,0:T(4,128)(2,1)S(1)}, bf16[3,128]{1,0:T(4,128)(2,1)}, u32[]{:S(2)}) copy-start(bf16[3,128]{1,0:T(4,128)(2,1)} %param.23) | copy-start | bytes 2308
  31.6 13.3 %copy-start.4 = (bf16[1,512,128]{2,1,0:T(8,128)(2,1)S(1)}, bf16[1,512,128]{2,1,0:T(8,128)(2,1)}, u32[]{:S(2)}) copy-start(bf16[1,512,128]{2,1,0:T(8,128)(2,1)} %param.17) | copy-start | bytes 393220
  31.6 14.1 %copy-start.12 = (s32[64]{0:T(128)S(1)}, s32[64]{0:T(128)}, u32[]{:S(2)}) copy-start(s32[64]{0:T(128)} %param.19) | copy-start | bytes 772
  31.6 15.4 %copy-start.5 = (bf16[2,1024]{1,0:T(2,128)(2,1)S(1)}, bf16[2,1024]{1,0:T(2,128)(2,1)}, u32[]{:S(2)}) copy-start(bf16[2,1024]{1,0:T(2,128)(2,1)} %param.27) | copy-start | bytes 12292
  31.6 15.4 %copy-start.6 = (bf16[2,1024]{1,0:T(2,128)(2,1)S(1)}, bf16[2,1024]{1,0:T(2,128)(2,1)}, u32[]{:S(2)}) copy-start(bf16[2,1024]{1,0:T(2,128)(2,1)} %param.26) | copy-start | bytes 12292
  31.6 21.6 %all-to-all-start.1 = ((bf16[512,8,128]{2,0,1:T(8,128)(2,1)}), bf16[512,8,128]{2,0,1:T(8,128)(2,1)S(1)}, u32[]{:S(2)}, u32[]{:S(2)}) async-start(bf16[512,8,128]{2,0,1:T(8,128)(2,1)} %broadcast_in_dim.43), calls=%async_computation.1 | async-start | bytes 2097152 | tf_op jit(solution)/shard_map/all_to_all | solution.py:84
  38.2 23.2 %collective-permute-start.1 = (bf16[128,1024]{1,0:T(8,128)(2,1)S(1)}, bf16[128,1024]{1,0:T(8,128)(2,1)S(1)}, u32[]{:S(2)}, u32[]{:S(2)}) collective-permute-start(bf16[128,1024]{1,0:T(8,128)(2,1)S(1)} %copy-done.2), channel_id=1, source_target_pairs={{0,1},{1,0},{2,3},{3,2},{4,5},{5,4},{6,7},{7,6},{8,9},{9,8},{10,11... | collective-permute-start | bytes 786440 | tf_op jit(solution)/shard_map/ppermute | solution.py:95
  40.2 45.6 %collective-permute-start.2 = (bf16[1024,512]{1,0:T(8,128)(2,1)}, bf16[1024,512]{1,0:T(8,128)(2,1)}, u32[]{:S(2)}, u32[]{:S(2)}) collective-permute-start(bf16[1024,512]{1,0:T(8,128)(2,1)} %param.28), channel_id=1, source_target_pairs={{0,1},{1,0},{2,3},{3,2},{4,5},{5,4},{6,7},{7,6},{8,9},{9,8},{10,11... | collective-permute-start | bytes 3145736 | tf_op jit(solution)/shard_map/ppermute | solution.py:95
  58.3 3.8 %collective-permute-start = (bf16[4,64,128]{2,1,0:T(8,128)(2,1)S(1)}, bf16[4,64,128]{2,1,0:T(8,128)(2,1)S(1)}, u32[]{:S(2)}, u32[]{:S(2)}) collective-permute-start(bf16[4,64,128]{2,1,0:T(8,128)(2,1)S(1)} %bitcast.135), channel_id=1, source_target_pairs={{0,1},{1,0},{2,3},{3,2},{4,5},{5,4},{6,7},{7,6},{8,9},{9,8},{10,11... | collective-permute-start | bytes 196616 | tf_op jit(solution)/shard_map/ppermute | solution.py:95
  63.1 12.7 %all-to-all-start.2 = ((bf16[4,64,1024]{2,1,0:T(8,128)(2,1)}), bf16[4,64,1024]{2,1,0:T(8,128)(2,1)S(1)}, u32[]{:S(2)}, u32[]{:S(2)}) async-start(bf16[4,64,1024]{2,1,0:T(8,128)(2,1)} %bitcast.26), calls=%async_computation.2 | async-start | bytes 1048576 | tf_op jit(solution)/shard_map/all_to_all | solution.py:90
  66.8 13.9 %copy-start.10 = (bf16[512]{0:T(512)(128)(2,1)S(1)}, bf16[512]{0:T(512)(128)(2,1)}, u32[]{:S(2)}) copy-start(bf16[512]{0:T(512)(128)(2,1)} %param.29) | copy-start | bytes 3076
  66.8 17.1 %copy-start = (bf16[512,1024]{1,0:T(8,128)(2,1)S(1)}, bf16[512,1024]{1,0:T(8,128)(2,1)}, u32[]{:S(2)}) copy-start(bf16[512,1024]{1,0:T(8,128)(2,1)} %param.30) | copy-start | bytes 3145732
  77.2 11.5 %all-to-all-start.3 = ((bf16[4,64,1024]{2,1,0:T(8,128)(2,1)}), bf16[4,64,1024]{2,1,0:T(8,128)(2,1)S(1)}, u32[]{:S(2)}, u32[]{:S(2)}) async-start(bf16[4,64,1024]{2,1,0:T(8,128)(2,1)} %broadcast_in_dim.74), calls=%async_computation.3 | async-start | bytes 1048576 | tf_op jit(solution)/shard_map/all_to_all | solution.py:84
  80.7 5.1 %collective-permute-start.3 = (bf16[512]{0:T(512)(128)(2,1)S(1)}, bf16[512]{0:T(512)(128)(2,1)S(1)}, u32[]{:S(2)}, u32[]{:S(2)}) collective-permute-start(bf16[512]{0:T(512)(128)(2,1)S(1)} %copy-done.10), channel_id=1, source_target_pairs={{0,1},{1,0},{2,3},{3,2},{4,5},{5,4},{6,7},{7,6},{8,9},{9,8},{10,11... | collective-permute-start | bytes 3080 | tf_op jit(solution)/shard_map/ppermute | solution.py:95
  83.8 9.8 %collective-permute-start.4 = (bf16[512,1024]{1,0:T(8,128)(2,1)S(1)}, bf16[512,1024]{1,0:T(8,128)(2,1)S(1)}, u32[]{:S(2)}, u32[]{:S(2)}) collective-permute-start(bf16[512,1024]{1,0:T(8,128)(2,1)S(1)} %copy-done), channel_id=1, source_target_pairs={{0,1},{1,0},{2,3},{3,2},{4,5},{5,4},{6,7},{7,6},{8,9},{9,8},{10,11... | collective-permute-start | bytes 3145736 | tf_op jit(solution)/shard_map/ppermute | solution.py:95
  93.6 5.1 %copy-start.8 = (bf16[1024]{0:T(1024)(128)(2,1)S(1)}, bf16[1024]{0:T(1024)(128)(2,1)}, u32[]{:S(2)}) copy-start(bf16[1024]{0:T(1024)(128)(2,1)} %param.31) | copy-start | bytes 6148
  94.9 23.8 %copy-start.13 = (s32[64]{0:T(128)S(1)}, s32[64]{0:T(128)}, u32[]{:S(2)}) copy-start(s32[64]{0:T(128)} %param.21) | copy-start | bytes 772
  94.9 10.5 %all-to-all-start.4 = ((bf16[4,64,1024]{2,1,0:T(8,128)(2,1)}), bf16[4,64,1024]{2,1,0:T(8,128)(2,1)S(1)}, u32[]{:S(2)}, u32[]{:S(2)}) async-start(bf16[4,64,1024]{2,1,0:T(8,128)(2,1)} %bitcast.30), calls=%async_computation.4 | async-start | bytes 1048576 | tf_op jit(solution)/shard_map/all_to_all | solution.py:90
  107.0 29.2 %all-to-all-start.5 = ((bf16[512,1,128]{2,1,0:T(2,128)(2,1)}), bf16[512,1,128]{2,1,0:T(2,128)(2,1)S(1)}, u32[]{:S(2)}, u32[]{:S(2)}) async-start(bf16[512,1,128]{2,1,0:T(2,128)(2,1)} %all_to_all.28), calls=%async_computation.5 | async-start | bytes 524288 | tf_op jit(solution)/shard_map/all_to_all | solution.py:208
